TPU v7x, 32 devices: a whole 2x2x4 slice. The times are simulated.
32 devices in a mesh: shard: 2 (over core), context: 4 (over z), tensor: 4 (over y, x).
Axes of the slice: x: 2, y: 2, z: 4, core: 2. Of those that a mesh axis runs over, the one named last changes fastest.
Arguments:
- inputs: bfloat16 [2, 2048, 2048], P('shard', 'context'), may hold values from -6 to 6
- segments: int32 [2, 2048], P('shard', 'context'), may hold values from 0 to 2, as said below
- positions: int32 [2, 2048], P('shard', 'context'), may hold values from 0 to 2047, as said below
- w_q: bfloat16 [2048, 2048], P(('shard', 'context'), 'tensor'), may hold values from -0.125 to 0.125
- w_k: bfloat16 [2048, 2048], P(('shard', 'context'), 'tensor'), may hold values from -0.125 to 0.125
- w_v: bfloat16 [2048, 2048], P(('shard', 'context'), 'tensor'), may hold values from -0.125 to 0.125
- w_o: bfloat16 [2048, 2048], P(('shard', 'context'), 'tensor'), may hold values from -0.75 to 0.75
- w_gate: bfloat16 [2048, 8192], P(('shard', 'context'), 'tensor'), may hold values from -0.125 to 0.125
- w_up: bfloat16 [2048, 8192], P(('shard', 'context'), 'tensor'), may hold values from -0.125 to 0.125
- w_down: bfloat16 [2048, 8192], P(('shard', 'context'), 'tensor'), may hold values from -0.0625 to 0.0625
- g_attn: bfloat16 [2048], P(('shard', 'context')), may hold values from 0.5 to 1.5
- g_mlp: bfloat16 [2048], P(('shard', 'context')), may hold values from 0.5 to 1.5
- d_out: bfloat16 [2, 2048, 2048], P('shard', 'context'), may hold values from -6 to 6
Outputs:
- out: bfloat16 [2, 2048, 2048], P('shard', 'context')
- d_x: bfloat16 [2, 2048, 2048], P('shard', 'context')
- d_w_q: float32 [2048, 2048], P(('shard', 'context'), 'tensor')
- d_w_k: float32 [2048, 2048], P(('shard', 'context'), 'tensor')
- d_w_v: float32 [2048, 2048], P(('shard', 'context'), 'tensor')
- d_w_o: float32 [2048, 2048], P(('shard', 'context'), 'tensor')
- d_w_gate: float32 [2048, 8192], P(('shard', 'context'), 'tensor')
- d_w_up: float32 [2048, 8192], P(('shard', 'context'), 'tensor')
- d_w_down: float32 [2048, 8192], P(('shard', 'context'), 'tensor')
- d_g_attn: float32 [2048], P(('shard', 'context'))
- d_g_mlp: float32 [2048], P(('shard', 'context'))
Inputs may be any that keep to these rules, and one draw needn't show every extreme that they name: In each sequence the positions are a permutation of 0 to 2047, laid out by halves of 512 tokens: with p a permutation of the context indices, device c holds either halves 2 * p(c) and 2 * p(c) + 1 in order, or halves p(c) and 7 - p(c). `segments`: segment numbers never fall as the position grows; the first position of a sequence is in segment 0, and every sequence holds exactly 3 documents.
All inputs are finite; a program needn't handle non-finite values.
Results may differ from a plain program's by a relative error of at most 0.024.
Values may be sent and summed in bfloat16 or wider, within the bound.
No kernel may reach another device: no remote copies, remote signals or barrier semaphores. Data moves between devices by JAX's collectives and lax.ppermute only.
A program may use at most 192 MiB of HBM per device.

v0:
```python
import math

import jax
import jax.numpy as jnp
from jax import lax
from jax.sharding import PartitionSpec as P

HD = 64


EPS = 1e-05
THETA = 130000.0
NEG = -1e30


def passed_along(value, axis, steps):
    count = lax.axis_size(axis)
    pairs = [(source, (source + steps) % count) for source in range(count)]
    return lax.ppermute(value, axis, pairs)


def rope_tables(position):
    index = jnp.arange(HD // 2, dtype=jnp.float32)
    inverse = jnp.power(jnp.float32(THETA), -2.0 * index / HD)
    angle = position.astype(jnp.float32)[:, None] * inverse[None, :]
    return (jnp.cos(angle), jnp.sin(angle))


def rotate(tensor, cosine, sine):
    half = tensor.shape[-1] // 2
    first = tensor[..., :half]
    second = tensor[..., half:]
    cosine = cosine[:, None, :]
    sine = sine[:, None, :]
    return jnp.concatenate(
        [first * cosine - second * sine, second * cosine + first * sine], axis=-1
    )


def rotate_back(grad, cosine, sine):
    half = grad.shape[-1] // 2
    first = grad[..., :half]
    second = grad[..., half:]
    cosine = cosine[:, None, :]
    sine = sine[:, None, :]
    return jnp.concatenate(
        [first * cosine + second * sine, second * cosine - first * sine], axis=-1
    )


def normalize(value):
    inv_rms = lax.rsqrt(jnp.mean(value * value, axis=-1, keepdims=True) + EPS)
    return (value * inv_rms, inv_rms)


def norm_back(grad, normed, inv_rms, gain):
    scaled = grad * gain.astype(jnp.float32)
    return inv_rms * (scaled - normed * jnp.mean(scaled * normed, axis=-1, keepdims=True))


def contract_last(left, right):
    return lax.dot_general(
        left, right, (((1,), (1,)), ((), ())), preferred_element_type=jnp.float32
    )


def contract_first(left, right):
    return lax.dot_general(
        left, right, (((0,), (0,)), ((), ())), preferred_element_type=jnp.float32
    )


def branch_total(partial_sum):
    return lax.psum(partial_sum.astype(jnp.bfloat16), "tensor").astype(jnp.float32)


def input_total(partial_sum):
    return lax.psum(partial_sum.astype(jnp.bfloat16), "tensor").astype(jnp.float32)


def pass_grads(grad_key, grad_value):
    return (
        passed_along(grad_key.astype(jnp.bfloat16), "context", 1).astype(grad_key.dtype),
        passed_along(grad_value.astype(jnp.bfloat16), "context", 1).astype(grad_value.dtype),
    )


def key_scores(query_heads, query_seg, query_pos, piece):
    key_flat, value_flat, key_seg, key_pos = piece
    heads = query_heads.shape[1]
    key_heads = key_flat.reshape(key_flat.shape[0], heads, HD)
    value_heads = value_flat.reshape(value_flat.shape[0], heads, HD)
    scores = jnp.einsum(
        "qhd,khd->hqk", query_heads, key_heads, preferred_element_type=jnp.float32
    ) * (1.0 / math.sqrt(HD))
    allowed = (query_seg[:, None] == key_seg[None, :]) & (key_pos[None, :] <= query_pos[:, None])
    return (jnp.where(allowed[None], scores, NEG), allowed, key_heads, value_heads)


def forward_fold(stats, piece, query_heads, query_seg, query_pos):
    peak, total, accum = stats
    scores, allowed, key_heads, value_heads = key_scores(query_heads, query_seg, query_pos, piece)
    new_peak = jnp.maximum(peak, jnp.max(scores, axis=-1))
    weights = jnp.where(allowed[None], jnp.exp(scores - new_peak[..., None]), 0.0)
    factor = jnp.exp(peak - new_peak)
    total = total * factor + jnp.sum(weights, axis=-1)
    accum = accum * factor[..., None] + jnp.einsum(
        "hqk,khd->hqd",
        weights.astype(jnp.bfloat16),
        value_heads,
        preferred_element_type=jnp.float32,
    )
    return (new_peak, total, accum)


def backward_piece(piece, query_heads, grad_heads, log_total, inner, query_seg, query_pos):
    scores, allowed, key_heads, value_heads = key_scores(query_heads, query_seg, query_pos, piece)
    probs = jnp.where(allowed[None], jnp.exp(scores - log_total[..., None]), 0.0)
    grad_value = jnp.einsum(
        "hqk,qhd->khd", probs.astype(jnp.bfloat16), grad_heads, preferred_element_type=jnp.float32
    )
    grad_probs = jnp.einsum(
        "qhd,khd->hqk", grad_heads, value_heads, preferred_element_type=jnp.float32
    )
    grad_scores = (probs * (grad_probs - inner[..., None]) * (1.0 / math.sqrt(HD))).astype(
        jnp.bfloat16
    )
    grad_query = jnp.einsum(
        "hqk,khd->qhd", grad_scores, key_heads, preferred_element_type=jnp.float32
    )
    grad_key = jnp.einsum(
        "hqk,qhd->khd", grad_scores, query_heads, preferred_element_type=jnp.float32
    )
    key_rows = grad_key.shape[0]
    return (grad_query, grad_key.reshape(key_rows, -1), grad_value.reshape(key_rows, -1))


def on_device(
    inputs, segments, positions, w_q, w_k, w_v, w_o, w_gate, w_up, w_down, g_attn, g_mlp, d_out
):
    f32 = jnp.float32
    bf16 = jnp.bfloat16
    rows = inputs.shape[1]
    width = inputs.shape[2]
    tokens = inputs.reshape(rows, width)
    segment = segments.reshape(rows)
    position = positions.reshape(rows)
    fetched = (
        lax.all_gather(w_q, ("shard", "context"), axis=0, tiled=True),
        lax.all_gather(w_k, ("shard", "context"), axis=0, tiled=True),
        lax.all_gather(w_v, ("shard", "context"), axis=0, tiled=True),
        lax.all_gather(w_o, ("shard", "context"), axis=0, tiled=True),
        lax.all_gather(w_gate, ("shard", "context"), axis=0, tiled=True),
        lax.all_gather(w_up, ("shard", "context"), axis=0, tiled=True),
        lax.all_gather(w_down, ("shard", "context"), axis=0, tiled=True),
        lax.all_gather(g_attn, ("shard", "context"), axis=0, tiled=True),
        lax.all_gather(g_mlp, ("shard", "context"), axis=0, tiled=True),
    )
    full_q, full_k, full_v, full_o, full_gate, full_up, full_down, gain_attn, gain_mlp = fetched
    heads = full_q.shape[1] // HD
    cosine, sine = rope_tables(position)
    resid1 = tokens.astype(f32)
    norm1, inv1 = normalize(resid1)
    h1 = (norm1 * gain_attn.astype(f32)).astype(bf16)
    query = rotate(
        jnp.dot(h1, full_q, preferred_element_type=f32).reshape(rows, heads, HD), cosine, sine
    ).astype(bf16)
    key_flat = (
        rotate(
            jnp.dot(h1, full_k, preferred_element_type=f32).reshape(rows, heads, HD), cosine, sine
        )
        .astype(bf16)
        .reshape(rows, heads * HD)
    )
    value_flat = jnp.dot(h1, full_v, preferred_element_type=f32).astype(bf16)
    start_stats = (
        jnp.full((heads, rows), NEG, f32),
        jnp.zeros((heads, rows), f32),
        jnp.zeros((heads, rows, HD), f32),
    )
    stats = forward_fold(
        start_stats, (key_flat, value_flat, segment, position), query, segment, position
    )

    def cycle_turn(index, carry):
        moving_key, moving_value, moving_seg, moving_pos, current = carry
        moving_key, moving_value, moving_seg, moving_pos = passed_along(
            (moving_key, moving_value, moving_seg, moving_pos), "context", 1
        )
        current = forward_fold(
            current, (moving_key, moving_value, moving_seg, moving_pos), query, segment, position
        )
        return (moving_key, moving_value, moving_seg, moving_pos, current)

    stats = lax.fori_loop(
        0,
        lax.axis_size("context") - 1,
        cycle_turn,
        (key_flat, value_flat, segment, position, stats),
    )[4]
    peak, total, accum = stats
    attended = jnp.transpose(accum / total[..., None], (1, 0, 2)).astype(bf16)
    log_total = peak + jnp.log(total)
    attended_flat = attended.reshape(rows, heads * HD)
    attn_partial = contract_last(attended_flat, full_o)
    resid2 = resid1 + branch_total(attn_partial)
    norm2, inv2 = normalize(resid2)
    h2_part = (norm2 * gain_mlp.astype(f32)).astype(bf16)
    gate = jnp.dot(h2_part, full_gate, preferred_element_type=f32)
    up = jnp.dot(h2_part, full_up, preferred_element_type=f32)
    active = jax.nn.silu(gate)
    hidden = (active * up).astype(bf16)
    mlp_partial = contract_last(hidden, full_down)
    result = (resid2 + branch_total(mlp_partial)).astype(bf16)
    fetched = (
        lax.all_gather(w_q, ("shard", "context"), axis=0, tiled=True),
        lax.all_gather(w_k, ("shard", "context"), axis=0, tiled=True),
        lax.all_gather(w_v, ("shard", "context"), axis=0, tiled=True),
        lax.all_gather(w_o, ("shard", "context"), axis=0, tiled=True),
        lax.all_gather(w_gate, ("shard", "context"), axis=0, tiled=True),
        lax.all_gather(w_up, ("shard", "context"), axis=0, tiled=True),
        lax.all_gather(w_down, ("shard", "context"), axis=0, tiled=True),
        lax.all_gather(g_attn, ("shard", "context"), axis=0, tiled=True),
        lax.all_gather(g_mlp, ("shard", "context"), axis=0, tiled=True),
    )
    full_q, full_k, full_v, full_o, full_gate, full_up, full_down, gain_attn, gain_mlp = fetched
    grad_y = d_out.reshape(rows, width)
    grad_hidden = jnp.dot(grad_y, full_down, preferred_element_type=f32)
    sigma = jax.nn.sigmoid(gate)
    grad_gate = (grad_hidden * up * sigma * (1.0 + gate * (1.0 - sigma))).astype(bf16)
    grad_up = (grad_hidden * active).astype(bf16)
    h2_grad_partial = contract_last(grad_gate, full_gate) + contract_last(grad_up, full_up)
    grad_h2 = input_total(h2_grad_partial)
    grad_gmlp = jnp.sum(grad_h2 * norm2, axis=0)
    grad_resid = grad_y.astype(f32) + norm_back(grad_h2, norm2, inv2, gain_mlp)
    grad_resid_part = grad_resid.astype(bf16)
    grad_heads = (
        jnp.dot(grad_resid_part, full_o, preferred_element_type=f32)
        .astype(bf16)
        .reshape(rows, heads, HD)
    )
    inner = jnp.sum(grad_heads.astype(f32) * attended.astype(f32), axis=-1).T

    def piece_grads(piece):
        return backward_piece(piece, query, grad_heads, log_total, inner, segment, position)

    grad_query, grad_key, grad_value = piece_grads((key_flat, value_flat, segment, position))

    def grad_turn(index, carry):
        moving_key, moving_value, moving_seg, moving_pos, acc_query, acc_key, acc_value = carry
        moving_key, moving_value, moving_seg, moving_pos = passed_along(
            (moving_key, moving_value, moving_seg, moving_pos), "context", 1
        )
        acc_key, acc_value = pass_grads(acc_key, acc_value)
        part_query, part_key, part_value = piece_grads(
            (moving_key, moving_value, moving_seg, moving_pos)
        )
        return (
            moving_key,
            moving_value,
            moving_seg,
            moving_pos,
            acc_query + part_query,
            acc_key + part_key,
            acc_value + part_value,
        )

    carried = lax.fori_loop(
        0,
        lax.axis_size("context") - 1,
        grad_turn,
        (key_flat, value_flat, segment, position, grad_query, grad_key, grad_value),
    )
    grad_query = carried[4]
    grad_key, grad_value = pass_grads(carried[5], carried[6])
    grad_qin = rotate_back(grad_query, cosine, sine).astype(bf16).reshape(rows, heads * HD)
    grad_kin = (
        rotate_back(grad_key.reshape(rows, heads, HD), cosine, sine)
        .astype(bf16)
        .reshape(rows, heads * HD)
    )
    grad_vin = grad_value.astype(bf16)
    h1_grad_partial = (
        contract_last(grad_qin, full_q)
        + contract_last(grad_kin, full_k)
        + contract_last(grad_vin, full_v)
    )
    grad_h1 = input_total(h1_grad_partial)
    grad_gattn = jnp.sum(grad_h1 * norm1, axis=0)
    grad_x_part = (grad_resid + norm_back(grad_h1, norm1, inv1, gain_attn)).astype(bf16)
    grad_wq = contract_first(h1, grad_qin)
    grad_wk = contract_first(h1, grad_kin)
    grad_wv = contract_first(h1, grad_vin)
    grad_wo = contract_first(grad_resid_part, attended_flat)
    grad_wgate = contract_first(h2_part, grad_gate)
    grad_wup = contract_first(h2_part, grad_up)
    grad_wdown = contract_first(grad_y, hidden)
    reduced = (
        lax.psum_scatter(
            grad_wq.astype(jnp.bfloat16), ("shard", "context"), scatter_dimension=0, tiled=True
        ).astype(jnp.float32),
        lax.psum_scatter(
            grad_wk.astype(jnp.bfloat16), ("shard", "context"), scatter_dimension=0, tiled=True
        ).astype(jnp.float32),
        lax.psum_scatter(
            grad_wv.astype(jnp.bfloat16), ("shard", "context"), scatter_dimension=0, tiled=True
        ).astype(jnp.float32),
        lax.psum_scatter(
            grad_wo.astype(jnp.bfloat16), ("shard", "context"), scatter_dimension=0, tiled=True
        ).astype(jnp.float32),
        lax.psum_scatter(
            grad_wgate.astype(jnp.bfloat16), ("shard", "context"), scatter_dimension=0, tiled=True
        ).astype(jnp.float32),
        lax.psum_scatter(
            grad_wup.astype(jnp.bfloat16), ("shard", "context"), scatter_dimension=0, tiled=True
        ).astype(jnp.float32),
        lax.psum_scatter(
            grad_wdown.astype(jnp.bfloat16), ("shard", "context"), scatter_dimension=0, tiled=True
        ).astype(jnp.float32),
        lax.psum_scatter(
            grad_gattn.astype(jnp.bfloat16), ("shard", "context"), scatter_dimension=0, tiled=True
        ).astype(jnp.float32),
        lax.psum_scatter(
            grad_gmlp.astype(jnp.bfloat16), ("shard", "context"), scatter_dimension=0, tiled=True
        ).astype(jnp.float32),
    )
    return (
        result.reshape(1, rows, width),
        grad_x_part.reshape(1, rows, width),
        reduced[0],
        reduced[1],
        reduced[2],
        reduced[3],
        reduced[4],
        reduced[5],
        reduced[6],
        reduced[7],
        reduced[8],
    )


def solution(mesh):
    placed = (
        P("shard", "context", None),
        P("shard", "context"),
        P("shard", "context"),
        P(("shard", "context"), "tensor"),
        P(("shard", "context"), "tensor"),
        P(("shard", "context"), "tensor"),
        P(("shard", "context"), "tensor"),
        P(("shard", "context"), "tensor"),
        P(("shard", "context"), "tensor"),
        P(("shard", "context"), "tensor"),
        P(("shard", "context")),
        P(("shard", "context")),
        P("shard", "context", None),
    )
    return jax.shard_map(
        on_device,
        mesh=mesh,
        in_specs=placed,
        out_specs=(
            P("shard", "context", None),
            P("shard", "context", None),
            P(("shard", "context"), "tensor"),
            P(("shard", "context"), "tensor"),
            P(("shard", "context"), "tensor"),
            P(("shard", "context"), "tensor"),
            P(("shard", "context"), "tensor"),
            P(("shard", "context"), "tensor"),
            P(("shard", "context"), "tensor"),
            P(("shard", "context")),
            P(("shard", "context")),
        ),
        check_vma=False,
    )
```

profile of v0, /device:TPU:0, one launch (start us, length us, event | category | flops | bytes accessed | tf_op | source)
XLA Modules:
  0.0 1685.4 jit_solution(14790218301723463259)
XLA Ops:
  16.6 18.3 %all-gather = bf16[8,1,256]{2,1,0:T(2,128)(2,1)S(1)} all-gather(bf16[1,1,256]{2,1,0:T(2,128)(2,1)S(1)} %reshape.451), channel_id=1, replica_groups=mesh['shard'=2,'context'=4,'tensor'=4] {'shard','context'}, dimensions={0}, use_global_device_ids=true | all-gather | bytes 4608 | tf_op jit(solution)/shard_map/all_gather | solution.py:156
  35.2 6.4 all-gather.12.cloned.1.call-done
  41.6 3.6 convolution_convert_fusion.9
  46.8 25.0 %all-gather.10.cloned.1.call-done = bf16[2048,512]{1,0:T(8,128)(2,1)} async-done(((bf16[256,512]{1,0:T(8,128)(2,1)}), bf16[2048,512]{1,0:T(8,128)(2,1)}) %all-gather.10.cloned.1.call-update) | async-done | bytes 2097168 | tf_op jit(solution)/shard_map/all_gather | solution.py:150
  71.8 3.9 copy.34
  75.7 2.9 fusion.62
  80.5 21.5 %all-gather.14.cloned.1.call-done = bf16[2048,512]{1,0:T(8,128)(2,1)} async-done(((bf16[256,512]{1,0:T(8,128)(2,1)}), bf16[2048,512]{1,0:T(8,128)(2,1)}) %all-gather.14.cloned.1.call-update) | async-done | bytes 2097168 | tf_op jit(solution)/shard_map/all_gather | solution.py:149
  102.0 3.9 copy.35
  105.9 3.0 fusion.60
  114.0 3.3 fusion.66
  117.3 105.5 %while.44 = (s32[]{:T(128)}, bf16[512,512]{0,1:T(8,128)(2,1)}, bf16[512,512]{0,1:T(8,128)(2,1)}, s32[512]{0:T(512)S(1)}, s32[512]{0:T(512)S(1)}, /*index=5*/f32[...) while((s32[]{:T(128)}, bf16[512,512]{0,1:T(8,128)(2,1)}, ...), condition=%wide.region_6.7_spmd, body=%wide.region_3.6_spmd.sunk | while | flops 565452800 | bytes 44859724 | solution.py:195
  122.5 20.8 %collective-permute-done.3 = s32[512]{0:T(512)S(1)} collective-permute-done((s32[512]{0:T(512)S(1)}, s32[512]{0:T(512)S(1)}, u32[]{:S(2)}, u32[]{:S(2)}) %collective-permute-start.3) | collective-permute-done | bytes 2080 | tf_op jit(solution)/shard_map/while/body/eval_jaxpr/ppermute | solution.py:19
  148.2 6.1 collective-permute-done.1
  161.1 3.3 collective-permute-start.1
  164.3 12.0 collective-permute-done.3
  181.2 5.2 collective-permute-done.1
  192.3 4.2 collective-permute-start.1
  196.5 12.0 collective-permute-done.3
  213.4 4.4 collective-permute-done.1
  224.2 4.4 convolution_convert_fusion.7
  230.8 12.8 all-gather.1
  243.6 52.8 %all-reduce.8.cloned.1.call-done = bf16[512,2048]{1,0:T(8,128)(2,1)} async-done(((bf16[512,2048]{1,0:T(8,128)(2,1)}), bf16[512,2048]{1,0:T(8,128)(2,1)}) %all-reduce.8.cloned.1.call-update) | async-done | bytes 2097168 | tf_op jit(solution)/shard_map/psum | solution.py:74
  301.3 78.6 %all-gather.20.cloned.1.call-done = bf16[2048,2048]{1,0:T(8,128)(2,1)} async-done(((bf16[256,2048]{1,0:T(8,128)(2,1)}), bf16[2048,2048]{1,0:T(8,128)(2,1)}) %all-gather.20.cloned.1.call-update) | async-done | bytes 8388624 | tf_op jit(solution)/shard_map/all_gather | solution.py:154
  379.9 10.6 fusion.91
  390.5 71.6 %all-gather.18.cloned.1.call-done = bf16[2048,2048]{1,0:T(8,128)(2,1)} async-done(((bf16[256,2048]{1,0:T(8,128)(2,1)}), bf16[2048,2048]{1,0:T(8,128)(2,1)}) %all-gather.18.cloned.1.call-update) | async-done | bytes 8388624 | tf_op jit(solution)/shard_map/all_gather | solution.py:153
  462.1 10.6 fusion.90
  472.7 71.6 %all-gather.22.cloned.1.call-done = bf16[2048,2048]{1,0:T(8,128)(2,1)} async-done(((bf16[256,2048]{1,0:T(8,128)(2,1)}), bf16[2048,2048]{1,0:T(8,128)(2,1)}) %all-gather.22.cloned.1.call-update) | async-done | bytes 8388624 | tf_op jit(solution)/shard_map/all_gather | solution.py:155
  544.3 14.1 multiply_convert_fusion.2
  558.3 4.5 fusion.92
  562.9 9.2 add_convert_fusion.1
  572.4 67.9 %all-reduce.10.cloned.1.call-done = bf16[512,2048]{1,0:T(8,128)(2,1)} async-done(((bf16[512,2048]{1,0:T(8,128)(2,1)}), bf16[512,2048]{1,0:T(8,128)(2,1)}) %all-reduce.10.cloned.1.call-update) | async-done | bytes 2097168 | tf_op jit(solution)/shard_map/psum | solution.py:78
  640.2 4.5 fusion.40
  644.8 4.9 multiply_reduce_fusion.1
  649.8 3.3 fusion.48
  653.1 3.6 multiply_convert_fusion.1
  660.8 4.2 convolution_convert_fusion.2
  665.3 227.0 %while.45 = (s32[]{:T(128)}, bf16[512,512]{0,1:T(8,128)(2,1)}, bf16[512,512]{0,1:T(8,128)(2,1)}, s32[512]{0:T(512)S(1)}, s32[512]{0:T(512)S(1)}, /*index=5*/f32[...) while((s32[]{:T(128)}, bf16[512,512]{0,1:T(8,128)(2,1)}, ...), condition=%wide.region_14.15_spmd, body=%wide.region_13.14_spmd.sunk | while | flops 1372061696 | bytes 71647696 | solution.py:268
  671.8 17.6 %collective-permute-done.7 = s32[512]{0:T(512)S(1)} collective-permute-done((s32[512]{0:T(512)S(1)}, s32[512]{0:T(512)S(1)}, u32[]{:S(2)}, u32[]{:S(2)}) %collective-permute-start.7) | collective-permute-done | bytes 2080 | tf_op jit(solution)/shard_map/while/body/eval_jaxpr/ppermute | solution.py:19
  692.6 61.4 %collective-permute-done.5 = bf16[512,512]{0,1:T(8,128)(2,1)S(1)} collective-permute-done((bf16[512,512]{0,1:T(8,128)(2,1)}, bf16[512,512]{0,1:T(8,128)(2,1)S(1)}, u32[]{:S(2)}, u32[]{:S(2)}) %collective-permute-start.5) | collective-permute-done | bytes 524320 | tf_op jit(solution)/shard_map/while/body/eval_jaxpr/ppermute | solution.py:19
  754.0 3.9 multiply_convert_fusion.7
  773.6 11.9 collective-permute-done.7
  787.2 29.1 %collective-permute-done.5 = bf16[512,512]{0,1:T(8,128)(2,1)S(1)} collective-permute-done((bf16[512,512]{0,1:T(8,128)(2,1)}, bf16[512,512]{0,1:T(8,128)(2,1)S(1)}, u32[]{:S(2)}, u32[]{:S(2)}) %collective-permute-start.5) | collective-permute-done | bytes 524320 | tf_op jit(solution)/shard_map/while/body/eval_jaxpr/ppermute | solution.py:19
  816.2 3.9 multiply_convert_fusion.7
  832.6 3.3 collective-permute-start.9
  835.9 11.9 collective-permute-done.7
  849.4 28.2 %collective-permute-done.5 = bf16[512,512]{0,1:T(8,128)(2,1)S(1)} collective-permute-done((bf16[512,512]{0,1:T(8,128)(2,1)}, bf16[512,512]{0,1:T(8,128)(2,1)S(1)}, u32[]{:S(2)}, u32[]{:S(2)}) %collective-permute-start.5) | collective-permute-done | bytes 524320 | tf_op jit(solution)/shard_map/while/body/eval_jaxpr/ppermute | solution.py:19
  877.6 3.9 multiply_convert_fusion.7
  892.4 12.1 collective-permute-done.11
  908.1 19.6 %collective-permute-done.10 = bf16[512,512]{0,1:T(8,128)(2,1)S(1)} collective-permute-done((bf16[512,512]{0,1:T(8,128)(2,1)}, bf16[512,512]{0,1:T(8,128)(2,1)S(1)}, u32[]{:S(2)}, u32[]{:S(2)}) %collective-permute-start.10) | collective-permute-done | bytes 524320 | tf_op jit(solution)/shard_map/ppermute | solution.py:19
  928.3 2.8 convolution_convert_fusion.4
  931.2 2.8 convolution_convert_fusion.5
  934.5 10.1 convolution_convert_fusion.6
  950.7 10.1 convert_bitcast_fusion
  960.9 10.1 convolution_convert_fusion
  971.3 10.1 convolution_convert_fusion.1
  987.0 21.2 %reduce-scatter.10.cloned.1.call-done = bf16[256,512]{1,0:T(8,128)(2,1)} async-done(((bf16[2048,512]{1,0:T(8,128)(2,1)}), bf16[256,512]{1,0:T(8,128)(2,1)}) %reduce-scatter.10.cloned.1.call-update) | async-done | bytes 262160 | tf_op jit(solution)/shard_map/reduce_scatter | solution.py:302
  1009.9 49.3 %reduce-scatter.8.cloned.1.call-done = bf16[256,512]{1,0:T(8,128)(2,1)} async-done(((bf16[2048,512]{1,0:T(8,128)(2,1)}), bf16[256,512]{1,0:T(8,128)(2,1)}) %reduce-scatter.8.cloned.1.call-update) | async-done | bytes 262160 | tf_op jit(solution)/shard_map/reduce_scatter | solution.py:299
  1061.1 105.0 %all-reduce.12.cloned.1.call-done = (bf16[512,2048]{1,0:T(8,128)(2,1)}, bf16[512,2048]{1,0:T(8,128)(2,1)}) async-done(((bf16[512,2048]{1,0:T(8,128)(2,1)}, bf16[512,2048]{1,0:T(8,128)(2,1)}), (bf16[512,2048]{1,0:T(8,128)(2,1)}, bf16[512,2048]{1,0:T(8,128)(2,1)})) %all-reduce.12.cloned.1.call-update) | async-done | bytes 4194320 | tf_op jit(solution)/shard_map/psum | solution.py:74
  1166.0 2.9 fusion.43
  1168.9 19.6 %all-reduce.2 = (bf16[2048]{0:T(1024)(128)(2,1)S(1)}, bf16[2048]{0:T(1024)(128)(2,1)S(1)}) all-reduce(bf16[2048]{0:T(1024)(128)(2,1)S(1)} %get-tuple-element.174, bf16[2048]{0:T(1024)(128)(2,1)S(1)} %copy-done.44), channel_id=9, replica_groups=mesh['shard'=2,'context'=4,'tensor'=4] {'shard','context'}, use_global_device_ids=true, to_apply=%region_25.26.clone | all-reduce | flops 4096 | bytes 16384
  1189.9 8.0 fusion.56
  1197.9 137.8 %reduce-scatter.20.cloned.1.call-done = bf16[256,2048]{0,1:T(8,128)(2,1)} async-done(((bf16[2048,2048]{0,1:T(8,128)(2,1)}), bf16[256,2048]{0,1:T(8,128)(2,1)}) %reduce-scatter.20.cloned.1.call-update) | async-done | bytes 1048592 | tf_op jit(solution)/shard_map/reduce_scatter | solution.py:317
  1338.3 167.5 %reduce-scatter.18.cloned.1.call-done = bf16[256,2048]{1,0:T(8,128)(2,1)} async-done(((bf16[2048,2048]{1,0:T(8,128)(2,1)}), bf16[256,2048]{1,0:T(8,128)(2,1)}) %reduce-scatter.18.cloned.1.call-update) | async-done | bytes 1048592 | tf_op jit(solution)/shard_map/reduce_scatter | solution.py:314
  1508.6 167.3 %reduce-scatter.16.cloned.1.call-done = bf16[256,2048]{1,0:T(8,128)(2,1)} async-done(((bf16[2048,2048]{1,0:T(8,128)(2,1)}), bf16[256,2048]{1,0:T(8,128)(2,1)}) %reduce-scatter.16.cloned.1.call-update) | async-done | bytes 1048592 | tf_op jit(solution)/shard_map/reduce_scatter | solution.py:311
  (333 shorter events, 148.9 us)
Async XLA Ops:
  7.2 34.5 %all-gather.12.cloned.1.call-start = ((), (), s32[]{:S(2)}) async-start(), calls=%async_computation.8 | async-start | bytes 2359296 | tf_op jit(solution)/shard_map/all_gather | solution.py:151
  7.9 63.9 %all-gather.10.cloned.1.call-start = ((), (), s32[]{:S(2)}) async-start(), calls=%async_computation.7 | async-start | bytes 2359296 | tf_op jit(solution)/shard_map/all_gather | solution.py:150
  8.7 93.3 %all-gather.14.cloned.1.call-start = ((), (), s32[]{:S(2)}) async-start(), calls=%async_computation.9 | async-start | bytes 2359296 | tf_op jit(solution)/shard_map/all_gather | solution.py:149
  9.4 214.8 %all-gather.16.cloned.1.call-start = ((), (), s32[]{:S(2)}) async-start(), calls=%async_computation.10 | async-start | bytes 2359296 | tf_op jit(solution)/shard_map/all_gather | solution.py:152
  10.0 286.5 %all-reduce.8.cloned.1.call-start = ((), (), s32[]{:S(2)}) async-start(), calls=%async_computation.11 | async-start | bytes 4194304 | tf_op jit(solution)/shard_map/psum | solution.py:74
  16.6 89.3 %copy-start.42 = (f32[512]{0:T(512)}, f32[512]{0:T(512)S(1)}, u32[]{:S(2)}) copy-start(f32[512]{0:T(512)S(1)} %add_rsqrt_fusion.1) | copy-start | bytes 6148
  34.9 71.0 %copy-start.38 = (f32[8,1,256]{2,1,0:T(1,128)}, f32[8,1,256]{2,1,0:T(1,128)S(1)}, u32[]{:S(2)}) copy-start(f32[8,1,256]{2,1,0:T(1,128)S(1)} %convert_element_type.298) | copy-start | bytes 24580
  35.2 73.7 %copy-start.23 = (f32[512,32]{0,1:T(8,128)}, f32[512,32]{0,1:T(8,128)S(1)}, u32[]{:S(2)}) copy-start(f32[512,32]{0,1:T(8,128)S(1)} %get-tuple-element.251) | copy-start | bytes 196612
  35.2 73.7 %copy-start.25 = (f32[512,32]{0,1:T(8,128)}, f32[512,32]{0,1:T(8,128)S(1)}, u32[]{:S(2)}) copy-start(f32[512,32]{0,1:T(8,128)S(1)} %get-tuple-element.252) | copy-start | bytes 196612
  117.5 26.1 %collective-permute-start = (bf16[512,512]{0,1:T(8,128)(2,1)}, bf16[512,512]{0,1:T(8,128)(2,1)}, u32[]{:S(2)}, u32[]{:S(2)}) collective-permute-start(bf16[512,512]{0,1:T(8,128)(2,1)} %get-tuple-element.432), channel_id=1, source_target_pairs={{0,4},{4,8},{8,12},{12,0},{1,5},{5,9},{9,13},{13,1},{2,6},{6,10},{... | collective-permute-start | bytes 1572872 | tf_op jit(solution)/shard_map/while/body/eval_jaxpr/ppermute | solution.py:19
  119.0 24.3 %collective-permute-start.3 = (s32[512]{0:T(512)S(1)}, s32[512]{0:T(512)S(1)}, u32[]{:S(2)}, u32[]{:S(2)}) collective-permute-start(s32[512]{0:T(512)S(1)} %get-tuple-element.435), channel_id=1, source_target_pairs={{0,4},{4,8},{8,12},{12,0},{1,5},{5,9},{9,13},{13,1},{2,6},{6,10},{... | collective-permute-start | bytes 6152 | tf_op jit(solution)/shard_map/while/body/eval_jaxpr/ppermute | solution.py:19
  119.9 23.4 %collective-permute-start.2 = (s32[512]{0:T(512)S(1)}, s32[512]{0:T(512)S(1)}, u32[]{:S(2)}, u32[]{:S(2)}) collective-permute-start(s32[512]{0:T(512)S(1)} %get-tuple-element.434), channel_id=1, source_target_pairs={{0,4},{4,8},{8,12},{12,0},{1,5},{5,9},{9,13},{13,1},{2,6},{6,10},{... | collective-permute-start | bytes 6152 | tf_op jit(solution)/shard_map/while/body/eval_jaxpr/ppermute | solution.py:19
  120.5 33.8 %collective-permute-start.1 = (bf16[512,512]{0,1:T(8,128)(2,1)}, bf16[512,512]{0,1:T(8,128)(2,1)S(1)}, u32[]{:S(2)}, u32[]{:S(2)}) collective-permute-start(bf16[512,512]{0,1:T(8,128)(2,1)} %get-tuple-element.433), channel_id=1, source_target_pairs={{0,4},{4,8},{8,12},{12,0},{1,5},{5,9},{9,13},{13,1},{2,6},{6,10},{... | collective-permute-start | bytes 1572872 | tf_op jit(solution)/shard_map/while/body/eval_jaxpr/ppermute | solution.py:19
  159.4 17.2 %collective-permute-start = (bf16[512,512]{0,1:T(8,128)(2,1)}, bf16[512,512]{0,1:T(8,128)(2,1)}, u32[]{:S(2)}, u32[]{:S(2)}) collective-permute-start(bf16[512,512]{0,1:T(8,128)(2,1)} %get-tuple-element.432), channel_id=1, source_target_pairs={{0,4},{4,8},{8,12},{12,0},{1,5},{5,9},{9,13},{13,1},{2,6},{6,10},{... | collective-permute-start | bytes 1572872 | tf_op jit(solution)/shard_map/while/body/eval_jaxpr/ppermute | solution.py:19
  159.4 16.9 %collective-permute-start.3 = (s32[512]{0:T(512)S(1)}, s32[512]{0:T(512)S(1)}, u32[]{:S(2)}, u32[]{:S(2)}) collective-permute-start(s32[512]{0:T(512)S(1)} %get-tuple-element.435), channel_id=1, source_target_pairs={{0,4},{4,8},{8,12},{12,0},{1,5},{5,9},{9,13},{13,1},{2,6},{6,10},{... | collective-permute-start | bytes 6152 | tf_op jit(solution)/shard_map/while/body/eval_jaxpr/ppermute | solution.py:19
  159.4 16.9 %collective-permute-start.2 = (s32[512]{0:T(512)S(1)}, s32[512]{0:T(512)S(1)}, u32[]{:S(2)}, u32[]{:S(2)}) collective-permute-start(s32[512]{0:T(512)S(1)} %get-tuple-element.434), channel_id=1, source_target_pairs={{0,4},{4,8},{8,12},{12,0},{1,5},{5,9},{9,13},{13,1},{2,6},{6,10},{... | collective-permute-start | bytes 6152 | tf_op jit(solution)/shard_map/while/body/eval_jaxpr/ppermute | solution.py:19
  161.1 25.4 %collective-permute-start.1 = (bf16[512,512]{0,1:T(8,128)(2,1)}, bf16[512,512]{0,1:T(8,128)(2,1)S(1)}, u32[]{:S(2)}, u32[]{:S(2)}) collective-permute-start(bf16[512,512]{0,1:T(8,128)(2,1)} %get-tuple-element.433), channel_id=1, source_target_pairs={{0,4},{4,8},{8,12},{12,0},{1,5},{5,9},{9,13},{13,1},{2,6},{6,10},{... | collective-permute-start | bytes 1572872 | tf_op jit(solution)/shard_map/while/body/eval_jaxpr/ppermute | solution.py:19
  191.5 17.2 %collective-permute-start = (bf16[512,512]{0,1:T(8,128)(2,1)}, bf16[512,512]{0,1:T(8,128)(2,1)}, u32[]{:S(2)}, u32[]{:S(2)}) collective-permute-start(bf16[512,512]{0,1:T(8,128)(2,1)} %get-tuple-element.432), channel_id=1, source_target_pairs={{0,4},{4,8},{8,12},{12,0},{1,5},{5,9},{9,13},{13,1},{2,6},{6,10},{... | collective-permute-start | bytes 1572872 | tf_op jit(solution)/shard_map/while/body/eval_jaxpr/ppermute | solution.py:19
  191.5 16.9 %collective-permute-start.3 = (s32[512]{0:T(512)S(1)}, s32[512]{0:T(512)S(1)}, u32[]{:S(2)}, u32[]{:S(2)}) collective-permute-start(s32[512]{0:T(512)S(1)} %get-tuple-element.435), channel_id=1, source_target_pairs={{0,4},{4,8},{8,12},{12,0},{1,5},{5,9},{9,13},{13,1},{2,6},{6,10},{... | collective-permute-start | bytes 6152 | tf_op jit(solution)/shard_map/while/body/eval_jaxpr/ppermute | solution.py:19
  191.6 16.9 %collective-permute-start.2 = (s32[512]{0:T(512)S(1)}, s32[512]{0:T(512)S(1)}, u32[]{:S(2)}, u32[]{:S(2)}) collective-permute-start(s32[512]{0:T(512)S(1)} %get-tuple-element.434), channel_id=1, source_target_pairs={{0,4},{4,8},{8,12},{12,0},{1,5},{5,9},{9,13},{13,1},{2,6},{6,10},{... | collective-permute-start | bytes 6152 | tf_op jit(solution)/shard_map/while/body/eval_jaxpr/ppermute | solution.py:19
  192.3 25.4 %collective-permute-start.1 = (bf16[512,512]{0,1:T(8,128)(2,1)}, bf16[512,512]{0,1:T(8,128)(2,1)S(1)}, u32[]{:S(2)}, u32[]{:S(2)}) collective-permute-start(bf16[512,512]{0,1:T(8,128)(2,1)} %get-tuple-element.433), channel_id=1, source_target_pairs={{0,4},{4,8},{8,12},{12,0},{1,5},{5,9},{9,13},{13,1},{2,6},{6,10},{... | collective-permute-start | bytes 1572872 | tf_op jit(solution)/shard_map/while/body/eval_jaxpr/ppermute | solution.py:19
  228.6 151.3 %all-gather.20.cloned.1.call-start = ((), (), s32[]{:S(2)}) async-start(), calls=%async_computation.13 | async-start | bytes 9437184 | tf_op jit(solution)/shard_map/all_gather | solution.py:154
  229.2 232.9 %all-gather.18.cloned.1.call-start = ((), (), s32[]{:S(2)}) async-start(), calls=%async_computation.12 | async-start | bytes 9437184 | tf_op jit(solution)/shard_map/all_gather | solution.py:153
  230.0 314.3 %all-gather.22.cloned.1.call-start = ((), (), s32[]{:S(2)}) async-start(), calls=%async_computation.14 | async-start | bytes 9437184 | tf_op jit(solution)/shard_map/all_gather | solution.py:155
  230.7 409.5 %all-reduce.10.cloned.1.call-start = ((), (), s32[]{:S(2)}) async-start(), calls=%async_computation.15 | async-start | bytes 4194304 | tf_op jit(solution)/shard_map/psum | solution.py:78
  243.6 417.2 %copy-start.36 = (f32[8,1,256]{2,1,0:T(1,128)}, f32[8,1,256]{2,1,0:T(1,128)S(1)}, u32[]{:S(2)}) copy-start(f32[8,1,256]{2,1,0:T(1,128)S(1)} %convert_element_type.299) | copy-start | bytes 24580
  298.9 361.8 %copy-start.40 = (f32[512]{0:T(512)}, f32[512]{0:T(512)S(1)}, u32[]{:S(2)}) copy-start(f32[512]{0:T(512)S(1)} %add_rsqrt_fusion) | copy-start | bytes 6148
  572.1 411.2 %reduce-scatter.14.cloned.1.call-start = ((), (), s32[]{:S(2)}) async-start(), calls=%async_computation.19 | async-start | bytes 2359296 | tf_op jit(solution)/shard_map/reduce_scatter | solution.py:308
  665.0 320.2 %reduce-scatter.12.cloned.1.call-start = ((), (), s32[]{:S(2)}) async-start(), calls=%async_computation.18 | async-start | bytes 2359296 | tf_op jit(solution)/shard_map/reduce_scatter | solution.py:305
  665.2 240.0 %copy-start.39 = (f32[8,1,256]{2,1,0:T(1,128)S(1)}, f32[8,1,256]{2,1,0:T(1,128)}, u32[]{:S(2)}) copy-start(f32[8,1,256]{2,1,0:T(1,128)} %copy-done.38) | copy-start | bytes 24580
  665.2 240.0 %copy-start.43 = (f32[512]{0:T(512)S(1)}, f32[512]{0:T(512)}, u32[]{:S(2)}) copy-start(f32[512]{0:T(512)} %copy-done.42) | copy-start | bytes 6148
  665.3 26.0 %collective-permute-start.4 = (bf16[512,512]{0,1:T(8,128)(2,1)}, bf16[512,512]{0,1:T(8,128)(2,1)S(1)}, u32[]{:S(2)}, u32[]{:S(2)}) collective-permute-start(bf16[512,512]{0,1:T(8,128)(2,1)} %get-tuple-element.471), channel_id=1, source_target_pairs={{0,4},{4,8},{8,12},{12,0},{1,5},{5,9},{9,13},{13,1},{2,6},{6,10},{... | collective-permute-start | bytes 1572872 | tf_op jit(solution)/shard_map/while/body/eval_jaxpr/ppermute | solution.py:19
  666.8 22.6 %collective-permute-start.7 = (s32[512]{0:T(512)S(1)}, s32[512]{0:T(512)S(1)}, u32[]{:S(2)}, u32[]{:S(2)}) collective-permute-start(s32[512]{0:T(512)S(1)} %get-tuple-element.474), channel_id=1, source_target_pairs={{0,4},{4,8},{8,12},{12,0},{1,5},{5,9},{9,13},{13,1},{2,6},{6,10},{... | collective-permute-start | bytes 6152 | tf_op jit(solution)/shard_map/while/body/eval_jaxpr/ppermute | solution.py:19
  668.3 22.7 %collective-permute-start.6 = (s32[512]{0:T(512)S(1)}, s32[512]{0:T(512)S(1)}, u32[]{:S(2)}, u32[]{:S(2)}) collective-permute-start(s32[512]{0:T(512)S(1)} %get-tuple-element.473), channel_id=1, source_target_pairs={{0,4},{4,8},{8,12},{12,0},{1,5},{5,9},{9,13},{13,1},{2,6},{6,10},{... | collective-permute-start | bytes 6152 | tf_op jit(solution)/shard_map/while/body/eval_jaxpr/ppermute | solution.py:19
  669.8 91.5 %collective-permute-start.9 = (bf16[512,512]{0,1:T(8,128)(2,1)}, bf16[512,512]{0,1:T(8,128)(2,1)}, u32[]{:S(2)}, u32[]{:S(2)}) collective-permute-start(bf16[512,512]{0,1:T(8,128)(2,1)} %get-tuple-element.477), channel_id=1, source_target_pairs={{0,4},{4,8},{8,12},{12,0},{1,5},{5,9},{9,13},{13,1},{2,6},{6,10},{... | collective-permute-start | bytes 1572872 | tf_op jit(solution)/shard_map/while/body/eval_jaxpr/ppermute | solution.py:19
  670.3 96.0 %collective-permute-start.8 = (bf16[512,512]{0,1:T(8,128)(2,1)}, bf16[512,512]{0,1:T(8,128)(2,1)}, u32[]{:S(2)}, u32[]{:S(2)}) collective-permute-start(bf16[512,512]{0,1:T(8,128)(2,1)} %get-tuple-element.476), channel_id=1, source_target_pairs={{0,4},{4,8},{8,12},{12,0},{1,5},{5,9},{9,13},{13,1},{2,6},{6,10},{... | collective-permute-start | bytes 1572872 | tf_op jit(solution)/shard_map/while/body/eval_jaxpr/ppermute | solution.py:19
  689.4 64.6 %collective-permute-start.5 = (bf16[512,512]{0,1:T(8,128)(2,1)}, bf16[512,512]{0,1:T(8,128)(2,1)S(1)}, u32[]{:S(2)}, u32[]{:S(2)}) collective-permute-start(bf16[512,512]{0,1:T(8,128)(2,1)} %get-tuple-element.472), channel_id=1, source_target_pairs={{0,4},{4,8},{8,12},{12,0},{1,5},{5,9},{9,13},{13,1},{2,6},{6,10},{... | collective-permute-start | bytes 1572872 | tf_op jit(solution)/shard_map/while/body/eval_jaxpr/ppermute | solution.py:19
  691.3 62.7 %copy-start.50 = (bf16[512,8,64]{0,2,1:T(8,128)(2,1)S(1)}, bf16[512,8,64]{0,2,1:T(8,128)(2,1)}, u32[]{:S(2)}) copy-start(bf16[512,8,64]{0,2,1:T(8,128)(2,1)} %get-tuple-element.497) | copy-start | bytes 1572868 | tf_op jit(solution)/shard_map/while
  768.7 17.2 %collective-permute-start.4 = (bf16[512,512]{0,1:T(8,128)(2,1)}, bf16[512,512]{0,1:T(8,128)(2,1)S(1)}, u32[]{:S(2)}, u32[]{:S(2)}) collective-permute-start(bf16[512,512]{0,1:T(8,128)(2,1)} %get-tuple-element.471), channel_id=1, source_target_pairs={{0,4},{4,8},{8,12},{12,0},{1,5},{5,9},{9,13},{13,1},{2,6},{6,10},{... | collective-permute-start | bytes 1572872 | tf_op jit(solution)/shard_map/while/body/eval_jaxpr/ppermute | solution.py:19
  768.7 16.8 collective-permute-start.7
  769.8 15.8 collective-permute-start.6
  771.3 52.2 %collective-permute-start.9 = (bf16[512,512]{0,1:T(8,128)(2,1)}, bf16[512,512]{0,1:T(8,128)(2,1)}, u32[]{:S(2)}, u32[]{:S(2)}) collective-permute-start(bf16[512,512]{0,1:T(8,128)(2,1)} %get-tuple-element.477), channel_id=1, source_target_pairs={{0,4},{4,8},{8,12},{12,0},{1,5},{5,9},{9,13},{13,1},{2,6},{6,10},{... | collective-permute-start | bytes 1572872 | tf_op jit(solution)/shard_map/while/body/eval_jaxpr/ppermute | solution.py:19
  773.6 54.9 %collective-permute-start.8 = (bf16[512,512]{0,1:T(8,128)(2,1)}, bf16[512,512]{0,1:T(8,128)(2,1)}, u32[]{:S(2)}, u32[]{:S(2)}) collective-permute-start(bf16[512,512]{0,1:T(8,128)(2,1)} %get-tuple-element.476), channel_id=1, source_target_pairs={{0,4},{4,8},{8,12},{12,0},{1,5},{5,9},{9,13},{13,1},{2,6},{6,10},{... | collective-permute-start | bytes 1572872 | tf_op jit(solution)/shard_map/while/body/eval_jaxpr/ppermute | solution.py:19
  785.5 30.7 %collective-permute-start.5 = (bf16[512,512]{0,1:T(8,128)(2,1)}, bf16[512,512]{0,1:T(8,128)(2,1)S(1)}, u32[]{:S(2)}, u32[]{:S(2)}) collective-permute-start(bf16[512,512]{0,1:T(8,128)(2,1)} %get-tuple-element.472), channel_id=1, source_target_pairs={{0,4},{4,8},{8,12},{12,0},{1,5},{5,9},{9,13},{13,1},{2,6},{6,10},{... | collective-permute-start | bytes 1572872 | tf_op jit(solution)/shard_map/while/body/eval_jaxpr/ppermute | solution.py:19
  830.9 17.2 %collective-permute-start.4 = (bf16[512,512]{0,1:T(8,128)(2,1)}, bf16[512,512]{0,1:T(8,128)(2,1)S(1)}, u32[]{:S(2)}, u32[]{:S(2)}) collective-permute-start(bf16[512,512]{0,1:T(8,128)(2,1)} %get-tuple-element.471), channel_id=1, source_target_pairs={{0,4},{4,8},{8,12},{12,0},{1,5},{5,9},{9,13},{13,1},{2,6},{6,10},{... | collective-permute-start | bytes 1572872 | tf_op jit(solution)/shard_map/while/body/eval_jaxpr/ppermute | solution.py:19
  830.9 16.8 collective-permute-start.7
  831.2 16.6 collective-permute-start.6
  832.6 52.3 %collective-permute-start.9 = (bf16[512,512]{0,1:T(8,128)(2,1)}, bf16[512,512]{0,1:T(8,128)(2,1)}, u32[]{:S(2)}, u32[]{:S(2)}) collective-permute-start(bf16[512,512]{0,1:T(8,128)(2,1)} %get-tuple-element.477), channel_id=1, source_target_pairs={{0,4},{4,8},{8,12},{12,0},{1,5},{5,9},{9,13},{13,1},{2,6},{6,10},{... | collective-permute-start | bytes 1572872 | tf_op jit(solution)/shard_map/while/body/eval_jaxpr/ppermute | solution.py:19
  835.9 54.1 %collective-permute-start.8 = (bf16[512,512]{0,1:T(8,128)(2,1)}, bf16[512,512]{0,1:T(8,128)(2,1)}, u32[]{:S(2)}, u32[]{:S(2)}) collective-permute-start(bf16[512,512]{0,1:T(8,128)(2,1)} %get-tuple-element.476), channel_id=1, source_target_pairs={{0,4},{4,8},{8,12},{12,0},{1,5},{5,9},{9,13},{13,1},{2,6},{6,10},{... | collective-permute-start | bytes 1572872 | tf_op jit(solution)/shard_map/while/body/eval_jaxpr/ppermute | solution.py:19
  847.8 29.9 %collective-permute-start.5 = (bf16[512,512]{0,1:T(8,128)(2,1)}, bf16[512,512]{0,1:T(8,128)(2,1)S(1)}, u32[]{:S(2)}, u32[]{:S(2)}) collective-permute-start(bf16[512,512]{0,1:T(8,128)(2,1)} %get-tuple-element.472), channel_id=1, source_target_pairs={{0,4},{4,8},{8,12},{12,0},{1,5},{5,9},{9,13},{13,1},{2,6},{6,10},{... | collective-permute-start | bytes 1572872 | tf_op jit(solution)/shard_map/while/body/eval_jaxpr/ppermute | solution.py:19
  892.3 35.5 %copy-start.24 = (f32[512,32]{0,1:T(8,128)S(1)}, f32[512,32]{0,1:T(8,128)}, u32[]{:S(2)}) copy-start(f32[512,32]{0,1:T(8,128)} %copy-done.23) | copy-start | bytes 196612
  892.3 35.6 %copy-start.26 = (f32[512,32]{0,1:T(8,128)S(1)}, f32[512,32]{0,1:T(8,128)}, u32[]{:S(2)}) copy-start(f32[512,32]{0,1:T(8,128)} %copy-done.25) | copy-start | bytes 196612
  892.3 12.1 collective-permute-start.11
  908.0 100.1 %reduce-scatter.10.cloned.1.call-start = ((), (), s32[]{:S(2)}) async-start(), calls=%async_computation.17 | async-start | bytes 2359296 | tf_op jit(solution)/shard_map/reduce_scatter | solution.py:302
  908.1 19.6 %collective-permute-start.10 = (bf16[512,512]{0,1:T(8,128)(2,1)}, bf16[512,512]{0,1:T(8,128)(2,1)S(1)}, u32[]{:S(2)}, u32[]{:S(2)}) collective-permute-start(bf16[512,512]{0,1:T(8,128)(2,1)} %get-tuple-element.148), channel_id=1, source_target_pairs={{0,4},{4,8},{8,12},{12,0},{1,5},{5,9},{9,13},{13,1},{2,6},{6,10},{... | collective-permute-start | bytes 1572872 | tf_op jit(solution)/shard_map/ppermute | solution.py:19
  931.1 128.1 %reduce-scatter.8.cloned.1.call-start = ((), (), s32[]{:S(2)}) async-start(), calls=%async_computation.16 | async-start | bytes 2359296 | tf_op jit(solution)/shard_map/reduce_scatter | solution.py:299
  934.0 232.0 %all-reduce.12.cloned.1.call-start = ((), (), s32[]{:S(2)}) async-start(), calls=%async_computation.23 | async-start | bytes 8388608 | tf_op jit(solution)/shard_map/psum | solution.py:74
  950.5 385.3 %reduce-scatter.20.cloned.1.call-start = ((), (), s32[]{:S(2)}) async-start(), calls=%async_computation.22 | async-start | bytes 9437184 | tf_op jit(solution)/shard_map/reduce_scatter | solution.py:317
  960.8 544.9 %reduce-scatter.18.cloned.1.call-start = ((), (), s32[]{:S(2)}) async-start(), calls=%async_computation.21 | async-start | bytes 9437184 | tf_op jit(solution)/shard_map/reduce_scatter | solution.py:314
  971.0 704.8 %reduce-scatter.16.cloned.1.call-start = ((), (), s32[]{:S(2)}) async-start(), calls=%async_computation.20 | async-start | bytes 9437184 | tf_op jit(solution)/shard_map/reduce_scatter | solution.py:311
  981.5 187.5 %copy-start.44 = (bf16[2048]{0:T(1024)(128)(2,1)S(1)}, bf16[2048]{0:T(1024)(128)(2,1)}, u32[]{:S(2)}) copy-start(bf16[2048]{0:T(1024)(128)(2,1)} %get-tuple-element.172) | copy-start | bytes 12292
  981.5 208.4 %copy-start.37 = (f32[8,1,256]{2,1,0:T(1,128)S(1)}, f32[8,1,256]{2,1,0:T(1,128)}, u32[]{:S(2)}) copy-start(f32[8,1,256]{2,1,0:T(1,128)} %copy-done.36) | copy-start | bytes 24580
  981.5 208.4 %copy-start.41 = (f32[512]{0:T(512)S(1)}, f32[512]{0:T(512)}, u32[]{:S(2)}) copy-start(f32[512]{0:T(512)} %copy-done.40) | copy-start | bytes 6148
  981.5 208.4 %copy-start.46 = (f32[512]{0:T(512)S(1)}, f32[512]{0:T(512)}, u32[]{:S(2)}) copy-start(f32[512]{0:T(512)} %copy-done.45) | copy-start | bytes 6148
  (51 other events, 329.0 us)
Sparse Core Ops, SparseCore 0:
  9.6 32.0 all-gather.11
  43.2 28.5 all-gather.9
  73.4 28.5 all-gather.13
  103.4 36.3 all-gather.15
  228.8 67.6 all-reduce.7
  297.9 82.0 all-gather.19
  381.5 80.5 all-gather.17
  463.7 80.5 all-gather.21
  572.2 67.9 all-reduce.9
  665.1 88.9 reduce-scatter.13
  908.1 51.4 reduce-scatter.11
  961.8 46.2 reduce-scatter.9
  1011.0 48.2 reduce-scatter.7
  1063.2 102.8 all-reduce.11
  1168.2 167.5 reduce-scatter.19
  1337.9 167.8 reduce-scatter.17
  1507.9 167.8 reduce-scatter.15
where the time goes:
time: 1690 us
  waiting for transfers between devices  1300 us (77%)
  matrix products  186 us (11%)
  other arithmetic  64.5 us (4%)
  blocking collectives  50.7 us (3%)
  starting transfers between devices  34.9 us (2%)
  local copies, waits for them, and re-layouts  32.6 us (2%)
    ppermute x32, waiting for transfers between devices, passed_along(): return lax.ppermute(value, axis, pairs)  252 us
    reduce_scatter x1, waiting for transfers between devices, on_device(): lax.psum_scatter(grad_wup.astype(jnp.bfloat16), ('shard', 'context'), sca...  167 us
    reduce_scatter x1, waiting for transfers between devices, on_device(): lax.psum_scatter(grad_wgate.astype(jnp.bfloat16), ('shard', 'context'), s...  167 us
    psum x2, waiting for transfers between devices, branch_total(): lax.psum(partial_sum.astype(jnp.bfloat16), 'tensor').astype(jnp.float32)  158 us
    reduce_scatter x1, waiting for transfers between devices, on_device(): lax.psum_scatter(grad_wdown.astype(jnp.bfloat16), ('shard', 'context'), s...  138 us
    all_gather x1, waiting for transfers between devices, on_device(): lax.all_gather(w_up, ('shard', 'context'), axis=0, tiled=True)  78.6 us
    all_gather x1, waiting for transfers between devices, on_device(): lax.all_gather(w_gate, ('shard', 'context'), axis=0, tiled=True)  71.6 us
    all_gather x1, waiting for transfers between devices, on_device(): lax.all_gather(w_down, ('shard', 'context'), axis=0, tiled=True)  71.6 us
  transfers between devices with their start and end apart: 49, of which 28 were waited for; matrix products, arithmetic and copies ran while one was open for 13% of the time, Pallas kernels for 0%

commit v1 on v0

v1 whole, which is shorter than its diff:
```python
import math

import jax
import jax.numpy as jnp
from jax import lax
from jax.sharding import PartitionSpec as P

HD = 64


EPS = 1e-05
THETA = 130000.0
NEG = -1e30
ROWS = ("shard", "context")


def passed_along(value, axis, steps):
    count = lax.axis_size(axis)
    pairs = [(source, (source + steps) % count) for source in range(count)]
    return lax.ppermute(value, axis, pairs)


def rope_tables(position):
    index = jnp.arange(HD // 2, dtype=jnp.float32)
    inverse = jnp.power(jnp.float32(THETA), -2.0 * index / HD)
    angle = position.astype(jnp.float32)[:, None] * inverse[None, :]
    return (jnp.cos(angle), jnp.sin(angle))


def rotate(tensor, cosine, sine):
    half = tensor.shape[-1] // 2
    first = tensor[..., :half]
    second = tensor[..., half:]
    cosine = cosine[:, None, :]
    sine = sine[:, None, :]
    return jnp.concatenate(
        [first * cosine - second * sine, second * cosine + first * sine], axis=-1
    )


def rotate_back(grad, cosine, sine):
    half = grad.shape[-1] // 2
    first = grad[..., :half]
    second = grad[..., half:]
    cosine = cosine[:, None, :]
    sine = sine[:, None, :]
    return jnp.concatenate(
        [first * cosine + second * sine, second * cosine - first * sine], axis=-1
    )


def normalize(value):
    inv_rms = lax.rsqrt(jnp.mean(value * value, axis=-1, keepdims=True) + EPS)
    return (value * inv_rms, inv_rms)


def norm_back(grad, normed, inv_rms, gain):
    scaled = grad * gain.astype(jnp.float32)
    return inv_rms * (scaled - normed * jnp.mean(scaled * normed, axis=-1, keepdims=True))


def contract_last(left, right):
    return lax.dot_general(
        left, right, (((1,), (1,)), ((), ())), preferred_element_type=jnp.float32
    )


def contract_first(left, right):
    return lax.dot_general(
        left, right, (((0,), (0,)), ((), ())), preferred_element_type=jnp.float32
    )


def half_of(value, bit):
    size = value.shape[0] // 2
    return lax.dynamic_slice_in_dim(value, bit * size, size, axis=0)


def joined(mine, other, bit):
    low = jnp.where(bit == 0, mine, other)
    high = jnp.where(bit == 0, other, mine)
    return jnp.concatenate([low, high], axis=0)


def tensor_total(partial_sum):
    count = lax.axis_size("tensor")
    rows = partial_sum.shape[0]
    if count != 4 or rows % 8:
        return lax.psum(partial_sum.astype(jnp.bfloat16), "tensor").astype(jnp.float32)
    f32 = jnp.float32
    bf16 = jnp.bfloat16
    index = lax.axis_index("tensor")
    x_bit = index % 2
    y_bit = index // 2
    x_pairs = [(i, i ^ 1) for i in range(4)]
    y_pairs = [(i, i ^ 2) for i in range(4)]

    def swap(value, pairs):
        return lax.ppermute(value.astype(bf16), "tensor", pairs).astype(f32)

    first = partial_sum[: rows // 2]
    second = partial_sum[rows // 2 :]
    first = half_of(first, x_bit) + swap(half_of(first, 1 - x_bit), x_pairs)
    second = half_of(second, y_bit) + swap(half_of(second, 1 - y_bit), y_pairs)
    first = half_of(first, y_bit) + swap(half_of(first, 1 - y_bit), y_pairs)
    second = half_of(second, x_bit) + swap(half_of(second, 1 - x_bit), x_pairs)
    first = first.astype(bf16)
    second = second.astype(bf16)
    first = joined(first, lax.ppermute(first, "tensor", y_pairs), y_bit)
    second = joined(second, lax.ppermute(second, "tensor", x_pairs), x_bit)
    first = joined(first, lax.ppermute(first, "tensor", x_pairs), x_bit)
    second = joined(second, lax.ppermute(second, "tensor", y_pairs), y_bit)
    return jnp.concatenate([first, second], axis=0).astype(f32)


def rows_total(grad):
    staged = lax.psum_scatter(grad.astype(jnp.bfloat16), "shard", scatter_dimension=0, tiled=True)
    return lax.psum_scatter(staged, "context", scatter_dimension=0, tiled=True).astype(jnp.float32)


def pass_grads(grad_key, grad_value):
    return (
        passed_along(grad_key.astype(jnp.bfloat16), "context", 1).astype(grad_key.dtype),
        passed_along(grad_value.astype(jnp.bfloat16), "context", 1).astype(grad_value.dtype),
    )


def key_scores(query_heads, query_seg, query_pos, piece):
    key_flat, value_flat, key_seg, key_pos = piece
    heads = query_heads.shape[1]
    key_heads = key_flat.reshape(key_flat.shape[0], heads, HD)
    value_heads = value_flat.reshape(value_flat.shape[0], heads, HD)
    scores = jnp.einsum(
        "qhd,khd->hqk", query_heads, key_heads, preferred_element_type=jnp.float32
    ) * (1.0 / math.sqrt(HD))
    allowed = (query_seg[:, None] == key_seg[None, :]) & (key_pos[None, :] <= query_pos[:, None])
    return (jnp.where(allowed[None], scores, NEG), allowed, key_heads, value_heads)


def forward_fold(stats, piece, query_heads, query_seg, query_pos):
    peak, total, accum = stats
    scores, allowed, key_heads, value_heads = key_scores(query_heads, query_seg, query_pos, piece)
    new_peak = jnp.maximum(peak, jnp.max(scores, axis=-1))
    weights = jnp.where(allowed[None], jnp.exp(scores - new_peak[..., None]), 0.0)
    factor = jnp.exp(peak - new_peak)
    total = total * factor + jnp.sum(weights, axis=-1)
    accum = accum * factor[..., None] + jnp.einsum(
        "hqk,khd->hqd",
        weights.astype(jnp.bfloat16),
        value_heads,
        preferred_element_type=jnp.float32,
    )
    return (new_peak, total, accum)


def backward_piece(piece, query_heads, grad_heads, log_total, inner, query_seg, query_pos):
    scores, allowed, key_heads, value_heads = key_scores(query_heads, query_seg, query_pos, piece)
    probs = jnp.where(allowed[None], jnp.exp(scores - log_total[..., None]), 0.0)
    grad_value = jnp.einsum(
        "hqk,qhd->khd", probs.astype(jnp.bfloat16), grad_heads, preferred_element_type=jnp.float32
    )
    grad_probs = jnp.einsum(
        "qhd,khd->hqk", grad_heads, value_heads, preferred_element_type=jnp.float32
    )
    grad_scores = (probs * (grad_probs - inner[..., None]) * (1.0 / math.sqrt(HD))).astype(
        jnp.bfloat16
    )
    grad_query = jnp.einsum(
        "hqk,khd->qhd", grad_scores, key_heads, preferred_element_type=jnp.float32
    )
    grad_key = jnp.einsum(
        "hqk,qhd->khd", grad_scores, query_heads, preferred_element_type=jnp.float32
    )
    key_rows = grad_key.shape[0]
    return (grad_query, grad_key.reshape(key_rows, -1), grad_value.reshape(key_rows, -1))


class RingAttention:
    def __init__(self, query, key_flat, value_flat, segment, position, cosine, sine):
        self.query = query
        self.piece = (key_flat, value_flat, segment, position)
        self.segment = segment
        self.position = position
        self.cosine = cosine
        self.sine = sine

    def forward(self):
        f32 = jnp.float32
        query, segment, position = self.query, self.segment, self.position
        rows, heads = query.shape[0], query.shape[1]
        start_stats = (
            jnp.full((heads, rows), NEG, f32),
            jnp.zeros((heads, rows), f32),
            jnp.zeros((heads, rows, HD), f32),
        )
        stats = forward_fold(start_stats, self.piece, query, segment, position)

        def cycle_turn(index, carry):
            moving, current = carry
            moving = passed_along(moving, "context", 1)
            current = forward_fold(current, moving, query, segment, position)
            return (moving, current)

        peak, total, accum = lax.fori_loop(
            0, lax.axis_size("context") - 1, cycle_turn, (self.piece, stats)
        )[1]
        self.attended = jnp.transpose(accum / total[..., None], (1, 0, 2)).astype(jnp.bfloat16)
        self.log_total = peak + jnp.log(total)
        return self.attended

    def backward(self, grad_heads):
        bf16 = jnp.bfloat16
        query, segment, position = self.query, self.segment, self.position
        rows, heads = query.shape[0], query.shape[1]
        inner = jnp.sum(grad_heads.astype(jnp.float32) * self.attended.astype(jnp.float32), axis=-1).T

        def piece_grads(piece):
            return backward_piece(piece, query, grad_heads, self.log_total, inner, segment, position)

        grad_query, grad_key, grad_value = piece_grads(self.piece)

        def grad_turn(index, carry):
            moving, acc_query, acc_key, acc_value = carry
            moving = passed_along(moving, "context", 1)
            acc_key, acc_value = pass_grads(acc_key, acc_value)
            part_query, part_key, part_value = piece_grads(moving)
            return (moving, acc_query + part_query, acc_key + part_key, acc_value + part_value)

        carried = lax.fori_loop(
            0,
            lax.axis_size("context") - 1,
            grad_turn,
            (self.piece, grad_query, grad_key, grad_value),
        )
        grad_query = carried[1]
        grad_key, grad_value = pass_grads(carried[2], carried[3])
        grad_qin = rotate_back(grad_query, self.cosine, self.sine).astype(bf16)
        grad_kin = rotate_back(grad_key.reshape(rows, heads, HD), self.cosine, self.sine).astype(bf16)
        grad_vin = grad_value.astype(bf16).reshape(rows, heads, HD)
        return grad_qin, grad_kin, grad_vin


class HeadAttention:
    BLOCK = 512

    def __init__(self, query, key_heads, value_heads, segment, position, cosine, sine):
        ways = lax.axis_size("context")
        rows, heads = query.shape[0], query.shape[1]
        self.ways = ways
        self.rows = rows
        self.heads = heads
        self.group = heads // ways
        stacked = jnp.stack([query, key_heads, value_heads], axis=1)
        stacked = stacked.reshape(rows, 3, ways, self.group, HD)
        stacked = lax.all_to_all(stacked, "context", 2, 0, tiled=True)
        stacked = stacked.reshape(rows * ways, 3, self.group, HD)
        self.query = stacked[:, 0]
        self.keys = stacked[:, 1]
        self.values = stacked[:, 2]
        tags = jnp.stack([segment, position], axis=0)[None]
        tags = jnp.broadcast_to(tags, (ways, 2, rows))
        tags = lax.all_to_all(tags, "context", 0, 0, tiled=True)
        tags = jnp.transpose(tags, (1, 0, 2)).reshape(2, rows * ways)
        self.seg_all = tags[0]
        self.pos_all = tags[1]
        self.cos_all, self.sin_all = rope_tables(self.pos_all)

    def _blocks(self):
        total = self.rows * self.ways
        block = min(self.BLOCK, total)
        return [(start, block) for start in range(0, total, block)]

    def _scores(self, start, size):
        query = lax.dynamic_slice_in_dim(self.query, start, size, axis=0)
        seg_q = lax.dynamic_slice_in_dim(self.seg_all, start, size, axis=0)
        pos_q = lax.dynamic_slice_in_dim(self.pos_all, start, size, axis=0)
        scores = jnp.einsum(
            "qhd,khd->hqk", query, self.keys, preferred_element_type=jnp.float32
        ) * (1.0 / math.sqrt(HD))
        allowed = (seg_q[:, None] == self.seg_all[None, :]) & (
            self.pos_all[None, :] <= pos_q[:, None]
        )
        return query, jnp.where(allowed[None], scores, NEG), allowed

    def forward(self):
        outs = []
        logs = []
        for start, size in self._blocks():
            _, scores, allowed = self._scores(start, size)
            peak = jnp.max(scores, axis=-1)
            weights = jnp.where(allowed[None], jnp.exp(scores - peak[..., None]), 0.0)
            total = jnp.sum(weights, axis=-1)
            mixed = jnp.einsum(
                "hqk,khd->qhd",
                weights.astype(jnp.bfloat16),
                self.values,
                preferred_element_type=jnp.float32,
            )
            outs.append((mixed / total.T[:, :, None]).astype(jnp.bfloat16))
            logs.append(peak + jnp.log(total))
        self.attended = jnp.concatenate(outs, axis=0)
        self.log_total = jnp.concatenate(logs, axis=1)
        back = self.attended.reshape(self.rows * self.ways, 1, self.group, HD)
        back = lax.all_to_all(back, "context", 0, 1, tiled=True)
        return back.reshape(self.rows, self.heads, HD)

    def backward(self, grad_heads):
        f32 = jnp.float32
        bf16 = jnp.bfloat16
        scale = 1.0 / math.sqrt(HD)
        grad = grad_heads.reshape(self.rows, self.ways, self.group, HD)
        grad = lax.all_to_all(grad, "context", 1, 0, tiled=True)
        grad = grad.reshape(self.rows * self.ways, self.group, HD)
        inner = jnp.sum(grad.astype(f32) * self.attended.astype(f32), axis=-1).T
        grad_key = jnp.zeros(self.keys.shape, f32)
        grad_value = jnp.zeros(self.values.shape, f32)
        grad_queries = []
        for start, size in self._blocks():
            query, scores, allowed = self._scores(start, size)
            log_block = lax.dynamic_slice_in_dim(self.log_total, start, size, axis=1)
            inner_block = lax.dynamic_slice_in_dim(inner, start, size, axis=1)
            grad_block = lax.dynamic_slice_in_dim(grad, start, size, axis=0)
            probs = jnp.where(allowed[None], jnp.exp(scores - log_block[..., None]), 0.0)
            grad_value = grad_value + jnp.einsum(
                "hqk,qhd->khd", probs.astype(bf16), grad_block, preferred_element_type=f32
            )
            grad_probs = jnp.einsum(
                "qhd,khd->hqk", grad_block, self.values, preferred_element_type=f32
            )
            grad_scores = (probs * (grad_probs - inner_block[..., None]) * scale).astype(bf16)
            grad_queries.append(
                jnp.einsum("hqk,khd->qhd", grad_scores, self.keys, preferred_element_type=f32)
            )
            grad_key = grad_key + jnp.einsum(
                "hqk,qhd->khd", grad_scores, query, preferred_element_type=f32
            )
        grad_query = jnp.concatenate(grad_queries, axis=0)
        grad_qin = rotate_back(grad_query, self.cos_all, self.sin_all).astype(bf16)
        grad_kin = rotate_back(grad_key, self.cos_all, self.sin_all).astype(bf16)
        grad_vin = grad_value.astype(bf16)
        stacked = jnp.stack([grad_qin, grad_kin, grad_vin], axis=1)
        stacked = stacked.reshape(self.rows * self.ways, 3, 1, self.group, HD)
        stacked = lax.all_to_all(stacked, "context", 0, 2, tiled=True)
        stacked = stacked.reshape(self.rows, 3, self.heads, HD)
        return stacked[:, 0], stacked[:, 1], stacked[:, 2]


def on_device(
    inputs, segments, positions, w_q, w_k, w_v, w_o, w_gate, w_up, w_down, g_attn, g_mlp, d_out
):
    f32 = jnp.float32
    bf16 = jnp.bfloat16
    rows = inputs.shape[1]
    width = inputs.shape[2]
    cols = w_q.shape[1]
    tokens = inputs.reshape(rows, width)
    segment = segments.reshape(rows)
    position = positions.reshape(rows)
    full_qkv = lax.all_gather(jnp.concatenate([w_q, w_k, w_v], axis=1), ROWS, axis=0, tiled=True)
    full_o = lax.all_gather(w_o, ROWS, axis=0, tiled=True)
    gains = lax.all_gather(
        jnp.concatenate([g_attn, g_mlp])[None], ROWS, axis=0, tiled=True
    )
    gain_attn = gains[:, : g_attn.shape[0]].reshape(width)
    gain_mlp = gains[:, g_attn.shape[0] :].reshape(width)
    full_gate = lax.all_gather(w_gate, ROWS, axis=0, tiled=True)
    full_up = lax.all_gather(w_up, ROWS, axis=0, tiled=True)
    full_down = lax.all_gather(w_down, ROWS, axis=0, tiled=True)
    heads = cols // HD
    cosine, sine = rope_tables(position)
    resid1 = tokens.astype(f32)
    norm1, inv1 = normalize(resid1)
    h1 = (norm1 * gain_attn.astype(f32)).astype(bf16)
    projected = jnp.dot(h1, full_qkv, preferred_element_type=f32)
    query = rotate(projected[:, :cols].reshape(rows, heads, HD), cosine, sine).astype(bf16)
    key_heads = rotate(projected[:, cols : 2 * cols].reshape(rows, heads, HD), cosine, sine).astype(
        bf16
    )
    value_heads = projected[:, 2 * cols :].astype(bf16).reshape(rows, heads, HD)
    if heads % lax.axis_size("context") == 0:
        attention = HeadAttention(query, key_heads, value_heads, segment, position, cosine, sine)
    else:
        attention = RingAttention(
            query,
            key_heads.reshape(rows, cols),
            value_heads.reshape(rows, cols),
            segment,
            position,
            cosine,
            sine,
        )
    attended = attention.forward()
    attended_flat = attended.reshape(rows, cols)
    resid2 = resid1 + tensor_total(contract_last(attended_flat, full_o))
    norm2, inv2 = normalize(resid2)
    h2_part = (norm2 * gain_mlp.astype(f32)).astype(bf16)
    gate = jnp.dot(h2_part, full_gate, preferred_element_type=f32)
    up = jnp.dot(h2_part, full_up, preferred_element_type=f32)
    active = jax.nn.silu(gate)
    hidden = (active * up).astype(bf16)
    grad_y = d_out.reshape(rows, width)
    reduced_down = rows_total(contract_first(grad_y, hidden))
    result = (resid2 + tensor_total(contract_last(hidden, full_down))).astype(bf16)
    grad_hidden = jnp.dot(grad_y, full_down, preferred_element_type=f32)
    sigma = jax.nn.sigmoid(gate)
    grad_gate = (grad_hidden * up * sigma * (1.0 + gate * (1.0 - sigma))).astype(bf16)
    grad_up = (grad_hidden * active).astype(bf16)
    reduced_gate = rows_total(contract_first(h2_part, grad_gate))
    reduced_up = rows_total(contract_first(h2_part, grad_up))
    grad_h2 = tensor_total(contract_last(grad_gate, full_gate) + contract_last(grad_up, full_up))
    grad_gmlp = jnp.sum(grad_h2 * norm2, axis=0)
    grad_resid = grad_y.astype(f32) + norm_back(grad_h2, norm2, inv2, gain_mlp)
    grad_resid_part = grad_resid.astype(bf16)
    reduced_o = rows_total(contract_first(grad_resid_part, attended_flat))
    grad_heads = (
        jnp.dot(grad_resid_part, full_o, preferred_element_type=f32)
        .astype(bf16)
        .reshape(rows, heads, HD)
    )
    grad_qin, grad_kin, grad_vin = attention.backward(grad_heads)
    grad_qkv = jnp.concatenate(
        [grad_qin.reshape(rows, cols), grad_kin.reshape(rows, cols), grad_vin.reshape(rows, cols)],
        axis=1,
    )
    grad_h1 = tensor_total(contract_last(grad_qkv, full_qkv))
    grad_gattn = jnp.sum(grad_h1 * norm1, axis=0)
    grad_x_part = (grad_resid + norm_back(grad_h1, norm1, inv1, gain_attn)).astype(bf16)
    reduced_qkv = rows_total(contract_first(h1, grad_qkv))
    reduced_gains = lax.psum_scatter(
        jnp.stack([grad_gattn, grad_gmlp], axis=1), ROWS, scatter_dimension=0, tiled=True
    )
    return (
        result.reshape(1, rows, width),
        grad_x_part.reshape(1, rows, width),
        reduced_qkv[:, :cols],
        reduced_qkv[:, cols : 2 * cols],
        reduced_qkv[:, 2 * cols :],
        reduced_o,
        reduced_gate,
        reduced_up,
        reduced_down,
        reduced_gains[:, 0],
        reduced_gains[:, 1],
    )


def solution(mesh):
    placed = (
        P("shard", "context", None),
        P("shard", "context"),
        P("shard", "context"),
        P(ROWS, "tensor"),
        P(ROWS, "tensor"),
        P(ROWS, "tensor"),
        P(ROWS, "tensor"),
        P(ROWS, "tensor"),
        P(ROWS, "tensor"),
        P(ROWS, "tensor"),
        P(ROWS),
        P(ROWS),
        P("shard", "context", None),
    )
    return jax.shard_map(
        on_device,
        mesh=mesh,
        in_specs=placed,
        out_specs=(
            P("shard", "context", None),
            P("shard", "context", None),
            P(ROWS, "tensor"),
            P(ROWS, "tensor"),
            P(ROWS, "tensor"),
            P(ROWS, "tensor"),
            P(ROWS, "tensor"),
            P(ROWS, "tensor"),
            P(ROWS, "tensor"),
            P(ROWS),
            P(ROWS),
        ),
        check_vma=False,
    )
```

time: 1690 us -> 1140 us (0.67)
  waiting for transfers between devices: 1300 us -> 645 us
  local copies, waits for them, and re-layouts: 32.6 us -> 77.9 us
  starting transfers between devices: 34.9 us -> 66.6 us
    psum x3 -> x0, waiting for transfers between devices: 226 us -> none  [the longest x2 158 us: branch_total(): lax.psum(partial_sum.astype(jnp.bfloat16), 'tensor').astype(jnp.float32)]
    reduce_scatter x7 -> x10, waiting for transfers between devices: 543 us -> 347 us  [the longest x5 302 us: rows_total(): lax.psum_scatter(staged, 'context', scatter_dimension=0, tiled=True)]
    all_gather x7 -> x5, waiting for transfers between devices: 275 us -> 98.3 us  [the longest x1 63.2 us: on_device(): full_gate = lax.all_gather(w_gate, ROWS, axis=0, tiled=True)]
    ppermute x32, waiting for transfers between devices: 252 us -> 97.9 us  [the longest x16 57 us: swap(): return lax.ppermute(value.astype(bf16), 'tensor', pairs).astype(f32)]
    all_to_all x0 -> x4, waiting for transfers between devices: none -> 98.9 us  [the longest x1 59.2 us: __init__(): stacked = lax.all_to_all(stacked, 'context', 2, 0, tiled=True)]
    all_to_all x0 -> x1, blocking collectives: none -> 38.5 us  [backward(): stacked = lax.all_to_all(stacked, 'context', 0, 2, tiled=True)]
    unnamed x1 -> x0, blocking collectives: 19.6 us -> none
    all_to_all x0 -> x4, starting transfers between devices: none -> 19.2 us  [the longest x1 6.35 us: __init__(): tags = lax.all_to_all(tags, 'context', 0, 0, tiled=True)]
  transfers between devices with their start and end apart: 49 -> 52, of which waited for: 28 -> 35; matrix products, arithmetic and copies ran while one was open for 13% -> 17% of each run, Pallas kernels for 0% -> 0%
where the time goes in v1:
time: 1140 us; the launch traced here: 1130 us
  waiting for transfers between devices  645 us (57%)
  matrix products  192 us (17%)
  local copies, waits for them, and re-layouts  77.9 us (7%)
  other arithmetic  72.7 us (6%)
  starting transfers between devices  66.6 us (6%)
  blocking collectives  61.8 us (5%)
  between operations  16.1 us (1%)
    reduce_scatter x5, waiting for transfers between devices, rows_total(): lax.psum_scatter(staged, 'context', scatter_dimension=0, tiled=True)  302 us
    all_gather x1, waiting for transfers between devices, on_device(): full_gate = lax.all_gather(w_gate, ROWS, axis=0, tiled=True)  63.2 us
    all_to_all x1, waiting for transfers between devices, __init__(): stacked = lax.all_to_all(stacked, 'context', 2, 0, tiled=True)  59.2 us
    ppermute x16, waiting for transfers between devices, swap(): return lax.ppermute(value.astype(bf16), 'tensor', pairs).astype(f32)  57 us
    reduce_scatter x5, waiting for transfers between devices, rows_total(): lax.psum_scatter(grad.astype(jnp.bfloat16), 'shard', scatter_dimension=0,...  44.2 us
    dot_general x5, matrix products, contract_first(): lax.dot_general(left, right, (((0,), (0,)), ((), ())), preferred_element_...  42.5 us
    all_to_all x1, blocking collectives, backward(): stacked = lax.all_to_all(stacked, 'context', 0, 2, tiled=True)  38.5 us
    all_gather x1, waiting for transfers between devices, on_device(): lax.all_gather(jnp.concatenate([w_q, w_k, w_v], axis=1), ROWS, axis=0, ti...  35.1 us
  transfers between devices with their start and end apart: 52, of which 35 were waited for; matrix products, arithmetic and copies ran while one was open for 17% of the time, Pallas kernels for 0%

profile of v1, /device:TPU:0, one launch (start us, length us, event | category | flops | bytes accessed | tf_op | source)
XLA Modules:
  0.0 1132.6 jit_solution(13529478597352263801)
XLA Ops:
  12.2 6.3 all-to-all-start.1
  18.6 23.3 %all-gather.1 = bf16[8,1,512]{2,1,0:T(2,128)(2,1)S(1)} all-gather(bf16[1,1,512]{2,1,0:T(2,128)(2,1)S(1)} %reshape.1044), channel_id=2, replica_groups=mesh['shard'=2,'context'=4,'tensor'=4] {'shard','context'}, dimensions={0}, use_global_device_ids=true | all-gather | bytes 9216 | tf_op jit(solution)/shard_map/all_gather | solution.py:361
  42.7 35.1 %all-gather.8.cloned.1.call-done = bf16[2048,1536]{1,0:T(8,128)(2,1)} async-done(((bf16[256,1536]{1,0:T(8,128)(2,1)}), bf16[2048,1536]{1,0:T(8,128)(2,1)}) %all-gather.8.cloned.1.call-update) | async-done | bytes 6291472 | tf_op jit(solution)/shard_map/all_gather | solution.py:359
  77.8 5.6 fusion.129
  96.0 4.4 all-to-all-start
  101.0 4.5 compare_and_fusion.3
  105.5 59.2 %all-to-all-done = bf16[512,3,4,2,64]{0,4,3,1,2:T(8,128)(2,1)} async-done(((bf16[512,3,4,2,64]{0,4,3,1,2:T(8,128)(2,1)}), bf16[512,3,4,2,64]{0,4,3,1,2:T(8,128)(2,1)}, u32[]{:S(2)}, u32[]{:S(2)}) %all-to-all-start) | async-done | bytes 1572896 | tf_op jit(solution)/shard_map/all_to_all | solution.py:255
  164.7 3.8 copy.48
  168.5 3.8 reshape.1034
  177.9 6.0 fusion
  193.4 5.7 fusion.4
  209.8 4.1 all-to-all-start.2
  214.0 27.9 %all-to-all-done.2 = bf16[4,2,32768]{2,1,0:T(2,128)(2,1)} async-done(((bf16[4,2,32768]{2,1,0:T(2,128)(2,1)}), bf16[4,2,32768]{2,1,0:T(2,128)(2,1)}, u32[]{:S(2)}, u32[]{:S(2)}) %all-to-all-start.2) | async-done | bytes 524320 | tf_op jit(solution)/shard_map/all_to_all | solution.py:304
  257.5 5.7 collective-permute-done
  268.7 5.0 collective-permute-done.1
  287.0 10.6 fusion.82
  301.2 4.9 multiply_convert_fusion.7
  306.1 11.3 fusion.180
  317.4 63.2 %all-gather.12.cloned.1.call-done = bf16[2048,2048]{1,0:T(8,128)(2,1)} async-done(((bf16[256,2048]{1,0:T(8,128)(2,1)}), bf16[2048,2048]{1,0:T(8,128)(2,1)}) %all-gather.12.cloned.1.call-update) | async-done | bytes 8388624 | tf_op jit(solution)/shard_map/all_gather | solution.py:366
  380.6 14.5 %multiply_convert_fusion.4 = (bf16[512,2048]{1,0:T(8,128)(2,1)}, bf16[512,2048]{1,0:T(8,128)(2,1)S(1)}, bf16[512,2048]{1,0:T(8,128)(2,1)}) fusion(f32[512,2048]{1,0:T(8,128)} %fusion.82, f32[512,2048]{1,0:T(8,128)} %fusion.180, bf16[512,2048]{1,0:T(8,128)(2,1)} %multiply_convert_fusion.7, bf16[2048,2048]{1,0:T(8,128)(2,1)} %all-gather.12.cloned.1.call-done), kind=kOutput, calls=%fused_computation.65 | convolution fusion | flops 4310695936 | bytes 25165824 | tf_op jit(solution)/shard_map/dot_general | solution.py:397
  395.1 7.9 fusion.182
  403.1 6.1 convolution_add_fusion
  412.7 11.0 collective-permute-done.16
  427.1 4.4 collective-permute-done.17
  456.3 3.9 fusion.28
  460.3 6.5 fusion.87
  466.8 4.3 all-to-all-start.3
  471.2 11.7 %all-to-all-done.3 = bf16[512,4,2,64]{0,3,2,1:T(8,128)(2,1)} async-done(((bf16[512,4,2,64]{0,3,2,1:T(8,128)(2,1)}), bf16[512,4,2,64]{0,3,2,1:T(8,128)(2,1)}, u32[]{:S(2)}, u32[]{:S(2)}) %all-to-all-start.3) | async-done | bytes 524320 | tf_op jit(solution)/shard_map/all_to_all | solution.py:312
  484.7 6.5 multiply_convert_fusion.3
  493.5 5.2 fusion.43
  498.7 4.8 multiply_convert_fusion.2
  506.2 6.4 multiply_convert_fusion.1
  515.2 5.6 multiply_convert_fusion
  523.4 3.7 fusion.65
  527.1 5.2 fusion.68
  532.3 3.7 fusion.77
  537.7 8.5 copy.53
  546.2 5.0 reshape.1051
  551.2 38.5 %all_to_all.65 = bf16[4,2,98304]{2,1,0:T(2,128)(2,1)} all-to-all(bf16[4,2,98304]{2,1,0:T(2,128)(2,1)} %reshape.1051), channel_id=1, replica_groups=mesh['shard'=2,'context'=4,'tensor'=4] {'context'}, dimensions={0} | all-to-all | bytes 3145728 | tf_op jit(solution)/shard_map/all_to_all | solution.py:343
  589.7 5.0 reshape.1052
  594.7 8.7 copy.58
  605.3 6.2 fusion.127
  614.1 9.8 collective-permute-done.24
  627.7 3.9 collective-permute-done.25
  638.7 3.9 collective-permute-done.30
  644.8 5.1 collective-permute-done.27
  654.9 10.3 fusion.37
  667.9 7.3 convolution_convert_fusion.2
  675.3 10.4 convolution_convert_fusion.1
  685.8 11.2 convolution_convert_fusion
  697.3 11.0 convert_bitcast_fusion
  711.1 4.6 reduce-scatter.22.cloned.1.call-done
  715.7 19.9 %reduce-scatter.26.cloned.1.call-done = bf16[1024,2048]{1,0:T(8,128)(2,1)} async-done(((bf16[2048,2048]{1,0:T(8,128)(2,1)}), bf16[1024,2048]{1,0:T(8,128)(2,1)}) %reduce-scatter.26.cloned.1.call-update) | async-done | bytes 4194320 | tf_op jit(solution)/shard_map/reduce_scatter | solution.py:117
  735.8 19.6 %reduce-scatter.30.cloned.1.call-done = bf16[1024,2048]{0,1:T(8,128)(2,1)} async-done(((bf16[2048,2048]{0,1:T(8,128)(2,1)}), bf16[1024,2048]{0,1:T(8,128)(2,1)}) %reduce-scatter.30.cloned.1.call-update) | async-done | bytes 4194320 | tf_op jit(solution)/shard_map/reduce_scatter | solution.py:117
  755.4 7.6 fusion.181
  766.9 10.7 collective-permute-done.8
  781.3 4.4 collective-permute-done.9
  788.9 4.0 collective-permute-done.10
  796.0 9.3 collective-permute-done.11
  811.1 13.0 %reduce-scatter.20.cloned.1.call-done = bf16[256,512]{1,0:T(8,128)(2,1)} async-done(((bf16[1024,512]{1,0:T(8,128)(2,1)}), bf16[256,512]{1,0:T(8,128)(2,1)}) %reduce-scatter.20.cloned.1.call-update) | async-done | bytes 262160 | tf_op jit(solution)/shard_map/reduce_scatter | solution.py:118
  825.9 59.4 %reduce-scatter.16.cloned.1.call-done = bf16[256,1536]{1,0:T(8,128)(2,1)} async-done(((bf16[1024,1536]{1,0:T(8,128)(2,1)}), bf16[256,1536]{1,0:T(8,128)(2,1)}) %reduce-scatter.16.cloned.1.call-update) | async-done | bytes 786448 | tf_op jit(solution)/shard_map/reduce_scatter | solution.py:118
  887.6 76.6 %reduce-scatter.24.cloned.1.call-done = bf16[256,2048]{1,0:T(8,128)(2,1)} async-done(((bf16[1024,2048]{1,0:T(8,128)(2,1)}), bf16[256,2048]{1,0:T(8,128)(2,1)}) %reduce-scatter.24.cloned.1.call-update) | async-done | bytes 1048592 | tf_op jit(solution)/shard_map/reduce_scatter | solution.py:118
  966.9 76.7 %reduce-scatter.28.cloned.1.call-done = bf16[256,2048]{1,0:T(8,128)(2,1)} async-done(((bf16[1024,2048]{1,0:T(8,128)(2,1)}), bf16[256,2048]{1,0:T(8,128)(2,1)}) %reduce-scatter.28.cloned.1.call-update) | async-done | bytes 1048592 | tf_op jit(solution)/shard_map/reduce_scatter | solution.py:118
  1046.4 76.7 %reduce-scatter.32.cloned.1.call-done = bf16[256,2048]{0,1:T(8,128)(2,1)} async-done(((bf16[1024,2048]{0,1:T(8,128)(2,1)}), bf16[256,2048]{0,1:T(8,128)(2,1)}) %reduce-scatter.32.cloned.1.call-update) | async-done | bytes 1048592 | tf_op jit(solution)/shard_map/reduce_scatter | solution.py:118
  (366 shorter events, 187.2 us)
Async XLA Ops:
  7.2 34.7 %copy-start = (bf16[1,512,2048]{2,1,0:T(8,128)(2,1)S(1)}, bf16[1,512,2048]{2,1,0:T(8,128)(2,1)}, u32[]{:S(2)}) copy-start(bf16[1,512,2048]{2,1,0:T(8,128)(2,1)} %param.13) | copy-start | bytes 6291460
  7.2 70.6 %all-gather.8.cloned.1.call-start = ((), (), s32[]{:S(2)}) async-start(), calls=%async_computation.16 | async-start | bytes 7077888 | tf_op jit(solution)/shard_map/all_gather | solution.py:359
  9.5 237.2 %all-gather.10.cloned.1.call-start = ((), (), s32[]{:S(2)}) async-start(), calls=%async_computation.17 | async-start | bytes 2359296 | tf_op jit(solution)/shard_map/all_gather | solution.py:360
  10.2 276.7 %all-gather.16.cloned.1.call-start = ((), (), s32[]{:S(2)}) async-start(), calls=%async_computation.20 | async-start | bytes 9437184 | tf_op jit(solution)/shard_map/all_gather | solution.py:368
  11.0 295.2 %all-gather.14.cloned.1.call-start = ((), (), s32[]{:S(2)}) async-start(), calls=%async_computation.19 | async-start | bytes 9437184 | tf_op jit(solution)/shard_map/all_gather | solution.py:367
  12.2 83.8 %all-to-all-start.1 = ((s32[4,2,512]{2,1,0:T(2,128)}), s32[4,2,512]{2,1,0:T(2,128)S(1)}, u32[]{:S(2)}, u32[]{:S(2)}) async-start(s32[4,2,512]{2,1,0:T(2,128)} %broadcast_in_dim.158), calls=%async_computation.1 | async-start | bytes 32768 | tf_op jit(solution)/shard_map/all_to_all | solution.py:262
  41.9 41.5 %copy-start.51 = (f32[1,2,8,128]{3,1,2,0:T(2,128)}, f32[1,2,8,128]{3,1,2,0:T(2,128)S(1)}, u32[]{:S(2)}) copy-start(f32[1,2,8,128]{3,1,2,0:T(2,128)S(1)} %copy.64) | copy-start | bytes 24580
  42.4 41.0 %copy-start.53 = (f32[512]{0:T(512)}, f32[512]{0:T(512)S(1)}, u32[]{:S(2)}) copy-start(f32[512]{0:T(512)S(1)} %add_rsqrt_fusion.1) | copy-start | bytes 6148
  96.0 68.7 %all-to-all-start = ((bf16[512,3,4,2,64]{0,4,3,1,2:T(8,128)(2,1)}), bf16[512,3,4,2,64]{0,4,3,1,2:T(8,128)(2,1)}, u32[]{:S(2)}, u32[]{:S(2)}) async-start(bf16[512,3,4,2,64]{0,4,3,1,2:T(8,128)(2,1)} %copy.47), calls=%async_computation | async-start | bytes 3145728 | tf_op jit(solution)/shard_map/all_to_all | solution.py:255
  100.4 280.3 %all-gather.12.cloned.1.call-start = ((), (), s32[]{:S(2)}) async-start(), calls=%async_computation.18 | async-start | bytes 9437184 | tf_op jit(solution)/shard_map/all_gather | solution.py:366
  105.5 96.4 %copy-start.25 = (pred[512,2048]{1,0:T(8,128)(4,1)}, pred[512,2048]{1,0:T(8,128)(4,1)S(1)}, u32[]{:S(2)}) copy-start(pred[512,2048]{1,0:T(8,128)(4,1)S(1)} %get-tuple-element.135) | copy-start | bytes 3145732
  209.8 32.1 %all-to-all-start.2 = ((bf16[4,2,32768]{2,1,0:T(2,128)(2,1)}), bf16[4,2,32768]{2,1,0:T(2,128)(2,1)}, u32[]{:S(2)}, u32[]{:S(2)}) async-start(bf16[4,2,32768]{2,1,0:T(2,128)(2,1)} %reshape.1049), calls=%async_computation.2 | async-start | bytes 1048576 | tf_op jit(solution)/shard_map/all_to_all | solution.py:304
  252.9 10.3 collective-permute-start
  254.4 13.6 %copy-start.15 = (f32[256,2048]{1,0:T(8,128)S(1)}, f32[256,2048]{1,0:T(8,128)}, u32[]{:S(2)}) copy-start(f32[256,2048]{1,0:T(8,128)} %get-tuple-element.71) | copy-start | bytes 6291460
  256.0 12.1 %collective-permute-start.4 = (bf16[128,2048]{1,0:T(8,128)(2,1)S(1)}, bf16[128,2048]{1,0:T(8,128)(2,1)S(1)}, u32[]{:S(2)}, u32[]{:S(2)}) collective-permute-start(bf16[128,2048]{1,0:T(8,128)(2,1)S(1)} %dynamic-slice_convert_fusion.6), channel_id=1, source_target_pairs={{0,2},{1,3},{2,0},{3,1},{4,6},{5,7},{6,4},{7,5},{8,10},{9,11},{10,... | collective-permute-start | bytes 1572872 | tf_op jit(solution)/shard_map/ppermute | solution.py:99
  264.6 9.2 collective-permute-start.1
  268.2 7.1 collective-permute-start.5
  273.8 6.7 collective-permute-start.2
  275.4 9.2 collective-permute-start.6
  281.3 16.3 %collective-permute-start.3 = (bf16[128,2048]{1,0:T(8,128)(2,1)S(1)}, bf16[128,2048]{1,0:T(8,128)(2,1)}, u32[]{:S(2)}, u32[]{:S(2)}) collective-permute-start(bf16[128,2048]{1,0:T(8,128)(2,1)S(1)} %pad_maximum_fusion.11), channel_id=1, source_target_pairs={{0,1},{1,0},{2,3},{3,2},{4,5},{5,4},{6,7},{7,6},{8,9},{9,8},{10,11... | collective-permute-start | bytes 1572872 | tf_op jit(solution)/shard_map/ppermute | solution.py:111
  286.2 12.7 %collective-permute-start.7 = (bf16[128,2048]{1,0:T(8,128)(2,1)}, bf16[128,2048]{1,0:T(8,128)(2,1)}, u32[]{:S(2)}, u32[]{:S(2)}) collective-permute-start(bf16[128,2048]{1,0:T(8,128)(2,1)} %pad_maximum_fusion.12), channel_id=1, source_target_pairs={{0,2},{1,3},{2,0},{3,1},{4,6},{5,7},{6,4},{7,5},{8,10},{9,11},{10,... | collective-permute-start | bytes 1572872 | tf_op jit(solution)/shard_map/ppermute | solution.py:112
  409.6 14.1 %collective-permute-start.16 = (bf16[128,2048]{1,0:T(8,128)(2,1)S(1)}, bf16[128,2048]{1,0:T(8,128)(2,1)S(1)}, u32[]{:S(2)}, u32[]{:S(2)}) collective-permute-start(bf16[128,2048]{1,0:T(8,128)(2,1)S(1)} %dynamic-slice_convert_fusion.3), channel_id=1, source_target_pairs={{0,1},{1,0},{2,3},{3,2},{4,5},{5,4},{6,7},{7,6},{8,9},{9,8},{10,11... | collective-permute-start | bytes 1572872 | tf_op jit(solution)/shard_map/ppermute | solution.py:99
  411.2 14.2 %collective-permute-start.20 = (bf16[128,2048]{1,0:T(8,128)(2,1)S(1)}, bf16[128,2048]{1,0:T(8,128)(2,1)S(1)}, u32[]{:S(2)}, u32[]{:S(2)}) collective-permute-start(bf16[128,2048]{1,0:T(8,128)(2,1)S(1)} %dynamic-slice_convert_fusion.2), channel_id=1, source_target_pairs={{0,2},{1,3},{2,0},{3,1},{4,6},{5,7},{6,4},{7,5},{8,10},{9,11},{10,... | collective-permute-start | bytes 1572872 | tf_op jit(solution)/shard_map/ppermute | solution.py:99
  423.9 7.7 collective-permute-start.17
  425.6 7.6 collective-permute-start.21
  431.6 6.8 collective-permute-start.18
  433.2 8.3 collective-permute-start.22
  440.0 11.8 %collective-permute-start.19 = (bf16[128,2048]{1,0:T(8,128)(2,1)}, bf16[128,2048]{1,0:T(8,128)(2,1)}, u32[]{:S(2)}, u32[]{:S(2)}) collective-permute-start(bf16[128,2048]{1,0:T(8,128)(2,1)} %pad_maximum_fusion.15), channel_id=1, source_target_pairs={{0,1},{1,0},{2,3},{3,2},{4,5},{5,4},{6,7},{7,6},{8,9},{9,8},{10,11... | collective-permute-start | bytes 1572872 | tf_op jit(solution)/shard_map/ppermute | solution.py:111
  443.1 11.5 %collective-permute-start.23 = (bf16[128,2048]{1,0:T(8,128)(2,1)}, bf16[128,2048]{1,0:T(8,128)(2,1)}, u32[]{:S(2)}, u32[]{:S(2)}) collective-permute-start(bf16[128,2048]{1,0:T(8,128)(2,1)} %pad_maximum_fusion.16), channel_id=1, source_target_pairs={{0,2},{1,3},{2,0},{3,1},{4,6},{5,7},{6,4},{7,5},{8,10},{9,11},{10,... | collective-permute-start | bytes 1572872 | tf_op jit(solution)/shard_map/ppermute | solution.py:112
  466.8 16.1 %all-to-all-start.3 = ((bf16[512,4,2,64]{0,3,2,1:T(8,128)(2,1)}), bf16[512,4,2,64]{0,3,2,1:T(8,128)(2,1)}, u32[]{:S(2)}, u32[]{:S(2)}) async-start(bf16[512,4,2,64]{0,3,2,1:T(8,128)(2,1)} %bitcast.321), calls=%async_computation.3 | async-start | bytes 1048576 | tf_op jit(solution)/shard_map/all_to_all | solution.py:312
  471.1 238.7 %reduce-scatter.18.cloned.1.call-start = ((), (), s32[]{:S(2)}) async-start(), calls=%async_computation.23 | async-start | bytes 3145728 | tf_op jit(solution)/shard_map/reduce_scatter | solution.py:117
  612.2 11.8 %collective-permute-start.24 = (bf16[128,2048]{1,0:T(8,128)(2,1)S(1)}, bf16[128,2048]{1,0:T(8,128)(2,1)S(1)}, u32[]{:S(2)}, u32[]{:S(2)}) collective-permute-start(bf16[128,2048]{1,0:T(8,128)(2,1)S(1)} %dynamic-slice_convert_fusion.1), channel_id=1, source_target_pairs={{0,1},{1,0},{2,3},{3,2},{4,5},{5,4},{6,7},{7,6},{8,9},{9,8},{10,11... | collective-permute-start | bytes 1572872 | tf_op jit(solution)/shard_map/ppermute | solution.py:99
  612.5 13.2 %collective-permute-start.28 = (bf16[128,2048]{1,0:T(8,128)(2,1)S(1)}, bf16[128,2048]{1,0:T(8,128)(2,1)S(1)}, u32[]{:S(2)}, u32[]{:S(2)}) collective-permute-start(bf16[128,2048]{1,0:T(8,128)(2,1)S(1)} %dynamic-slice_convert_fusion), channel_id=1, source_target_pairs={{0,2},{1,3},{2,0},{3,1},{4,6},{5,7},{6,4},{7,5},{8,10},{9,11},{10,... | collective-permute-start | bytes 1572872 | tf_op jit(solution)/shard_map/ppermute | solution.py:99
  624.1 7.5 collective-permute-start.25
  625.9 7.4 collective-permute-start.29
  631.7 6.8 collective-permute-start.26
  633.3 18.9 %copy-start.52 = (f32[1,2,8,128]{3,1,2,0:T(2,128)S(1)}, f32[1,2,8,128]{3,1,2,0:T(2,128)}, u32[]{:S(2)}) copy-start(f32[1,2,8,128]{3,1,2,0:T(2,128)} %copy-done.51) | copy-start | bytes 24580
  633.4 18.9 %copy-start.54 = (f32[512]{0:T(512)S(1)}, f32[512]{0:T(512)}, u32[]{:S(2)}) copy-start(f32[512]{0:T(512)} %copy-done.53) | copy-start | bytes 6148
  633.4 9.2 collective-permute-start.30
  638.6 11.4 %collective-permute-start.27 = (bf16[128,2048]{1,0:T(8,128)(2,1)S(1)}, bf16[128,2048]{1,0:T(8,128)(2,1)S(1)}, u32[]{:S(2)}, u32[]{:S(2)}) collective-permute-start(bf16[128,2048]{1,0:T(8,128)(2,1)S(1)} %pad_maximum_fusion.17), channel_id=1, source_target_pairs={{0,1},{1,0},{2,3},{3,2},{4,5},{5,4},{6,7},{7,6},{8,9},{9,8},{10,11... | collective-permute-start | bytes 1572872 | tf_op jit(solution)/shard_map/ppermute | solution.py:111
  642.7 12.1 %copy-start.3 = (bf16[128,2048]{1,0:T(8,128)(2,1)S(1)}, bf16[128,2048]{1,0:T(8,128)(2,1)}, u32[]{:S(2)}) copy-start(bf16[128,2048]{1,0:T(8,128)(2,1)} %copy-done.1) | copy-start | bytes 1572868
  642.7 12.1 %copy-start.7 = (bf16[128,2048]{1,0:T(8,128)(2,1)S(1)}, bf16[128,2048]{1,0:T(8,128)(2,1)}, u32[]{:S(2)}) copy-start(bf16[128,2048]{1,0:T(8,128)(2,1)} %copy-done.5) | copy-start | bytes 1572868
  642.7 12.1 %copy-start.18 = (bf16[128,2048]{1,0:T(8,128)(2,1)S(1)}, bf16[128,2048]{1,0:T(8,128)(2,1)}, u32[]{:S(2)}) copy-start(bf16[128,2048]{1,0:T(8,128)(2,1)} %copy-done.17) | copy-start | bytes 1572868
  642.8 9.2 collective-permute-start.31
  667.9 42.5 %reduce-scatter.14.cloned.1.call-start = ((), (), s32[]{:S(2)}) async-start(), calls=%async_computation.21 | async-start | bytes 9437184 | tf_op jit(solution)/shard_map/reduce_scatter | solution.py:117
  675.3 40.4 %reduce-scatter.22.cloned.1.call-start = ((), (), s32[]{:S(2)}) async-start(), calls=%async_computation.25 | async-start | bytes 12582912 | tf_op jit(solution)/shard_map/reduce_scatter | solution.py:117
  685.7 50.0 %reduce-scatter.26.cloned.1.call-start = ((), (), s32[]{:S(2)}) async-start(), calls=%async_computation.27 | async-start | bytes 12582912 | tf_op jit(solution)/shard_map/reduce_scatter | solution.py:117
  697.0 58.4 %reduce-scatter.30.cloned.1.call-start = ((), (), s32[]{:S(2)}) async-start(), calls=%async_computation.29 | async-start | bytes 12582912 | tf_op jit(solution)/shard_map/reduce_scatter | solution.py:117
  708.3 100.4 %reduce-scatter.34.cloned.1.call-start = ((), (), s32[]{:S(2)}) async-start(), calls=%async_computation.31 | async-start | bytes 1179648
  709.7 114.3 %reduce-scatter.20.cloned.1.call-start = ((), (), s32[]{:S(2)}) async-start(), calls=%async_computation.24 | async-start | bytes 1310720 | tf_op jit(solution)/shard_map/reduce_scatter | solution.py:118
  710.3 175.0 %reduce-scatter.16.cloned.1.call-start = ((), (), s32[]{:S(2)}) async-start(), calls=%async_computation.22 | async-start | bytes 3932160 | tf_op jit(solution)/shard_map/reduce_scatter | solution.py:118
  711.1 253.1 %reduce-scatter.24.cloned.1.call-start = ((), (), s32[]{:S(2)}) async-start(), calls=%async_computation.26 | async-start | bytes 5242880 | tf_op jit(solution)/shard_map/reduce_scatter | solution.py:118
  715.7 327.9 %reduce-scatter.28.cloned.1.call-start = ((), (), s32[]{:S(2)}) async-start(), calls=%async_computation.28 | async-start | bytes 5242880 | tf_op jit(solution)/shard_map/reduce_scatter | solution.py:118
  735.7 387.4 %reduce-scatter.32.cloned.1.call-start = ((), (), s32[]{:S(2)}) async-start(), calls=%async_computation.30 | async-start | bytes 5242880 | tf_op jit(solution)/shard_map/reduce_scatter | solution.py:118
  763.4 14.2 %collective-permute-start.8 = (bf16[128,2048]{1,0:T(8,128)(2,1)S(1)}, bf16[128,2048]{1,0:T(8,128)(2,1)S(1)}, u32[]{:S(2)}, u32[]{:S(2)}) collective-permute-start(bf16[128,2048]{1,0:T(8,128)(2,1)S(1)} %dynamic-slice_convert_fusion.5), channel_id=1, source_target_pairs={{0,1},{1,0},{2,3},{3,2},{4,5},{5,4},{6,7},{7,6},{8,9},{9,8},{10,11... | collective-permute-start | bytes 1572872 | tf_op jit(solution)/shard_map/ppermute | solution.py:99
  765.4 14.2 %collective-permute-start.12 = (bf16[128,2048]{1,0:T(8,128)(2,1)S(1)}, bf16[128,2048]{1,0:T(8,128)(2,1)S(1)}, u32[]{:S(2)}, u32[]{:S(2)}) collective-permute-start(bf16[128,2048]{1,0:T(8,128)(2,1)S(1)} %dynamic-slice_convert_fusion.4), channel_id=1, source_target_pairs={{0,2},{1,3},{2,0},{3,1},{4,6},{5,7},{6,4},{7,5},{8,10},{9,11},{10,... | collective-permute-start | bytes 1572872 | tf_op jit(solution)/shard_map/ppermute | solution.py:99
  777.8 7.9 collective-permute-start.9
  779.7 7.6 collective-permute-start.13
  785.7 7.1 collective-permute-start.10
  787.4 18.8 %copy-start.4 = (bf16[128,2048]{1,0:T(8,128)(2,1)S(1)}, bf16[128,2048]{1,0:T(8,128)(2,1)}, u32[]{:S(2)}) copy-start(bf16[128,2048]{1,0:T(8,128)(2,1)} %copy-done.1) | copy-start | bytes 1572868
  787.4 18.8 %copy-start.8 = (bf16[128,2048]{1,0:T(8,128)(2,1)S(1)}, bf16[128,2048]{1,0:T(8,128)(2,1)}, u32[]{:S(2)}) copy-start(bf16[128,2048]{1,0:T(8,128)(2,1)} %copy-done.5) | copy-start | bytes 1572868
  787.4 7.1 collective-permute-start.14
  793.0 12.3 %collective-permute-start.11 = (bf16[128,2048]{1,0:T(8,128)(2,1)S(1)}, bf16[128,2048]{1,0:T(8,128)(2,1)S(1)}, u32[]{:S(2)}, u32[]{:S(2)}) collective-permute-start(bf16[128,2048]{1,0:T(8,128)(2,1)S(1)} %pad_maximum_fusion.13), channel_id=1, source_target_pairs={{0,1},{1,0},{2,3},{3,2},{4,5},{5,4},{6,7},{7,6},{8,9},{9,8},{10,11... | collective-permute-start | bytes 1572872 | tf_op jit(solution)/shard_map/ppermute | solution.py:111
  794.6 11.4 %collective-permute-start.15 = (bf16[128,2048]{1,0:T(8,128)(2,1)S(1)}, bf16[128,2048]{1,0:T(8,128)(2,1)S(1)}, u32[]{:S(2)}, u32[]{:S(2)}) collective-permute-start(bf16[128,2048]{1,0:T(8,128)(2,1)S(1)} %pad_maximum_fusion.14), channel_id=1, source_target_pairs={{0,2},{1,3},{2,0},{3,1},{4,6},{5,7},{6,4},{7,5},{8,10},{9,11},{10,... | collective-permute-start | bytes 1572872 | tf_op jit(solution)/shard_map/ppermute | solution.py:112
  (55 other events, 336.9 us)
Sparse Core Ops, SparseCore 0:
  10.2 67.5 all-gather.7
  79.4 37.3 all-gather.9
  118.4 90.7 all-gather.15
  210.7 87.3 all-gather.13
  299.5 81.0 all-gather.11
  668.0 9.2 reduce-scatter.17
  679.6 15.3 reduce-scatter.13
  697.2 18.4 reduce-scatter.21
  718.0 17.6 reduce-scatter.25
  737.8 17.5 reduce-scatter.29
  758.2 37.2 reduce-scatter.33
  797.7 26.2 reduce-scatter.19
  826.4 58.8 reduce-scatter.15
  887.4 76.6 reduce-scatter.23
  966.3 77.2 reduce-scatter.27
  1045.8 77.2 reduce-scatter.31

commit v2 on v1

--- a/solution.py
+++ b/solution.py
@@ -113,9 +113,16 @@
     return jnp.concatenate([first, second], axis=0).astype(f32)
 
 
+def chip_total(grad):
+    return lax.psum_scatter(grad.astype(jnp.bfloat16), "shard", scatter_dimension=0, tiled=True)
+
+
+def line_total(staged):
+    return lax.psum_scatter(staged, "context", scatter_dimension=0, tiled=True).astype(jnp.float32)
+
+
 def rows_total(grad):
-    staged = lax.psum_scatter(grad.astype(jnp.bfloat16), "shard", scatter_dimension=0, tiled=True)
-    return lax.psum_scatter(staged, "context", scatter_dimension=0, tiled=True).astype(jnp.float32)
+    return line_total(chip_total(grad))
 
 
 def pass_grads(grad_key, grad_value):
@@ -208,7 +215,7 @@
         self.log_total = peak + jnp.log(total)
         return self.attended
 
-    def backward(self, grad_heads):
+    def backward(self, grad_heads, early, late):
         bf16 = jnp.bfloat16
         query, segment, position = self.query, self.segment, self.position
         rows, heads = query.shape[0], query.shape[1]
@@ -237,7 +244,7 @@
         grad_qin = rotate_back(grad_query, self.cosine, self.sine).astype(bf16)
         grad_kin = rotate_back(grad_key.reshape(rows, heads, HD), self.cosine, self.sine).astype(bf16)
         grad_vin = grad_value.astype(bf16).reshape(rows, heads, HD)
-        return grad_qin, grad_kin, grad_vin
+        return grad_qin, grad_kin, grad_vin, early, late
 
 
 class HeadAttention:
@@ -304,12 +311,13 @@
         back = lax.all_to_all(back, "context", 0, 1, tiled=True)
         return back.reshape(self.rows, self.heads, HD)
 
-    def backward(self, grad_heads):
+    def backward(self, grad_heads, early, late):
         f32 = jnp.float32
         bf16 = jnp.bfloat16
         scale = 1.0 / math.sqrt(HD)
         grad = grad_heads.reshape(self.rows, self.ways, self.group, HD)
         grad = lax.all_to_all(grad, "context", 1, 0, tiled=True)
+        grad, early = lax.optimization_barrier((grad, early))
         grad = grad.reshape(self.rows * self.ways, self.group, HD)
         inner = jnp.sum(grad.astype(f32) * self.attended.astype(f32), axis=-1).T
         grad_key = jnp.zeros(self.keys.shape, f32)
@@ -339,10 +347,18 @@
         grad_kin = rotate_back(grad_key, self.cos_all, self.sin_all).astype(bf16)
         grad_vin = grad_value.astype(bf16)
         stacked = jnp.stack([grad_qin, grad_kin, grad_vin], axis=1)
+        stacked, late = lax.optimization_barrier((stacked, late))
         stacked = stacked.reshape(self.rows * self.ways, 3, 1, self.group, HD)
         stacked = lax.all_to_all(stacked, "context", 0, 2, tiled=True)
         stacked = stacked.reshape(self.rows, 3, self.heads, HD)
-        return stacked[:, 0], stacked[:, 1], stacked[:, 2]
+        return stacked[:, 0], stacked[:, 1], stacked[:, 2], early, late
+
+
+def mlp_chunks(hidden_cols):
+    for count in (2, 1):
+        if hidden_cols % (count * 128) == 0:
+            return count
+    return 1
 
 
 def on_device(
@@ -353,6 +369,7 @@
     rows = inputs.shape[1]
     width = inputs.shape[2]
     cols = w_q.shape[1]
+    hidden_cols = w_gate.shape[1]
     tokens = inputs.reshape(rows, width)
     segment = segments.reshape(rows)
     position = positions.reshape(rows)
@@ -363,9 +380,17 @@
     )
     gain_attn = gains[:, : g_attn.shape[0]].reshape(width)
     gain_mlp = gains[:, g_attn.shape[0] :].reshape(width)
-    full_gate = lax.all_gather(w_gate, ROWS, axis=0, tiled=True)
-    full_up = lax.all_gather(w_up, ROWS, axis=0, tiled=True)
-    full_down = lax.all_gather(w_down, ROWS, axis=0, tiled=True)
+    count = mlp_chunks(hidden_cols)
+    step = hidden_cols // count
+    fetched = []
+    for index in range(count):
+        part = slice(index * step, (index + 1) * step)
+        fetched.append(
+            tuple(
+                lax.all_gather(weight[:, part], ROWS, axis=0, tiled=True)
+                for weight in (w_gate, w_up, w_down)
+            )
+        )
     heads = cols // HD
     cosine, sine = rope_tables(position)
     resid1 = tokens.astype(f32)
@@ -394,40 +419,65 @@
     resid2 = resid1 + tensor_total(contract_last(attended_flat, full_o))
     norm2, inv2 = normalize(resid2)
     h2_part = (norm2 * gain_mlp.astype(f32)).astype(bf16)
-    gate = jnp.dot(h2_part, full_gate, preferred_element_type=f32)
-    up = jnp.dot(h2_part, full_up, preferred_element_type=f32)
-    active = jax.nn.silu(gate)
-    hidden = (active * up).astype(bf16)
     grad_y = d_out.reshape(rows, width)
-    reduced_down = rows_total(contract_first(grad_y, hidden))
-    result = (resid2 + tensor_total(contract_last(hidden, full_down))).astype(bf16)
-    grad_hidden = jnp.dot(grad_y, full_down, preferred_element_type=f32)
-    sigma = jax.nn.sigmoid(gate)
-    grad_gate = (grad_hidden * up * sigma * (1.0 + gate * (1.0 - sigma))).astype(bf16)
-    grad_up = (grad_hidden * active).astype(bf16)
-    reduced_gate = rows_total(contract_first(h2_part, grad_gate))
-    reduced_up = rows_total(contract_first(h2_part, grad_up))
-    grad_h2 = tensor_total(contract_last(grad_gate, full_gate) + contract_last(grad_up, full_up))
+    mlp_partial = None
+    h2_grad_partial = None
+    staged = []
+    for full_gate, full_up, full_down in fetched:
+        gate = jnp.dot(h2_part, full_gate, preferred_element_type=f32)
+        up = jnp.dot(h2_part, full_up, preferred_element_type=f32)
+        active = jax.nn.silu(gate)
+        hidden = (active * up).astype(bf16)
+        out_part = contract_last(hidden, full_down)
+        mlp_partial = out_part if mlp_partial is None else mlp_partial + out_part
+        grad_hidden = jnp.dot(grad_y, full_down, preferred_element_type=f32)
+        sigma = jax.nn.sigmoid(gate)
+        grad_gate = (grad_hidden * up * sigma * (1.0 + gate * (1.0 - sigma))).astype(bf16)
+        grad_up = (grad_hidden * active).astype(bf16)
+        back_part = contract_last(grad_gate, full_gate) + contract_last(grad_up, full_up)
+        pending = (
+            contract_first(h2_part, grad_gate),
+            contract_first(h2_part, grad_up),
+            contract_first(grad_y, hidden),
+        )
+        if staged:
+            back_part, staged[-1] = lax.optimization_barrier((back_part, staged[-1]))
+        h2_grad_partial = back_part if h2_grad_partial is None else h2_grad_partial + back_part
+        staged.append(tuple(chip_total(value) for value in pending))
+    grad_h2 = tensor_total(h2_grad_partial)
+    grad_h2, staged[-1] = lax.optimization_barrier((grad_h2, staged[-1]))
+    reduced = [tuple(line_total(value) for value in chunk) for chunk in staged]
+    result = (resid2 + tensor_total(mlp_partial)).astype(bf16)
     grad_gmlp = jnp.sum(grad_h2 * norm2, axis=0)
     grad_resid = grad_y.astype(f32) + norm_back(grad_h2, norm2, inv2, gain_mlp)
     grad_resid_part = grad_resid.astype(bf16)
-    reduced_o = rows_total(contract_first(grad_resid_part, attended_flat))
     grad_heads = (
         jnp.dot(grad_resid_part, full_o, preferred_element_type=f32)
         .astype(bf16)
         .reshape(rows, heads, HD)
     )
-    grad_qin, grad_kin, grad_vin = attention.backward(grad_heads)
+    grad_heads, partial_o = lax.optimization_barrier(
+        (grad_heads, contract_first(grad_resid_part, attended_flat))
+    )
+    early = (chip_total(partial_o), reduced[:-1])
+    grad_qin, grad_kin, grad_vin, early, late = attention.backward(grad_heads, early, reduced[-1])
+    staged_o, reduced[:-1] = early
+    reduced[-1] = late
+    reduced_o = line_total(staged_o)
     grad_qkv = jnp.concatenate(
         [grad_qin.reshape(rows, cols), grad_kin.reshape(rows, cols), grad_vin.reshape(rows, cols)],
         axis=1,
     )
     grad_h1 = tensor_total(contract_last(grad_qkv, full_qkv))
+    grad_h1, reduced_o = lax.optimization_barrier((grad_h1, reduced_o))
     grad_gattn = jnp.sum(grad_h1 * norm1, axis=0)
     grad_x_part = (grad_resid + norm_back(grad_h1, norm1, inv1, gain_attn)).astype(bf16)
     reduced_qkv = rows_total(contract_first(h1, grad_qkv))
     reduced_gains = lax.psum_scatter(
         jnp.stack([grad_gattn, grad_gmlp], axis=1), ROWS, scatter_dimension=0, tiled=True
+    )
+    reduced_gate, reduced_up, reduced_down = (
+        jnp.concatenate([chunk[which] for chunk in reduced], axis=1) for which in range(3)
     )
     return (
         result.reshape(1, rows, width),

time: 1140 us -> 1100 us (0.965)
  waiting for transfers between devices: 645 us -> 568 us
  blocking collectives: 61.8 us -> 24.1 us
  other arithmetic: 72.7 us -> 107 us
  local copies, waits for them, and re-layouts: 77.9 us -> 95.9 us
  matrix products: 192 us -> 209 us
    reduce_scatter x10 -> x16, waiting for transfers between devices: 347 us -> 225 us  [the longest x8 209 us: line_total(): lax.psum_scatter(staged, 'context', scatter_dimension=0, tiled=True)]
    all_to_all x0 -> x1, waiting for transfers between devices: none -> 53 us  [backward(): stacked = lax.all_to_all(stacked, 'context', 0, 2, tiled=True)]
    all_to_all x1 -> x0, blocking collectives: 38.5 us -> none  [backward(): stacked = lax.all_to_all(stacked, 'context', 0, 2, tiled=True)]
    ppermute x4, waiting for transfers between devices: 3.7 us -> 15.4 us  [tensor_total(): second = joined(second, lax.ppermute(second, 'tensor', y_pairs), y_bit)]
    unnamed x146 -> x228, local copies, waits for them, and re-layouts: 24.1 us -> 34.1 us
    all_gather x3 -> x6, waiting for transfers between devices: 63.2 us -> 57 us  [on_device(): lax.all_gather(weight[:, part], ROWS, axis=0, tiled=True)]
    dot_general x5 -> x8, matrix products: 42.5 us -> 43.5 us  [contract_first(): lax.dot_general(left, right, (((0,), (0,)), ((), ())), preferred_element_...]
    dot_general x5 -> x8, matrix products: 31 us -> 30.9 us  [contract_last(): lax.dot_general(left, right, (((1,), (1,)), ((), ())), preferred_element_...]
  transfers between devices with their start and end apart: 52 -> 62, of which waited for: 35 -> 42; matrix products, arithmetic and copies ran while one was open for 17% -> 35% of each run, Pallas kernels for 0% -> 0%
where the time goes in v2:
time: 1100 us; the launch traced here: 1090 us
  waiting for transfers between devices  568 us (52%)
  matrix products  209 us (19%)
  other arithmetic  107 us (10%)
  local copies, waits for them, and re-layouts  95.9 us (9%)
  starting transfers between devices  69.4 us (6%)
  blocking collectives  24.1 us (2%)
  between operations  16.5 us (2%)
    reduce_scatter x8, waiting for transfers between devices, line_total(): lax.psum_scatter(staged, 'context', scatter_dimension=0, tiled=True)  209 us
    ppermute x16, waiting for transfers between devices, swap(): return lax.ppermute(value.astype(bf16), 'tensor', pairs).astype(f32)  59.8 us
    all_gather x6, waiting for transfers between devices, on_device(): lax.all_gather(weight[:, part], ROWS, axis=0, tiled=True)  57 us
    all_to_all x1, waiting for transfers between devices, __init__(): stacked = lax.all_to_all(stacked, 'context', 2, 0, tiled=True)  54.5 us
    all_to_all x1, waiting for transfers between devices, backward(): stacked = lax.all_to_all(stacked, 'context', 0, 2, tiled=True)  53 us
    dot_general x8, matrix products, contract_first(): lax.dot_general(left, right, (((0,), (0,)), ((), ())), preferred_element_...  43.5 us
    unnamed x228, local copies, waits for them, and re-layouts  34.1 us
    dot_general x8, matrix products, contract_last(): lax.dot_general(left, right, (((1,), (1,)), ((), ())), preferred_element_...  30.9 us
  transfers between devices with their start and end apart: 62, of which 42 were waited for; matrix products, arithmetic and copies ran while one was open for 35% of the time, Pallas kernels for 0%

profile of v2, /device:TPU:0, one launch (start us, length us, event | category | flops | bytes accessed | tf_op | source)
XLA Modules:
  0.0 1089.5 jit_solution(5106185330423082750)
XLA Ops:
  17.3 6.3 all-to-all-start.1
  23.7 24.1 %all-gather.1 = bf16[8,1,512]{2,1,0:T(2,128)(2,1)S(1)} all-gather(bf16[1,1,512]{2,1,0:T(2,128)(2,1)S(1)} %reshape.803), channel_id=2, replica_groups=mesh['shard'=2,'context'=4,'tensor'=4] {'shard','context'}, dimensions={0}, use_global_device_ids=true | all-gather | bytes 9216 | tf_op jit(solution)/shard_map/all_gather | solution.py:378
  48.7 29.5 %all-gather.11.cloned.1.call-done = bf16[2048,1536]{1,0:T(8,128)(2,1)} async-done(((bf16[256,1536]{1,0:T(8,128)(2,1)}), bf16[2048,1536]{1,0:T(8,128)(2,1)}) %all-gather.11.cloned.1.call-update) | async-done | bytes 6291472 | tf_op jit(solution)/shard_map/all_gather | solution.py:376
  78.1 5.6 fusion.125
  96.4 4.3 all-to-all-start
  102.1 4.4 compare_and_fusion.3
  106.5 54.5 %all-to-all-done = bf16[512,3,4,2,64]{0,4,3,1,2:T(8,128)(2,1)} async-done(((bf16[512,3,4,2,64]{0,4,3,1,2:T(8,128)(2,1)}), bf16[512,3,4,2,64]{0,4,3,1,2:T(8,128)(2,1)}, u32[]{:S(2)}, u32[]{:S(2)}) %all-to-all-start) | async-done | bytes 1572896 | tf_op jit(solution)/shard_map/all_to_all | solution.py:262
  172.3 6.1 fusion.20
  178.4 5.2 fusion.21
  185.6 10.7 fusion
  196.3 5.2 fusion.110
  204.3 8.2 fusion.4
  215.4 5.2 fusion.104
  230.2 29.1 %all-to-all-done.2 = bf16[4,2,32768]{2,1,0:T(2,128)(2,1)} async-done(((bf16[4,2,32768]{2,1,0:T(2,128)(2,1)}), bf16[4,2,32768]{2,1,0:T(2,128)(2,1)}, u32[]{:S(2)}, u32[]{:S(2)}) %all-to-all-start.2) | async-done | bytes 524320 | tf_op jit(solution)/shard_map/all_to_all | solution.py:311
  274.9 5.5 collective-permute-done.4
  286.4 4.8 collective-permute-done.5
  304.4 6.5 fusion.79
  315.0 4.5 multiply_convert_fusion.4
  319.5 6.5 fusion.194
  326.0 8.7 multiply_convert_fusion.7
  335.7 4.3 convert_bitcast_fusion.2
  340.1 6.3 convolution_convert_fusion.4
  346.7 6.3 convolution_convert_fusion.3
  353.1 6.5 fusion.77
  359.6 16.2 %all-gather.23.cloned.1.call-done = bf16[2048,1024]{1,0:T(8,128)(2,1)} async-done(((bf16[256,1024]{1,0:T(8,128)(2,1)}), bf16[2048,1024]{1,0:T(8,128)(2,1)}) %all-gather.23.cloned.1.call-update) | async-done | bytes 4194320 | tf_op jit(solution)/shard_map/all_gather | solution.py:390
  375.7 6.5 fusion.196
  382.2 40.8 %all-gather.21.cloned.1.call-done = bf16[2048,1024]{1,0:T(8,128)(2,1)} async-done(((bf16[256,1024]{1,0:T(8,128)(2,1)}), bf16[2048,1024]{1,0:T(8,128)(2,1)}) %all-gather.21.cloned.1.call-update) | async-done | bytes 4194320 | tf_op jit(solution)/shard_map/all_gather | solution.py:390
  423.0 8.7 multiply_convert_fusion.5
  432.7 4.4 convert_bitcast_fusion.1
  437.6 6.2 convolution_convert_fusion.1
  443.9 6.8 convolution_convert_fusion.2
  450.8 5.1 fusion.198
  455.9 4.4 convolution_add_fusion
  460.3 6.9 reduce-scatter.22.cloned.1.call-done
  468.1 5.0 fusion.197
  481.3 10.2 collective-permute-done.20
  513.3 8.3 collective-permute-done.23
  538.9 5.0 convolution_convert_fusion.5
  547.1 4.5 all-to-all-start.3
  556.3 14.8 %all-to-all-done.3 = bf16[512,4,2,64]{0,3,2,1:T(8,128)(2,1)} async-done(((bf16[512,4,2,64]{0,3,2,1:T(8,128)(2,1)}), bf16[512,4,2,64]{0,3,2,1:T(8,128)(2,1)}, u32[]{:S(2)}, u32[]{:S(2)}) %all-to-all-start.3) | async-done | bytes 524320 | tf_op jit(solution)/shard_map/all_to_all | solution.py:319
  575.1 39.3 %reduce-scatter.36.cloned.1.call-done = bf16[256,1024]{1,0:T(8,128)(2,1)} async-done(((bf16[1024,1024]{1,0:T(8,128)(2,1)}), bf16[256,1024]{1,0:T(8,128)(2,1)}) %reduce-scatter.36.cloned.1.call-update) | async-done | bytes 524304 | tf_op jit(solution)/shard_map/reduce_scatter | solution.py:121
  616.6 42.9 %reduce-scatter.34.cloned.1.call-done = bf16[256,1024]{1,0:T(8,128)(2,1)} async-done(((bf16[1024,1024]{1,0:T(8,128)(2,1)}), bf16[256,1024]{1,0:T(8,128)(2,1)}) %reduce-scatter.34.cloned.1.call-update) | async-done | bytes 524304 | tf_op jit(solution)/shard_map/reduce_scatter | solution.py:121
  661.5 9.5 reduce-scatter.32.cloned.1.call-done
  672.4 6.5 multiply_convert_fusion.3
  682.4 6.4 multiply_convert_fusion
  697.0 4.9 multiply_convert_fusion.2
  707.6 10.7 reduce-scatter.44.cloned.1.call-done
  720.4 42.9 %reduce-scatter.42.cloned.1.call-done = bf16[256,1024]{1,0:T(8,128)(2,1)} async-done(((bf16[1024,1024]{1,0:T(8,128)(2,1)}), bf16[256,1024]{1,0:T(8,128)(2,1)}) %reduce-scatter.42.cloned.1.call-update) | async-done | bytes 524304 | tf_op jit(solution)/shard_map/reduce_scatter | solution.py:121
  768.5 5.5 fusion.37
  783.7 24.8 %reduce-scatter.40.cloned.1.call-done = bf16[256,1024]{1,0:T(8,128)(2,1)} async-done(((bf16[1024,1024]{1,0:T(8,128)(2,1)}), bf16[256,1024]{1,0:T(8,128)(2,1)}) %reduce-scatter.40.cloned.1.call-update) | async-done | bytes 524304 | tf_op jit(solution)/shard_map/reduce_scatter | solution.py:121
  810.6 8.4 copy.52
  819.0 5.0 reshape.810
  824.0 4.4 all-to-all-start.4
  829.2 53.0 %all-to-all-done.4 = bf16[4,2,98304]{2,1,0:T(2,128)(2,1)} async-done(((bf16[4,2,98304]{2,1,0:T(2,128)(2,1)}), bf16[4,2,98304]{2,1,0:T(2,128)(2,1)}, u32[]{:S(2)}, u32[]{:S(2)}) %all-to-all-start.4) | async-done | bytes 1572896 | tf_op jit(solution)/shard_map/all_to_all | solution.py:352
  882.1 5.0 reshape.811
  887.1 8.7 copy.57
  898.9 6.6 convolution_convert_fusion
  905.8 5.0 fusion.195
  924.5 9.6 collective-permute-done.28
  935.6 12.8 %collective-permute-done.24 = bf16[128,2048]{1,0:T(8,128)(2,1)S(1)} collective-permute-done((bf16[128,2048]{1,0:T(8,128)(2,1)S(1)}, bf16[128,2048]{1,0:T(8,128)(2,1)S(1)}, u32[]{:S(2)}, u32[]{:S(2)}) %collective-permute-start.24) | collective-permute-done | bytes 524320 | tf_op jit(solution)/shard_map/ppermute | solution.py:99
  952.8 4.6 collective-permute-done.25
  961.1 5.6 collective-permute-done.26
  1004.7 6.8 collective-permute-done.15
  1032.3 47.9 %reduce-scatter.50.cloned.1.call-done = bf16[256,1536]{1,0:T(8,128)(2,1)} async-done(((bf16[1024,1536]{1,0:T(8,128)(2,1)}), bf16[256,1536]{1,0:T(8,128)(2,1)}) %reduce-scatter.50.cloned.1.call-update) | async-done | bytes 786448 | tf_op jit(solution)/shard_map/reduce_scatter | solution.py:121
  (501 shorter events, 283.9 us)
Async XLA Ops:
  7.2 71.0 %all-gather.11.cloned.1.call-start = ((), (), s32[]{:S(2)}) async-start(), calls=%async_computation.22 | async-start | bytes 7077888 | tf_op jit(solution)/shard_map/all_gather | solution.py:376
  9.4 254.8 %all-gather.13.cloned.1.call-start = ((), (), s32[]{:S(2)}) async-start(), calls=%async_computation.23 | async-start | bytes 2359296 | tf_op jit(solution)/shard_map/all_gather | solution.py:377
  10.2 294.3 %all-gather.19.cloned.1.call-start = ((), (), s32[]{:S(2)}) async-start(), calls=%async_computation.26 | async-start | bytes 4718592 | tf_op jit(solution)/shard_map/all_gather | solution.py:390
  12.6 306.9 %all-gather.17.cloned.1.call-start = ((), (), s32[]{:S(2)}) async-start(), calls=%async_computation.25 | async-start | bytes 4718592 | tf_op jit(solution)/shard_map/all_gather | solution.py:390
  13.8 312.2 %all-gather.15.cloned.1.call-start = ((), (), s32[]{:S(2)}) async-start(), calls=%async_computation.24 | async-start | bytes 4718592 | tf_op jit(solution)/shard_map/all_gather | solution.py:390
  16.1 337.0 %all-gather.25.cloned.1.call-start = ((), (), s32[]{:S(2)}) async-start(), calls=%async_computation.29 | async-start | bytes 4718592 | tf_op jit(solution)/shard_map/all_gather | solution.py:390
  17.3 79.0 %all-to-all-start.1 = ((s32[4,2,512]{2,1,0:T(2,128)}), s32[4,2,512]{2,1,0:T(2,128)S(1)}, u32[]{:S(2)}, u32[]{:S(2)}) async-start(s32[4,2,512]{2,1,0:T(2,128)} %broadcast_in_dim.158), calls=%async_computation.1 | async-start | bytes 32768 | tf_op jit(solution)/shard_map/all_to_all | solution.py:269
  96.4 64.7 %all-to-all-start = ((bf16[512,3,4,2,64]{0,4,3,1,2:T(8,128)(2,1)}), bf16[512,3,4,2,64]{0,4,3,1,2:T(8,128)(2,1)}, u32[]{:S(2)}, u32[]{:S(2)}) async-start(bf16[512,3,4,2,64]{0,4,3,1,2:T(8,128)(2,1)} %copy.46), calls=%async_computation | async-start | bytes 3145728 | tf_op jit(solution)/shard_map/all_to_all | solution.py:262
  100.7 275.0 %all-gather.23.cloned.1.call-start = ((), (), s32[]{:S(2)}) async-start(), calls=%async_computation.28 | async-start | bytes 4718592 | tf_op jit(solution)/shard_map/all_gather | solution.py:390
  226.0 33.3 %all-to-all-start.2 = ((bf16[4,2,32768]{2,1,0:T(2,128)(2,1)}), bf16[4,2,32768]{2,1,0:T(2,128)(2,1)}, u32[]{:S(2)}, u32[]{:S(2)}) async-start(bf16[4,2,32768]{2,1,0:T(2,128)(2,1)} %reshape.808), calls=%async_computation.2 | async-start | bytes 1048576 | tf_op jit(solution)/shard_map/all_to_all | solution.py:311
  230.2 192.9 %all-gather.21.cloned.1.call-start = ((), (), s32[]{:S(2)}) async-start(), calls=%async_computation.27 | async-start | bytes 4718592 | tf_op jit(solution)/shard_map/all_gather | solution.py:390
  270.3 10.1 collective-permute-start.4
  271.8 188.5 %reduce-scatter.24.cloned.1.call-start = ((), (), s32[]{:S(2)}) async-start(), calls=%async_computation.32 | async-start | bytes 6291456 | tf_op jit(solution)/shard_map/reduce_scatter | solution.py:117
  273.4 12.1 %collective-permute-start = (bf16[128,2048]{1,0:T(8,128)(2,1)S(1)}, bf16[128,2048]{1,0:T(8,128)(2,1)S(1)}, u32[]{:S(2)}, u32[]{:S(2)}) collective-permute-start(bf16[128,2048]{1,0:T(8,128)(2,1)S(1)} %dynamic-slice_convert_fusion.7), channel_id=1, source_target_pairs={{0,1},{1,0},{2,3},{3,2},{4,5},{5,4},{6,7},{7,6},{8,9},{9,8},{10,11... | collective-permute-start | bytes 1572872 | tf_op jit(solution)/shard_map/ppermute | solution.py:99
  282.0 9.2 collective-permute-start.5
  285.6 7.1 collective-permute-start.1
  291.3 6.8 collective-permute-start.6
  292.8 9.2 collective-permute-start.2
  298.9 12.1 %collective-permute-start.7 = (bf16[128,2048]{1,0:T(8,128)(2,1)}, bf16[128,2048]{1,0:T(8,128)(2,1)}, u32[]{:S(2)}, u32[]{:S(2)}) collective-permute-start(bf16[128,2048]{1,0:T(8,128)(2,1)} %pad_maximum_fusion.13), channel_id=1, source_target_pairs={{0,2},{1,3},{2,0},{3,1},{4,6},{5,7},{6,4},{7,5},{8,10},{9,11},{10,... | collective-permute-start | bytes 1572872 | tf_op jit(solution)/shard_map/ppermute | solution.py:112
  303.0 9.5 collective-permute-start.3
  340.1 120.2 %reduce-scatter.20.cloned.1.call-start = ((), (), s32[]{:S(2)}) async-start(), calls=%async_computation.30 | async-start | bytes 6291456 | tf_op jit(solution)/shard_map/reduce_scatter | solution.py:117
  346.4 120.8 %reduce-scatter.22.cloned.1.call-start = ((), (), s32[]{:S(2)}) async-start(), calls=%async_computation.31 | async-start | bytes 6291456 | tf_op jit(solution)/shard_map/reduce_scatter | solution.py:117
  353.0 172.3 %reduce-scatter.30.cloned.1.call-start = ((), (), s32[]{:S(2)}) async-start(), calls=%async_computation.35 | async-start | bytes 6291456 | tf_op jit(solution)/shard_map/reduce_scatter | solution.py:117
  437.2 88.2 %reduce-scatter.28.cloned.1.call-start = ((), (), s32[]{:S(2)}) async-start(), calls=%async_computation.34 | async-start | bytes 6291456 | tf_op jit(solution)/shard_map/reduce_scatter | solution.py:117
  443.9 81.5 %reduce-scatter.26.cloned.1.call-start = ((), (), s32[]{:S(2)}) async-start(), calls=%async_computation.33 | async-start | bytes 6291456 | tf_op jit(solution)/shard_map/reduce_scatter | solution.py:117
  450.7 122.3 %reduce-scatter.38.cloned.1.call-start = ((), (), s32[]{:S(2)}) async-start(), calls=%async_computation.39 | async-start | bytes 2621440 | tf_op jit(solution)/shard_map/reduce_scatter | solution.py:121
  467.2 147.2 %reduce-scatter.36.cloned.1.call-start = ((), (), s32[]{:S(2)}) async-start(), calls=%async_computation.38 | async-start | bytes 2621440 | tf_op jit(solution)/shard_map/reduce_scatter | solution.py:121
  467.8 191.6 %reduce-scatter.34.cloned.1.call-start = ((), (), s32[]{:S(2)}) async-start(), calls=%async_computation.37 | async-start | bytes 2621440 | tf_op jit(solution)/shard_map/reduce_scatter | solution.py:121
  477.0 14.5 %collective-permute-start.20 = (bf16[128,2048]{1,0:T(8,128)(2,1)}, bf16[128,2048]{1,0:T(8,128)(2,1)}, u32[]{:S(2)}, u32[]{:S(2)}) collective-permute-start(bf16[128,2048]{1,0:T(8,128)(2,1)} %dynamic-slice_convert_fusion.2), channel_id=1, source_target_pairs={{0,2},{1,3},{2,0},{3,1},{4,6},{5,7},{6,4},{7,5},{8,10},{9,11},{10,... | collective-permute-start | bytes 1572872 | tf_op jit(solution)/shard_map/ppermute | solution.py:99
  479.7 15.5 %collective-permute-start.16 = (bf16[128,2048]{1,0:T(8,128)(2,1)}, bf16[128,2048]{1,0:T(8,128)(2,1)}, u32[]{:S(2)}, u32[]{:S(2)}) collective-permute-start(bf16[128,2048]{1,0:T(8,128)(2,1)} %dynamic-slice_convert_fusion.3), channel_id=1, source_target_pairs={{0,1},{1,0},{2,3},{3,2},{4,5},{5,4},{6,7},{7,6},{8,9},{9,8},{10,11... | collective-permute-start | bytes 1572872 | tf_op jit(solution)/shard_map/ppermute | solution.py:99
  481.2 189.9 %reduce-scatter.32.cloned.1.call-start = ((), (), s32[]{:S(2)}) async-start(), calls=%async_computation.36 | async-start | bytes 3145728 | tf_op jit(solution)/shard_map/reduce_scatter | solution.py:117
  493.4 7.4 collective-permute-start.21
  497.1 6.8 collective-permute-start.17
  500.8 6.5 collective-permute-start.22
  503.9 9.2 collective-permute-start.18
  507.5 14.1 %collective-permute-start.23 = (bf16[128,2048]{1,0:T(8,128)(2,1)S(1)}, bf16[128,2048]{1,0:T(8,128)(2,1)S(1)}, u32[]{:S(2)}, u32[]{:S(2)}) collective-permute-start(bf16[128,2048]{1,0:T(8,128)(2,1)S(1)} %pad_maximum_fusion.17), channel_id=1, source_target_pairs={{0,2},{1,3},{2,0},{3,1},{4,6},{5,7},{6,4},{7,5},{8,10},{9,11},{10,... | collective-permute-start | bytes 1572872 | tf_op jit(solution)/shard_map/ppermute | solution.py:112
  513.2 9.2 collective-permute-start.19
  543.9 174.4 %reduce-scatter.44.cloned.1.call-start = ((), (), s32[]{:S(2)}) async-start(), calls=%async_computation.42 | async-start | bytes 2621440 | tf_op jit(solution)/shard_map/reduce_scatter | solution.py:121
  544.7 218.6 %reduce-scatter.42.cloned.1.call-start = ((), (), s32[]{:S(2)}) async-start(), calls=%async_computation.41 | async-start | bytes 2621440 | tf_op jit(solution)/shard_map/reduce_scatter | solution.py:121
  547.1 24.0 %all-to-all-start.3 = ((bf16[512,4,2,64]{0,3,2,1:T(8,128)(2,1)}), bf16[512,4,2,64]{0,3,2,1:T(8,128)(2,1)}, u32[]{:S(2)}, u32[]{:S(2)}) async-start(bf16[512,4,2,64]{0,3,2,1:T(8,128)(2,1)} %bitcast.346), calls=%async_computation.9 | async-start | bytes 1048576 | tf_op jit(solution)/shard_map/all_to_all | solution.py:319
  551.6 119.5 %copy-start.58 = (bf16[512,2,64]{0,2,1:T(8,128)(2,1)S(1)}, bf16[512,2,64]{0,2,1:T(8,128)(2,1)}, u32[]{:S(2)}) copy-start(bf16[512,2,64]{0,2,1:T(8,128)(2,1)} %copy-done.57) | copy-start | bytes 393220
  551.6 119.5 %copy-start.60 = (bf16[512,2,64]{0,2,1:T(8,128)(2,1)S(1)}, bf16[512,2,64]{0,2,1:T(8,128)(2,1)}, u32[]{:S(2)}) copy-start(bf16[512,2,64]{0,2,1:T(8,128)(2,1)} %copy-done.59) | copy-start | bytes 393220
  551.6 256.9 %reduce-scatter.40.cloned.1.call-start = ((), (), s32[]{:S(2)}) async-start(), calls=%async_computation.40 | async-start | bytes 2621440 | tf_op jit(solution)/shard_map/reduce_scatter | solution.py:121
  824.0 58.1 %all-to-all-start.4 = ((bf16[4,2,98304]{2,1,0:T(2,128)(2,1)}), bf16[4,2,98304]{2,1,0:T(2,128)(2,1)}, u32[]{:S(2)}, u32[]{:S(2)}) async-start(bf16[4,2,98304]{2,1,0:T(2,128)(2,1)} %reshape.810), calls=%async_computation.17 | async-start | bytes 3145728 | tf_op jit(solution)/shard_map/all_to_all | solution.py:352
  828.4 142.1 %reduce-scatter.46.cloned.1.call-start = ((), (), s32[]{:S(2)}) async-start(), calls=%async_computation.43 | async-start | bytes 1310720 | tf_op jit(solution)/shard_map/reduce_scatter | solution.py:121
  829.1 157.7 %reduce-scatter.48.cloned.1.call-start = ((), (), s32[]{:S(2)}) async-start(), calls=%async_computation.44 | async-start | bytes 9437184 | tf_op jit(solution)/shard_map/reduce_scatter | solution.py:117
  905.5 124.4 %reduce-scatter.52.cloned.1.call-start = ((), (), s32[]{:S(2)}) async-start(), calls=%async_computation.46 | async-start | bytes 1179648
  919.2 14.9 %collective-permute-start.28 = (bf16[128,2048]{1,0:T(8,128)(2,1)S(1)}, bf16[128,2048]{1,0:T(8,128)(2,1)S(1)}, u32[]{:S(2)}, u32[]{:S(2)}) collective-permute-start(bf16[128,2048]{1,0:T(8,128)(2,1)S(1)} %dynamic-slice_convert_fusion), channel_id=1, source_target_pairs={{0,2},{1,3},{2,0},{3,1},{4,6},{5,7},{6,4},{7,5},{8,10},{9,11},{10,... | collective-permute-start | bytes 1572872 | tf_op jit(solution)/shard_map/ppermute | solution.py:99
  920.7 48.8 %collective-permute-start.12 = (bf16[128,2048]{1,0:T(8,128)(2,1)S(1)}, bf16[128,2048]{1,0:T(8,128)(2,1)S(1)}, u32[]{:S(2)}, u32[]{:S(2)}) collective-permute-start(bf16[128,2048]{1,0:T(8,128)(2,1)S(1)} %dynamic-slice_convert_fusion.4), channel_id=1, source_target_pairs={{0,2},{1,3},{2,0},{3,1},{4,6},{5,7},{6,4},{7,5},{8,10},{9,11},{10,... | collective-permute-start | bytes 1572872 | tf_op jit(solution)/shard_map/ppermute | solution.py:99
  922.3 64.6 %collective-permute-start.8 = (bf16[128,2048]{1,0:T(8,128)(2,1)}, bf16[128,2048]{1,0:T(8,128)(2,1)}, u32[]{:S(2)}, u32[]{:S(2)}) collective-permute-start(bf16[128,2048]{1,0:T(8,128)(2,1)} %dynamic-slice_convert_fusion.5), channel_id=1, source_target_pairs={{0,1},{1,0},{2,3},{3,2},{4,5},{5,4},{6,7},{7,6},{8,9},{9,8},{10,11... | collective-permute-start | bytes 1572872 | tf_op jit(solution)/shard_map/ppermute | solution.py:99
  923.7 24.7 %collective-permute-start.24 = (bf16[128,2048]{1,0:T(8,128)(2,1)S(1)}, bf16[128,2048]{1,0:T(8,128)(2,1)S(1)}, u32[]{:S(2)}, u32[]{:S(2)}) collective-permute-start(bf16[128,2048]{1,0:T(8,128)(2,1)S(1)} %dynamic-slice_convert_fusion.1), channel_id=1, source_target_pairs={{0,1},{1,0},{2,3},{3,2},{4,5},{5,4},{6,7},{7,6},{8,9},{9,8},{10,11... | collective-permute-start | bytes 1572872 | tf_op jit(solution)/shard_map/ppermute | solution.py:99
  934.2 17.1 %collective-permute-start.29 = (bf16[64,2048]{1,0:T(8,128)(2,1)S(1)}, bf16[64,2048]{1,0:T(8,128)(2,1)S(1)}, u32[]{:S(2)}, u32[]{:S(2)}) collective-permute-start(bf16[64,2048]{1,0:T(8,128)(2,1)S(1)} %dynamic-slice_convert_fusion.8), channel_id=1, source_target_pairs={{0,1},{1,0},{2,3},{3,2},{4,5},{5,4},{6,7},{7,6},{8,9},{9,8},{10,11... | collective-permute-start | bytes 786440 | tf_op jit(solution)/shard_map/ppermute | solution.py:99
  948.5 8.9 collective-permute-start.25
  951.4 7.6 collective-permute-start.30
  957.5 9.2 collective-permute-start.26
  960.6 12.1 %collective-permute-start.31 = (bf16[128,2048]{1,0:T(8,128)(2,1)}, bf16[128,2048]{1,0:T(8,128)(2,1)}, u32[]{:S(2)}, u32[]{:S(2)}) collective-permute-start(bf16[128,2048]{1,0:T(8,128)(2,1)} %pad_maximum_fusion.19), channel_id=1, source_target_pairs={{0,2},{1,3},{2,0},{3,1},{4,6},{5,7},{6,4},{7,5},{8,10},{9,11},{10,... | collective-permute-start | bytes 1572872 | tf_op jit(solution)/shard_map/ppermute | solution.py:112
  968.3 9.5 collective-permute-start.27
  984.3 96.0 %reduce-scatter.50.cloned.1.call-start = ((), (), s32[]{:S(2)}) async-start(), calls=%async_computation.45 | async-start | bytes 3932160 | tf_op jit(solution)/shard_map/reduce_scatter | solution.py:121
  985.7 6.5 collective-permute-start.13
  988.5 9.2 collective-permute-start.9
  993.4 8.8 collective-permute-start.14
  997.8 6.4 collective-permute-start.10
  1002.2 9.2 collective-permute-start.15
  1004.3 9.2 collective-permute-start.11
  (106 other events, 1054.5 us)
Sparse Core Ops, SparseCore 0:
  10.2 67.9 all-gather.10
  79.7 37.3 all-gather.12
  119.3 56.3 all-gather.18
  177.7 45.7 all-gather.16
  225.0 55.4 all-gather.14
  282.6 45.8 all-gather.24
  330.0 45.6 all-gather.22
  377.3 45.6 all-gather.20
  425.3 10.6 reduce-scatter.23
  438.2 13.3 reduce-scatter.19
  453.9 13.3 reduce-scatter.21
  469.4 13.1 reduce-scatter.29
  484.9 13.2 reduce-scatter.27
  500.3 13.3 reduce-scatter.25
  515.8 50.2 reduce-scatter.37
  568.3 46.1 reduce-scatter.35
  616.6 42.8 reduce-scatter.33
  662.1 8.9 reduce-scatter.31
  673.4 44.9 reduce-scatter.43
  720.5 42.8 reduce-scatter.41
  765.6 42.8 reduce-scatter.39
  831.5 47.6 reduce-scatter.45
  905.6 13.0 reduce-scatter.47
  984.4 33.8 reduce-scatter.51
  1020.6 59.5 reduce-scatter.49

commit v3 on v2

--- a/solution.py
+++ b/solution.py
@@ -114,11 +114,41 @@
 
 
 def chip_total(grad):
-    return lax.psum_scatter(grad.astype(jnp.bfloat16), "shard", scatter_dimension=0, tiled=True)
+    f32 = jnp.float32
+    shard = lax.axis_index("shard")
+    mine = half_of(grad, shard)
+    other = half_of(grad, 1 - shard)
+    got = lax.ppermute(other.astype(jnp.bfloat16), "shard", [(0, 1), (1, 0)])
+    return mine.astype(f32) + got.astype(f32)
 
 
 def line_total(staged):
-    return lax.psum_scatter(staged, "context", scatter_dimension=0, tiled=True).astype(jnp.float32)
+    return lax.psum_scatter(
+        staged.astype(jnp.bfloat16), "context", scatter_dimension=0, tiled=True
+    ).astype(jnp.float32)
+
+
+def line_pipeline(staged):
+    f32 = jnp.float32
+    bf16 = jnp.bfloat16
+    ways = lax.axis_size("context")
+    me = lax.axis_index("context")
+    size = staged.shape[0] // ways
+
+    def block(index):
+        index = jnp.clip(index, 0, ways - 1)
+        return lax.dynamic_slice_in_dim(staged, index * size, size, axis=0)
+
+    rightward = jnp.zeros((size,) + staged.shape[1:], f32)
+    leftward = jnp.zeros((size,) + staged.shape[1:], f32)
+    for step in range(1, ways):
+        right_pairs = [(d, d + 1) for d in range(step)]
+        left_pairs = [(d, d - 1) for d in range(ways - step, ways)]
+        sent_right = block(ways - step + me) + rightward
+        sent_left = block(me + step - ways) + leftward
+        rightward = lax.ppermute(sent_right.astype(bf16), "context", right_pairs).astype(f32)
+        leftward = lax.ppermute(sent_left.astype(bf16), "context", left_pairs).astype(f32)
+    return block(me) + rightward + leftward
 
 
 def rows_total(grad):
@@ -446,7 +476,17 @@
         staged.append(tuple(chip_total(value) for value in pending))
     grad_h2 = tensor_total(h2_grad_partial)
     grad_h2, staged[-1] = lax.optimization_barrier((grad_h2, staged[-1]))
-    reduced = [tuple(line_total(value) for value in chunk) for chunk in staged]
+    reduced = []
+    for index, chunk in enumerate(staged):
+        if index == 0 and len(staged) > 1:
+            widths = [value.shape[1] for value in chunk]
+            joined_sum = line_pipeline(jnp.concatenate(chunk, axis=1))
+            edges = [sum(widths[:i]) for i in range(len(widths) + 1)]
+            reduced.append(
+                tuple(joined_sum[:, edges[i] : edges[i + 1]] for i in range(len(widths)))
+            )
+        else:
+            reduced.append(tuple(line_total(value) for value in chunk))
     result = (resid2 + tensor_total(mlp_partial)).astype(bf16)
     grad_gmlp = jnp.sum(grad_h2 * norm2, axis=0)
     grad_resid = grad_y.astype(f32) + norm_back(grad_h2, norm2, inv2, gain_mlp)
@@ -472,10 +512,11 @@
     grad_h1, reduced_o = lax.optimization_barrier((grad_h1, reduced_o))
     grad_gattn = jnp.sum(grad_h1 * norm1, axis=0)
     grad_x_part = (grad_resid + norm_back(grad_h1, norm1, inv1, gain_attn)).astype(bf16)
-    reduced_qkv = rows_total(contract_first(h1, grad_qkv))
-    reduced_gains = lax.psum_scatter(
-        jnp.stack([grad_gattn, grad_gmlp], axis=1), ROWS, scatter_dimension=0, tiled=True
-    )
+    gain_slab = jnp.pad(jnp.stack([grad_gattn, grad_gmlp], axis=1), ((0, 0), (0, 126)))
+    reduced_qkv = rows_total(
+        jnp.concatenate([contract_first(h1, grad_qkv), gain_slab], axis=1)
+    )
+    reduced_gains = reduced_qkv[:, 3 * cols :]
     reduced_gate, reduced_up, reduced_down = (
         jnp.concatenate([chunk[which] for chunk in reduced], axis=1) for which in range(3)
     )
@@ -484,7 +525,7 @@
         grad_x_part.reshape(1, rows, width),
         reduced_qkv[:, :cols],
         reduced_qkv[:, cols : 2 * cols],
-        reduced_qkv[:, 2 * cols :],
+        reduced_qkv[:, 2 * cols : 3 * cols],
         reduced_o,
         reduced_gate,
         reduced_up,

time: 1100 us -> 1140 us (1.036)
  waiting for transfers between devices: 568 us -> 486 us
  starting transfers between devices: 69.4 us -> 139 us
  other arithmetic: 107 us -> 151 us
  local copies, waits for them, and re-layouts: 95.9 us -> 131 us
  matrix products: 209 us -> 187 us
    reduce_scatter x16 -> x5, waiting for transfers between devices: 225 us -> 13.8 us  [line_total(): lax.psum_scatter(staged.astype(jnp.bfloat16), 'context', scatter_dimensio...]
    ppermute x0 -> x14, waiting for transfers between devices: none -> 110 us  [the longest x3 110 us: line_pipeline(): lax.ppermute(sent_right.astype(bf16), 'context', right_pairs).astype(f32)]
    all_to_all x1, starting transfers between devices: 4.48 us -> 59.8 us  [backward(): grad = lax.all_to_all(grad, 'context', 1, 0, tiled=True)]
    add x0 -> x9, other arithmetic: none -> 39.6 us  [the longest x7 29.9 us: chip_total(): return mine.astype(f32) + got.astype(f32)]
    all_to_all x1, waiting for transfers between devices: 14.8 us -> 40.1 us  [backward(): grad = lax.all_to_all(grad, 'context', 1, 0, tiled=True)]
    dot_general x8, matrix products: 43.5 us -> 21.9 us  [contract_first(): lax.dot_general(left, right, (((0,), (0,)), ((), ())), preferred_element_...]
    ppermute x0 -> x14, starting transfers between devices: none -> 21 us  [the longest x3 15.4 us: line_pipeline(): lax.ppermute(sent_right.astype(bf16), 'context', right_pairs).astype(f32)]
    unnamed x228 -> x275, local copies, waits for them, and re-layouts: 34.1 us -> 52.7 us
  transfers between devices with their start and end apart: 62 -> 64, of which waited for: 42 -> 37; matrix products, arithmetic and copies ran while one was open for 35% -> 31% of each run, Pallas kernels for 0% -> 0%
where the time goes in v3:
time: 1140 us; the launch traced here: 1130 us
  waiting for transfers between devices  486 us (43%)
  matrix products  187 us (16%)
  other arithmetic  151 us (13%)
  starting transfers between devices  139 us (12%)
  local copies, waits for them, and re-layouts  131 us (11%)
  blocking collectives  24.1 us (2%)
  between operations  16.5 us (1%)
    ppermute x3, waiting for transfers between devices, line_pipeline(): lax.ppermute(sent_right.astype(bf16), 'context', right_pairs).astype(f32)  110 us
    all_gather x6, waiting for transfers between devices, on_device(): lax.all_gather(weight[:, part], ROWS, axis=0, tiled=True)  75 us
    all_to_all x1, starting transfers between devices, backward(): grad = lax.all_to_all(grad, 'context', 1, 0, tiled=True)  59.8 us
    all_to_all x1, waiting for transfers between devices, __init__(): stacked = lax.all_to_all(stacked, 'context', 2, 0, tiled=True)  54.2 us
    all_to_all x1, waiting for transfers between devices, backward(): stacked = lax.all_to_all(stacked, 'context', 0, 2, tiled=True)  52.7 us
    unnamed x275, local copies, waits for them, and re-layouts  52.7 us
    ppermute x16, waiting for transfers between devices, swap(): return lax.ppermute(value.astype(bf16), 'tensor', pairs).astype(f32)  43.7 us
    dot_general x8, matrix products, contract_last(): lax.dot_general(left, right, (((1,), (1,)), ((), ())), preferred_element_...  43.4 us
  transfers between devices with their start and end apart: 64, of which 37 were waited for; matrix products, arithmetic and copies ran while one was open for 31% of the time, Pallas kernels for 0%

profile of v3, /device:TPU:0, one launch (start us, length us, event | category | flops | bytes accessed | tf_op | source)
XLA Modules:
  0.0 1133.7 jit_solution(4613472825467513167)
XLA Ops:
  17.3 6.3 all-to-all-start.1
  23.7 24.1 %all-gather.1 = bf16[8,1,512]{2,1,0:T(2,128)(2,1)S(1)} all-gather(bf16[1,1,512]{2,1,0:T(2,128)(2,1)S(1)} %reshape.803), channel_id=2, replica_groups=mesh['shard'=2,'context'=4,'tensor'=4] {'shard','context'}, dimensions={0}, use_global_device_ids=true | all-gather | bytes 9216 | tf_op jit(solution)/shard_map/all_gather | solution.py:408
  48.7 29.5 %all-gather.11.cloned.1.call-done = bf16[2048,1536]{1,0:T(8,128)(2,1)} async-done(((bf16[256,1536]{1,0:T(8,128)(2,1)}), bf16[2048,1536]{1,0:T(8,128)(2,1)}) %all-gather.11.cloned.1.call-update) | async-done | bytes 6291472 | tf_op jit(solution)/shard_map/all_gather | solution.py:406
  78.1 5.6 fusion.135
  96.3 4.3 all-to-all-start
  102.1 4.6 compare_and_fusion.3
  106.7 54.2 %all-to-all-done = bf16[512,3,4,2,64]{0,4,3,1,2:T(8,128)(2,1)} async-done(((bf16[512,3,4,2,64]{0,4,3,1,2:T(8,128)(2,1)}), bf16[512,3,4,2,64]{0,4,3,1,2:T(8,128)(2,1)}, u32[]{:S(2)}, u32[]{:S(2)}) %all-to-all-start) | async-done | bytes 1572896 | tf_op jit(solution)/shard_map/all_to_all | solution.py:292
  172.2 5.6 fusion.25
  181.8 11.7 %fusion = (f32[2,512]{1,0:T(2,128)S(1)}, f32[2,512]{1,0:T(2,128)S(1)}) fusion(f32[2,512,2048]{2,1,0:T(8,128)S(1)} %get-tuple-element.213, f32[2,512]{1,0:T(2,128)S(1)} %get-tuple-element.212, pred[512,2048]{1,0:T(8,128)(4,1)} %get-tuple-element.186, f32[2,512]{1,0:T(2,128)S(1)} %get-tuple-element.210, f32[2,512,2048]{2,1,0:T(8,128)} %get-tuple-element.211, ...), kind=kLoop, calls=%fused_computation.20 | loop fusion | flops 20969472 | bytes 18890752 | tf_op jit(solution)/shard_map/reduce_sum | solution.py:329
  193.6 6.0 fusion.119
  203.0 7.1 fusion.4
  221.2 4.1 all-to-all-start.2
  226.2 22.7 %all-to-all-done.2 = bf16[4,2,32768]{2,1,0:T(2,128)(2,1)} async-done(((bf16[4,2,32768]{2,1,0:T(2,128)(2,1)}), bf16[4,2,32768]{2,1,0:T(2,128)(2,1)}, u32[]{:S(2)}, u32[]{:S(2)}) %all-to-all-start.2) | async-done | bytes 524320 | tf_op jit(solution)/shard_map/all_to_all | solution.py:341
  262.0 6.7 fusion.88
  271.4 9.4 collective-permute-done
  288.1 5.5 collective-permute-done.6
  298.9 6.6 fusion.86
  309.2 4.6 multiply_convert_fusion.4
  313.9 6.5 fusion.207
  322.9 8.7 multiply_convert_fusion.5
  339.1 31.6 %all-gather.17.cloned.1.call-done = bf16[2048,1024]{1,0:T(8,128)(2,1)} async-done(((bf16[256,1024]{1,0:T(8,128)(2,1)}), bf16[2048,1024]{1,0:T(8,128)(2,1)}) %all-gather.17.cloned.1.call-update) | async-done | bytes 4194320 | tf_op jit(solution)/shard_map/all_gather | solution.py:420
  370.7 6.5 fusion.205
  377.2 40.8 %all-gather.15.cloned.1.call-done = bf16[2048,1024]{1,0:T(8,128)(2,1)} async-done(((bf16[256,1024]{1,0:T(8,128)(2,1)}), bf16[2048,1024]{1,0:T(8,128)(2,1)}) %all-gather.15.cloned.1.call-update) | async-done | bytes 4194320 | tf_op jit(solution)/shard_map/all_gather | solution.py:420
  418.0 7.4 multiply_convert_fusion.7
  447.7 7.0 fusion.209
  454.7 4.8 fusion.210
  468.0 6.8 fusion.208
  474.8 7.8 convolution_add_fusion
  482.9 4.2 bitcast_add_fusion.1
  487.1 4.2 convert_add_fusion.4
  491.4 4.5 convert_add_fusion.3
  495.8 6.1 add_add_fusion
  507.2 3.9 bitcast_add_fusion
  511.2 4.9 convert_add_fusion.1
  540.0 4.9 convert_add_fusion.2
  560.7 4.5 copy-done.4
  572.8 52.6 %collective-permute-done.31 = bf16[256,3072]{1,0:T(8,128)(2,1)} collective-permute-done((bf16[256,3072]{1,0:T(8,128)(2,1)}, bf16[256,3072]{1,0:T(8,128)(2,1)}, u32[]{:S(2)}, u32[]{:S(2)}) %collective-permute-start.31) | collective-permute-done | bytes 1572896 | tf_op jit(solution)/shard_map/ppermute | solution.py:149
  625.5 3.9 add_convert_fusion.3
  629.4 5.6 collective-permute-start.32
  638.3 57.6 %collective-permute-done.32 = bf16[256,3072]{1,0:T(8,128)(2,1)} collective-permute-done((bf16[256,3072]{1,0:T(8,128)(2,1)}, bf16[256,3072]{1,0:T(8,128)(2,1)}, u32[]{:S(2)}, u32[]{:S(2)}) %collective-permute-start.32) | collective-permute-done | bytes 1572896 | tf_op jit(solution)/shard_map/ppermute | solution.py:149
  695.9 5.8 add_convert_fusion.2
  702.7 4.3 multiply_add_fusion
  713.5 6.1 collective-permute-start.33
  726.3 59.8 %all-to-all-start.3 = ((bf16[512,4,2,64]{0,3,2,1:T(8,128)(2,1)}), bf16[512,4,2,64]{0,3,2,1:T(8,128)(2,1)}, u32[]{:S(2)}, u32[]{:S(2)}) async-start(bf16[512,4,2,64]{0,3,2,1:T(8,128)(2,1)} %bitcast.349), calls=%async_computation.3 | async-start | bytes 1048576 | tf_op jit(solution)/shard_map/all_to_all | solution.py:349
  786.3 40.1 %all-to-all-done.3 = bf16[512,4,2,64]{0,3,2,1:T(8,128)(2,1)} async-done(((bf16[512,4,2,64]{0,3,2,1:T(8,128)(2,1)}), bf16[512,4,2,64]{0,3,2,1:T(8,128)(2,1)}, u32[]{:S(2)}, u32[]{:S(2)}) %all-to-all-start.3) | async-done | bytes 524320 | tf_op jit(solution)/shard_map/all_to_all | solution.py:349
  844.4 6.4 multiply_convert_fusion.3
  856.2 6.6 multiply_convert_fusion.2
  868.5 6.2 multiply_convert_fusion.1
  877.5 4.1 multiply_convert_fusion
  890.1 8.5 copy.74
  898.5 5.0 reshape.808
  903.6 4.3 all-to-all-start.4
  908.5 52.7 %all-to-all-done.4 = bf16[4,2,98304]{2,1,0:T(2,128)(2,1)} async-done(((bf16[4,2,98304]{2,1,0:T(2,128)(2,1)}), bf16[4,2,98304]{2,1,0:T(2,128)(2,1)}, u32[]{:S(2)}, u32[]{:S(2)}) %all-to-all-start.4) | async-done | bytes 1572896 | tf_op jit(solution)/shard_map/all_to_all | solution.py:382
  961.2 5.0 reshape.809
  966.2 8.7 copy.83
  976.8 6.4 fusion.133
  993.3 7.1 collective-permute-done.41
  1012.9 4.1 collective-permute-done.43
  1040.3 5.0 fusion.206
  1052.5 7.1 fusion.16
  1059.6 3.8 collective-permute-done.12
  1069.2 3.9 collective-permute-done.13
  1084.7 9.6 collective-permute-done.15
  1107.5 13.8 %reduce-scatter.14.cloned.1.call-done = bf16[256,1664]{0,1:T(8,128)(2,1)} async-done(((bf16[1024,1664]{0,1:T(8,128)(2,1)}), bf16[256,1664]{0,1:T(8,128)(2,1)}) %reduce-scatter.14.cloned.1.call-update) | async-done | bytes 851984 | tf_op jit(solution)/shard_map/reduce_scatter | solution.py:126
  (560 shorter events, 328.6 us)
Async XLA Ops:
  7.2 71.0 %all-gather.11.cloned.1.call-start = ((), (), s32[]{:S(2)}) async-start(), calls=%async_computation.10 | async-start | bytes 7077888 | tf_op jit(solution)/shard_map/all_gather | solution.py:406
  9.4 244.8 %all-gather.13.cloned.1.call-start = ((), (), s32[]{:S(2)}) async-start(), calls=%async_computation.11 | async-start | bytes 2359296 | tf_op jit(solution)/shard_map/all_gather | solution.py:407
  10.2 251.8 %all-gather.19.cloned.1.call-start = ((), (), s32[]{:S(2)}) async-start(), calls=%async_computation.14 | async-start | bytes 4718592 | tf_op jit(solution)/shard_map/all_gather | solution.py:420
  12.6 286.3 %all-gather.25.cloned.1.call-start = ((), (), s32[]{:S(2)}) async-start(), calls=%async_computation.17 | async-start | bytes 4718592 | tf_op jit(solution)/shard_map/all_gather | solution.py:420
  13.2 300.6 %all-gather.23.cloned.1.call-start = ((), (), s32[]{:S(2)}) async-start(), calls=%async_computation.16 | async-start | bytes 4718592 | tf_op jit(solution)/shard_map/all_gather | solution.py:420
  14.3 308.5 %all-gather.21.cloned.1.call-start = ((), (), s32[]{:S(2)}) async-start(), calls=%async_computation.15 | async-start | bytes 4718592 | tf_op jit(solution)/shard_map/all_gather | solution.py:420
  17.3 79.0 %all-to-all-start.1 = ((s32[4,2,512]{2,1,0:T(2,128)}), s32[4,2,512]{2,1,0:T(2,128)S(1)}, u32[]{:S(2)}, u32[]{:S(2)}) async-start(s32[4,2,512]{2,1,0:T(2,128)} %broadcast_in_dim.158), calls=%async_computation.1 | async-start | bytes 32768 | tf_op jit(solution)/shard_map/all_to_all | solution.py:299
  96.3 64.6 %all-to-all-start = ((bf16[512,3,4,2,64]{0,4,3,1,2:T(8,128)(2,1)}), bf16[512,3,4,2,64]{0,4,3,1,2:T(8,128)(2,1)}, u32[]{:S(2)}, u32[]{:S(2)}) async-start(bf16[512,3,4,2,64]{0,4,3,1,2:T(8,128)(2,1)} %copy.64), calls=%async_computation | async-start | bytes 3145728 | tf_op jit(solution)/shard_map/all_to_all | solution.py:292
  100.7 270.0 %all-gather.17.cloned.1.call-start = ((), (), s32[]{:S(2)}) async-start(), calls=%async_computation.13 | async-start | bytes 4718592 | tf_op jit(solution)/shard_map/all_gather | solution.py:420
  221.2 27.8 %all-to-all-start.2 = ((bf16[4,2,32768]{2,1,0:T(2,128)(2,1)}), bf16[4,2,32768]{2,1,0:T(2,128)(2,1)}, u32[]{:S(2)}, u32[]{:S(2)}) async-start(bf16[4,2,32768]{2,1,0:T(2,128)(2,1)} %reshape.806), calls=%async_computation.2 | async-start | bytes 1048576 | tf_op jit(solution)/shard_map/all_to_all | solution.py:341
  225.3 192.7 %all-gather.15.cloned.1.call-start = ((), (), s32[]{:S(2)}) async-start(), calls=%async_computation.12 | async-start | bytes 4718592 | tf_op jit(solution)/shard_map/all_gather | solution.py:420
  226.1 605.5 %reduce-scatter.10.cloned.1.call-start = ((), (), s32[]{:S(2)}) async-start(), calls=%async_computation.20 | async-start | bytes 2621440 | tf_op jit(solution)/shard_map/reduce_scatter | solution.py:126
  260.5 9.9 collective-permute-start.4
  268.8 12.0 %collective-permute-start = (bf16[128,2048]{1,0:T(8,128)(2,1)S(1)}, bf16[128,2048]{1,0:T(8,128)(2,1)S(1)}, u32[]{:S(2)}, u32[]{:S(2)}) collective-permute-start(bf16[128,2048]{1,0:T(8,128)(2,1)S(1)} %dynamic-slice_convert_fusion.16), channel_id=1, source_target_pairs={{0,1},{1,0},{2,3},{3,2},{4,5},{5,4},{6,7},{7,6},{8,9},{9,8},{10,11... | collective-permute-start | bytes 1572872 | tf_op jit(solution)/shard_map/ppermute | solution.py:99
  270.5 14.4 %collective-permute-start.5 = (bf16[64,2048]{1,0:T(8,128)(2,1)S(1)}, bf16[64,2048]{1,0:T(8,128)(2,1)S(1)}, u32[]{:S(2)}, u32[]{:S(2)}) collective-permute-start(bf16[64,2048]{1,0:T(8,128)(2,1)S(1)} %dynamic-slice_convert_fusion.23), channel_id=1, source_target_pairs={{0,1},{1,0},{2,3},{3,2},{4,5},{5,4},{6,7},{7,6},{8,9},{9,8},{10,11... | collective-permute-start | bytes 786440 | tf_op jit(solution)/shard_map/ppermute | solution.py:99
  281.0 6.9 collective-permute-start.1
  284.9 8.7 collective-permute-start.6
  288.0 7.9 collective-permute-start.2
  294.4 11.1 collective-permute-start.7
  297.4 9.5 collective-permute-start.3
  338.9 168.3 %collective-permute-start.29 = (bf16[1024,1024]{1,0:T(8,128)(2,1)}, bf16[1024,1024]{1,0:T(8,128)(2,1)}, u32[]{:S(2)}, u32[]{:S(2)}) collective-permute-start(bf16[1024,1024]{1,0:T(8,128)(2,1)} %fusion.80), channel_id=1, source_target_pairs={{0,16},{16,0},{1,17},{17,1},{2,18},{18,2},{3,19},{19,3},{4,20},{20... | collective-permute-start | bytes 6291464 | tf_op jit(solution)/shard_map/ppermute | solution.py:121
  429.8 52.8 %collective-permute-start.18 = (bf16[1024,1024]{1,0:T(8,128)(2,1)}, bf16[1024,1024]{1,0:T(8,128)(2,1)}, u32[]{:S(2)}, u32[]{:S(2)}) collective-permute-start(bf16[1024,1024]{1,0:T(8,128)(2,1)} %fusion.79), channel_id=1, source_target_pairs={{0,16},{16,0},{1,17},{17,1},{2,18},{18,2},{3,19},{19,3},{4,20},{20... | collective-permute-start | bytes 6291464 | tf_op jit(solution)/shard_map/ppermute | solution.py:121
  434.4 52.7 %collective-permute-start.16 = (bf16[1024,1024]{1,0:T(8,128)(2,1)}, bf16[1024,1024]{1,0:T(8,128)(2,1)}, u32[]{:S(2)}, u32[]{:S(2)}) collective-permute-start(bf16[1024,1024]{1,0:T(8,128)(2,1)} %dynamic-slice_convert_fusion.5), channel_id=1, source_target_pairs={{0,16},{16,0},{1,17},{17,1},{2,18},{18,2},{3,19},{19,3},{4,20},{20... | collective-permute-start | bytes 6291464 | tf_op jit(solution)/shard_map/ppermute | solution.py:121
  438.7 52.7 %collective-permute-start.17 = (bf16[1024,1024]{1,0:T(8,128)(2,1)}, bf16[1024,1024]{1,0:T(8,128)(2,1)}, u32[]{:S(2)}, u32[]{:S(2)}) collective-permute-start(bf16[1024,1024]{1,0:T(8,128)(2,1)} %dynamic-slice_convert_fusion.4), channel_id=1, source_target_pairs={{0,16},{16,0},{1,17},{17,1},{2,18},{18,2},{3,19},{19,3},{4,20},{20... | collective-permute-start | bytes 6291464 | tf_op jit(solution)/shard_map/ppermute | solution.py:121
  447.5 63.7 %collective-permute-start.28 = (bf16[1024,1024]{1,0:T(8,128)(2,1)}, bf16[1024,1024]{1,0:T(8,128)(2,1)}, u32[]{:S(2)}, u32[]{:S(2)}) collective-permute-start(bf16[1024,1024]{1,0:T(8,128)(2,1)} %dynamic-slice_convert_fusion.1), channel_id=1, source_target_pairs={{0,16},{16,0},{1,17},{17,1},{2,18},{18,2},{3,19},{19,3},{4,20},{20... | collective-permute-start | bytes 6291464 | tf_op jit(solution)/shard_map/ppermute | solution.py:121
  482.6 57.4 %collective-permute-start.27 = (bf16[1024,1024]{1,0:T(8,128)(2,1)}, bf16[1024,1024]{1,0:T(8,128)(2,1)}, u32[]{:S(2)}, u32[]{:S(2)}) collective-permute-start(bf16[1024,1024]{1,0:T(8,128)(2,1)} %dynamic-slice_convert_fusion.2), channel_id=1, source_target_pairs={{0,16},{16,0},{1,17},{17,1},{2,18},{18,2},{3,19},{19,3},{4,20},{20... | collective-permute-start | bytes 6291464 | tf_op jit(solution)/shard_map/ppermute | solution.py:121
  503.4 14.4 %collective-permute-start.23 = (bf16[128,2048]{1,0:T(8,128)(2,1)}, bf16[128,2048]{1,0:T(8,128)(2,1)}, u32[]{:S(2)}, u32[]{:S(2)}) collective-permute-start(bf16[128,2048]{1,0:T(8,128)(2,1)} %dynamic-slice_convert_fusion.11), channel_id=1, source_target_pairs={{0,2},{1,3},{2,0},{3,1},{4,6},{5,7},{6,4},{7,5},{8,10},{9,11},{10,... | collective-permute-start | bytes 1572872 | tf_op jit(solution)/shard_map/ppermute | solution.py:99
  505.7 15.1 %collective-permute-start.19 = (bf16[128,2048]{1,0:T(8,128)(2,1)}, bf16[128,2048]{1,0:T(8,128)(2,1)}, u32[]{:S(2)}, u32[]{:S(2)}) collective-permute-start(bf16[128,2048]{1,0:T(8,128)(2,1)} %dynamic-slice_convert_fusion.12), channel_id=1, source_target_pairs={{0,1},{1,0},{2,3},{3,2},{4,5},{5,4},{6,7},{7,6},{8,9},{9,8},{10,11... | collective-permute-start | bytes 1572872 | tf_op jit(solution)/shard_map/ppermute | solution.py:99
  519.3 7.6 collective-permute-start.24
  522.4 7.4 collective-permute-start.20
  527.0 6.8 collective-permute-start.25
  529.8 7.1 collective-permute-start.21
  535.4 12.3 %collective-permute-start.26 = (bf16[128,2048]{1,0:T(8,128)(2,1)}, bf16[128,2048]{1,0:T(8,128)(2,1)}, u32[]{:S(2)}, u32[]{:S(2)}) collective-permute-start(bf16[128,2048]{1,0:T(8,128)(2,1)} %pad_maximum_fusion.17), channel_id=1, source_target_pairs={{0,2},{1,3},{2,0},{3,1},{4,6},{5,7},{6,4},{7,5},{8,10},{9,11},{10,... | collective-permute-start | bytes 1572872 | tf_op jit(solution)/shard_map/ppermute | solution.py:112
  538.5 11.5 %collective-permute-start.22 = (bf16[128,2048]{1,0:T(8,128)(2,1)}, bf16[128,2048]{1,0:T(8,128)(2,1)}, u32[]{:S(2)}, u32[]{:S(2)}) collective-permute-start(bf16[128,2048]{1,0:T(8,128)(2,1)} %pad_maximum_fusion.16), channel_id=1, source_target_pairs={{0,1},{1,0},{2,3},{3,2},{4,5},{5,4},{6,7},{7,6},{8,9},{9,8},{10,11... | collective-permute-start | bytes 1572872 | tf_op jit(solution)/shard_map/ppermute | solution.py:111
  554.0 279.8 %reduce-scatter.8.cloned.1.call-start = ((), (), s32[]{:S(2)}) async-start(), calls=%async_computation.19 | async-start | bytes 2621440 | tf_op jit(solution)/shard_map/reduce_scatter | solution.py:126
  554.5 281.3 %reduce-scatter.6.cloned.1.call-start = ((), (), s32[]{:S(2)}) async-start(), calls=%async_computation.18 | async-start | bytes 2621440 | tf_op jit(solution)/shard_map/reduce_scatter | solution.py:126
  567.3 58.2 %collective-permute-start.31 = (bf16[256,3072]{1,0:T(8,128)(2,1)}, bf16[256,3072]{1,0:T(8,128)(2,1)}, u32[]{:S(2)}, u32[]{:S(2)}) collective-permute-start(bf16[256,3072]{1,0:T(8,128)(2,1)} %get-tuple-element.103), channel_id=1, source_target_pairs={{0,4},{1,5},{2,6},{3,7},{16,20},{17,21},{18,22},{19,23}} | collective-permute-start | bytes 4718600 | tf_op jit(solution)/shard_map/ppermute | solution.py:149
  571.0 67.3 %collective-permute-start.34 = (bf16[256,3072]{1,0:T(8,128)(2,1)}, bf16[256,3072]{1,0:T(8,128)(2,1)}, u32[]{:S(2)}, u32[]{:S(2)}) collective-permute-start(bf16[256,3072]{1,0:T(8,128)(2,1)} %get-tuple-element.104), channel_id=1, source_target_pairs={{12,8},{13,9},{14,10},{15,11},{28,24},{29,25},{30,26},{31,27}} | collective-permute-start | bytes 4718600 | tf_op jit(solution)/shard_map/ppermute | solution.py:150
  629.4 66.5 %collective-permute-start.32 = (bf16[256,3072]{1,0:T(8,128)(2,1)}, bf16[256,3072]{1,0:T(8,128)(2,1)}, u32[]{:S(2)}, u32[]{:S(2)}) collective-permute-start(bf16[256,3072]{1,0:T(8,128)(2,1)} %add_convert_fusion.3), channel_id=1, source_target_pairs={{0,4},{4,8},{1,5},{5,9},{2,6},{6,10},{3,7},{7,11},{16,20},{20,24},... | collective-permute-start | bytes 4718600 | tf_op jit(solution)/shard_map/ppermute | solution.py:149
  701.7 17.9 %collective-permute-start.35 = (bf16[256,3072]{1,0:T(8,128)(2,1)S(1)}, bf16[256,3072]{1,0:T(8,128)(2,1)S(1)}, u32[]{:S(2)}, u32[]{:S(2)}) collective-permute-start(bf16[256,3072]{1,0:T(8,128)(2,1)S(1)} %get-tuple-element.102), channel_id=1, source_target_pairs={{8,4},{12,8},{9,5},{13,9},{10,6},{14,10},{11,7},{15,11},{24,20},{2... | collective-permute-start | bytes 4718600 | tf_op jit(solution)/shard_map/ppermute | solution.py:150
  713.5 114.9 %collective-permute-start.30 = (bf16[1024,512]{1,0:T(8,128)(2,1)}, bf16[1024,512]{1,0:T(8,128)(2,1)}, u32[]{:S(2)}, u32[]{:S(2)}) collective-permute-start(bf16[1024,512]{1,0:T(8,128)(2,1)} %dynamic-slice_convert_fusion.8), channel_id=1, source_target_pairs={{0,16},{16,0},{1,17},{17,1},{2,18},{18,2},{3,19},{19,3},{4,20},{20... | collective-permute-start | bytes 3145736 | tf_op jit(solution)/shard_map/ppermute | solution.py:121
  713.5 124.5 %collective-permute-start.33 = (bf16[256,3072]{1,0:T(8,128)(2,1)}, bf16[256,3072]{1,0:T(8,128)(2,1)}, u32[]{:S(2)}, u32[]{:S(2)}) collective-permute-start(bf16[256,3072]{1,0:T(8,128)(2,1)} %get-tuple-element.101), channel_id=1, source_target_pairs={{0,4},{4,8},{8,12},{1,5},{5,9},{9,13},{2,6},{6,10},{10,14},{3,7},{... | collective-permute-start | bytes 4718600 | tf_op jit(solution)/shard_map/ppermute | solution.py:149
  723.2 114.8 %collective-permute-start.36 = (bf16[256,3072]{1,0:T(8,128)(2,1)}, bf16[256,3072]{1,0:T(8,128)(2,1)}, u32[]{:S(2)}, u32[]{:S(2)}) collective-permute-start(bf16[256,3072]{1,0:T(8,128)(2,1)} %add_convert_fusion), channel_id=1, source_target_pairs={{4,0},{8,4},{12,8},{5,1},{9,5},{13,9},{6,2},{10,6},{14,10},{7,3},{... | collective-permute-start | bytes 4718600 | tf_op jit(solution)/shard_map/ppermute | solution.py:150
  726.3 100.1 %all-to-all-start.3 = ((bf16[512,4,2,64]{0,3,2,1:T(8,128)(2,1)}), bf16[512,4,2,64]{0,3,2,1:T(8,128)(2,1)}, u32[]{:S(2)}, u32[]{:S(2)}) async-start(bf16[512,4,2,64]{0,3,2,1:T(8,128)(2,1)} %bitcast.349), calls=%async_computation.3 | async-start | bytes 1048576 | tf_op jit(solution)/shard_map/all_to_all | solution.py:349
  903.6 57.7 %all-to-all-start.4 = ((bf16[4,2,98304]{2,1,0:T(2,128)(2,1)}), bf16[4,2,98304]{2,1,0:T(2,128)(2,1)}, u32[]{:S(2)}, u32[]{:S(2)}) async-start(bf16[4,2,98304]{2,1,0:T(2,128)(2,1)} %reshape.808), calls=%async_computation.7 | async-start | bytes 3145728 | tf_op jit(solution)/shard_map/all_to_all | solution.py:382
  907.9 80.6 %reduce-scatter.12.cloned.1.call-start = ((), (), s32[]{:S(2)}) async-start(), calls=%async_computation.21 | async-start | bytes 1310720 | tf_op jit(solution)/shard_map/reduce_scatter | solution.py:126
  908.5 212.8 %reduce-scatter.14.cloned.1.call-start = ((), (), s32[]{:S(2)}) async-start(), calls=%async_computation.22 | async-start | bytes 4259840 | tf_op jit(solution)/shard_map/reduce_scatter | solution.py:126
  987.2 13.3 %collective-permute-start.41 = (bf16[128,2048]{1,0:T(8,128)(2,1)}, bf16[128,2048]{1,0:T(8,128)(2,1)}, u32[]{:S(2)}, u32[]{:S(2)}) collective-permute-start(bf16[128,2048]{1,0:T(8,128)(2,1)} %dynamic-slice_convert_fusion.9), channel_id=1, source_target_pairs={{0,2},{1,3},{2,0},{3,1},{4,6},{5,7},{6,4},{7,5},{8,10},{9,11},{10,... | collective-permute-start | bytes 1572872 | tf_op jit(solution)/shard_map/ppermute | solution.py:99
  991.8 14.3 %collective-permute-start.37 = (bf16[128,2048]{1,0:T(8,128)(2,1)S(1)}, bf16[128,2048]{1,0:T(8,128)(2,1)S(1)}, u32[]{:S(2)}, u32[]{:S(2)}) collective-permute-start(bf16[128,2048]{1,0:T(8,128)(2,1)S(1)} %dynamic-slice_convert_fusion.10), channel_id=1, source_target_pairs={{0,1},{1,0},{2,3},{3,2},{4,5},{5,4},{6,7},{7,6},{8,9},{9,8},{10,11... | collective-permute-start | bytes 1572872 | tf_op jit(solution)/shard_map/ppermute | solution.py:99
  1002.0 8.1 collective-permute-start.42
  1006.3 6.5 collective-permute-start.38
  1010.2 6.8 collective-permute-start.43
  1012.9 8.3 collective-permute-start.39
  1017.1 13.4 %collective-permute-start.44 = (bf16[128,2048]{1,0:T(8,128)(2,1)S(1)}, bf16[128,2048]{1,0:T(8,128)(2,1)S(1)}, u32[]{:S(2)}, u32[]{:S(2)}) collective-permute-start(bf16[128,2048]{1,0:T(8,128)(2,1)S(1)} %pad_maximum_fusion.19), channel_id=1, source_target_pairs={{0,2},{1,3},{2,0},{3,1},{4,6},{5,7},{6,4},{7,5},{8,10},{9,11},{10,... | collective-permute-start | bytes 1572872 | tf_op jit(solution)/shard_map/ppermute | solution.py:112
  1021.2 10.7 collective-permute-start.40
  1040.3 12.2 %collective-permute-start.45 = (bf16[1024,1664]{0,1:T(8,128)(2,1)}, bf16[1024,1664]{0,1:T(8,128)(2,1)}, u32[]{:S(2)}, u32[]{:S(2)}) collective-permute-start(bf16[1024,1664]{0,1:T(8,128)(2,1)} %fusion.13), channel_id=1, source_target_pairs={{0,16},{16,0},{1,17},{17,1},{2,18},{18,2},{3,19},{19,3},{4,20},{20... | collective-permute-start | bytes 10223624 | tf_op jit(solution)/shard_map/ppermute | solution.py:121
  1048.9 14.5 %collective-permute-start.12 = (bf16[128,2048]{1,0:T(8,128)(2,1)}, bf16[128,2048]{1,0:T(8,128)(2,1)}, u32[]{:S(2)}, u32[]{:S(2)}) collective-permute-start(bf16[128,2048]{1,0:T(8,128)(2,1)} %dynamic-slice_convert_fusion.13), channel_id=1, source_target_pairs={{0,2},{1,3},{2,0},{3,1},{4,6},{5,7},{6,4},{7,5},{8,10},{9,11},{10,... | collective-permute-start | bytes 1572872 | tf_op jit(solution)/shard_map/ppermute | solution.py:99
  1050.4 16.6 %collective-permute-start.8 = (bf16[128,2048]{1,0:T(8,128)(2,1)}, bf16[128,2048]{1,0:T(8,128)(2,1)}, u32[]{:S(2)}, u32[]{:S(2)}) collective-permute-start(bf16[128,2048]{1,0:T(8,128)(2,1)} %dynamic-slice_convert_fusion.14), channel_id=1, source_target_pairs={{0,1},{1,0},{2,3},{3,2},{4,5},{5,4},{6,7},{7,6},{8,9},{9,8},{10,11... | collective-permute-start | bytes 1572872 | tf_op jit(solution)/shard_map/ppermute | solution.py:99
  1065.0 8.2 collective-permute-start.13
  1068.6 7.6 collective-permute-start.9
  1073.2 7.4 collective-permute-start.14
  1076.3 8.3 collective-permute-start.10
  1080.7 13.7 %collective-permute-start.15 = (bf16[128,2048]{1,0:T(8,128)(2,1)S(1)}, bf16[128,2048]{1,0:T(8,128)(2,1)S(1)}, u32[]{:S(2)}, u32[]{:S(2)}) collective-permute-start(bf16[128,2048]{1,0:T(8,128)(2,1)S(1)} %pad_maximum_fusion.15), channel_id=1, source_target_pairs={{0,2},{1,3},{2,0},{3,1},{4,6},{5,7},{6,4},{7,5},{8,10},{9,11},{10,... | collective-permute-start | bytes 1572872 | tf_op jit(solution)/shard_map/ppermute | solution.py:112
  1084.6 10.3 collective-permute-start.11
  (131 other events, 1894.8 us)
Sparse Core Ops, SparseCore 0:
  10.2 67.9 all-gather.10
  79.7 37.2 all-gather.12
  119.2 56.3 all-gather.18
  177.6 45.7 all-gather.24
  225.5 50.0 all-gather.22
  277.0 45.8 all-gather.20
  325.0 45.6 all-gather.16
  372.3 45.6 all-gather.14
  554.1 63.2 reduce-scatter.9
  620.1 71.7 reduce-scatter.7
  694.8 75.7 reduce-scatter.5
  911.3 46.9 reduce-scatter.11
  1059.7 61.5 reduce-scatter.13

commit v4 on v2

--- a/solution.py
+++ b/solution.py
@@ -114,11 +114,18 @@
 
 
 def chip_total(grad):
-    return lax.psum_scatter(grad.astype(jnp.bfloat16), "shard", scatter_dimension=0, tiled=True)
+    f32 = jnp.float32
+    shard = lax.axis_index("shard")
+    mine = half_of(grad, shard)
+    other = half_of(grad, 1 - shard)
+    got = lax.ppermute(other.astype(jnp.bfloat16), "shard", [(0, 1), (1, 0)])
+    return mine.astype(f32) + got.astype(f32)
 
 
 def line_total(staged):
-    return lax.psum_scatter(staged, "context", scatter_dimension=0, tiled=True).astype(jnp.float32)
+    return lax.psum_scatter(
+        staged.astype(jnp.bfloat16), "context", scatter_dimension=0, tiled=True
+    ).astype(jnp.float32)
 
 
 def rows_total(grad):
@@ -472,10 +479,11 @@
     grad_h1, reduced_o = lax.optimization_barrier((grad_h1, reduced_o))
     grad_gattn = jnp.sum(grad_h1 * norm1, axis=0)
     grad_x_part = (grad_resid + norm_back(grad_h1, norm1, inv1, gain_attn)).astype(bf16)
-    reduced_qkv = rows_total(contract_first(h1, grad_qkv))
-    reduced_gains = lax.psum_scatter(
-        jnp.stack([grad_gattn, grad_gmlp], axis=1), ROWS, scatter_dimension=0, tiled=True
-    )
+    gain_slab = jnp.pad(jnp.stack([grad_gattn, grad_gmlp], axis=1), ((0, 0), (0, 126)))
+    reduced_qkv = rows_total(
+        jnp.concatenate([contract_first(h1, grad_qkv), gain_slab], axis=1)
+    )
+    reduced_gains = reduced_qkv[:, 3 * cols :]
     reduced_gate, reduced_up, reduced_down = (
         jnp.concatenate([chunk[which] for chunk in reduced], axis=1) for which in range(3)
     )
@@ -484,7 +492,7 @@
         grad_x_part.reshape(1, rows, width),
         reduced_qkv[:, :cols],
         reduced_qkv[:, cols : 2 * cols],
-        reduced_qkv[:, 2 * cols :],
+        reduced_qkv[:, 2 * cols : 3 * cols],
         reduced_o,
         reduced_gate,
         reduced_up,

time: 1100 us -> 984 us (0.89)
  waiting for transfers between devices: 568 us -> 420 us
  other arithmetic: 107 us -> 145 us
  local copies, waits for them, and re-layouts: 95.9 us -> 124 us
  matrix products: 209 us -> 184 us
    reduce_scatter x16 -> x8, waiting for transfers between devices: 225 us -> 81.1 us  [line_total(): lax.psum_scatter(staged.astype(jnp.bfloat16), 'context', scatter_dimensio...]
    add x0 -> x8, other arithmetic: none -> 33.5 us  [the longest x7 31.8 us: chip_total(): return mine.astype(f32) + got.astype(f32)]
    ppermute x16, waiting for transfers between devices: 59.8 us -> 41.9 us  [swap(): return lax.ppermute(value.astype(bf16), 'tensor', pairs).astype(f32)]
    dot_general x8, matrix products: 43.5 us -> 26.2 us  [contract_first(): lax.dot_general(left, right, (((0,), (0,)), ((), ())), preferred_element_...]
    convert_element_type x0 -> x7, local copies, waits for them, and re-layouts: none -> 16.3 us  [chip_total(): got = lax.ppermute(other.astype(jnp.bfloat16), 'shard', [(0, 1), (1, 0)])]
    all_to_all x1, waiting for transfers between devices: 14.8 us -> 28.6 us  [backward(): grad = lax.all_to_all(grad, 'context', 1, 0, tiled=True)]
    unnamed x228 -> x282, local copies, waits for them, and re-layouts: 34.1 us -> 44.7 us
    convert_element_type x7 -> x9, other arithmetic: 14.7 us -> 24.4 us  [the longest x7 14.8 us: line_total(): return lax.psum_scatter(staged.astype(jnp.bfloat16), 'context', scatter_d...]
  transfers between devices with their start and end apart: 62 -> 61, of which waited for: 42 -> 37; matrix products, arithmetic and copies ran while one was open for 35% -> 40% of each run, Pallas kernels for 0% -> 0%
where the time goes in v4:
time: 984 us; the launch traced here: 977 us
  waiting for transfers between devices  420 us (43%)
  matrix products  184 us (19%)
  other arithmetic  145 us (15%)
  local copies, waits for them, and re-layouts  124 us (13%)
  starting transfers between devices  63.5 us (6%)
  blocking collectives  24.1 us (2%)
  between operations  16.6 us (2%)
    reduce_scatter x8, waiting for transfers between devices, line_total(): lax.psum_scatter(staged.astype(jnp.bfloat16), 'context', scatter_dimensio...  81.1 us
    all_gather x6, waiting for transfers between devices, on_device(): lax.all_gather(weight[:, part], ROWS, axis=0, tiled=True)  57.5 us
    all_to_all x1, waiting for transfers between devices, __init__(): stacked = lax.all_to_all(stacked, 'context', 2, 0, tiled=True)  54.5 us
    all_to_all x1, waiting for transfers between devices, backward(): stacked = lax.all_to_all(stacked, 'context', 0, 2, tiled=True)  53.1 us
    unnamed x282, local copies, waits for them, and re-layouts  44.7 us
    ppermute x16, waiting for transfers between devices, swap(): return lax.ppermute(value.astype(bf16), 'tensor', pairs).astype(f32)  41.9 us
    add x7, other arithmetic, chip_total(): return mine.astype(f32) + got.astype(f32)  31.8 us
    all_gather x1, waiting for transfers between devices, on_device(): lax.all_gather(jnp.concatenate([w_q, w_k, w_v], axis=1), ROWS, axis=0, ti...  29.5 us
  transfers between devices with their start and end apart: 61, of which 37 were waited for; matrix products, arithmetic and copies ran while one was open for 40% of the time, Pallas kernels for 0%

profile of v4, /device:TPU:0, one launch (start us, length us, event | category | flops | bytes accessed | tf_op | source)
XLA Modules:
  0.0 977.3 jit_solution(10960397700452773397)
XLA Ops:
  17.3 6.3 all-to-all-start.1
  23.7 24.1 %all-gather.1 = bf16[8,1,512]{2,1,0:T(2,128)(2,1)S(1)} all-gather(bf16[1,1,512]{2,1,0:T(2,128)(2,1)S(1)} %reshape.803), channel_id=2, replica_groups=mesh['shard'=2,'context'=4,'tensor'=4] {'shard','context'}, dimensions={0}, use_global_device_ids=true | all-gather | bytes 9216 | tf_op jit(solution)/shard_map/all_gather | solution.py:385
  48.7 29.5 %all-gather.11.cloned.1.call-done = bf16[2048,1536]{1,0:T(8,128)(2,1)} async-done(((bf16[256,1536]{1,0:T(8,128)(2,1)}), bf16[2048,1536]{1,0:T(8,128)(2,1)}) %all-gather.11.cloned.1.call-update) | async-done | bytes 6291472 | tf_op jit(solution)/shard_map/all_gather | solution.py:383
  78.1 5.6 fusion.135
  96.4 4.3 all-to-all-start
  102.1 4.5 compare_and_fusion.3
  106.6 54.5 %all-to-all-done = bf16[512,3,4,2,64]{0,4,3,1,2:T(8,128)(2,1)} async-done(((bf16[512,3,4,2,64]{0,4,3,1,2:T(8,128)(2,1)}), bf16[512,3,4,2,64]{0,4,3,1,2:T(8,128)(2,1)}, u32[]{:S(2)}, u32[]{:S(2)}) %all-to-all-start) | async-done | bytes 1572896 | tf_op jit(solution)/shard_map/all_to_all | solution.py:269
  164.8 3.8 reshape.790
  172.3 5.9 fusion.25
  178.2 5.1 fusion.26
  185.3 10.7 %fusion = (f32[2,512]{1,0:T(2,128)S(1)}, f32[2,512]{1,0:T(2,128)S(1)}) fusion(f32[2,512,2048]{2,1,0:T(8,128)S(1)} %get-tuple-element.206, f32[2,512]{1,0:T(2,128)S(1)} %get-tuple-element.205, pred[512,2048]{1,0:T(8,128)(4,1)S(1)} %copy-done.45, f32[2,512]{1,0:T(2,128)S(1)} %get-tuple-element.203, f32[2,512,2048]{2,1,0:T(8,128)} %get-tuple-element.204, ...), kind=kLoop, calls=%fused_computation.20 | loop fusion | flops 20969472 | bytes 18890752 | tf_op jit(solution)/shard_map/reduce_sum | solution.py:306
  196.0 5.2 fusion.119
  204.0 7.8 fusion.4
  214.6 5.3 fusion.113
  225.3 4.1 all-to-all-start.2
  230.4 28.2 %all-to-all-done.2 = bf16[4,2,32768]{2,1,0:T(2,128)(2,1)} async-done(((bf16[4,2,32768]{2,1,0:T(2,128)(2,1)}), bf16[4,2,32768]{2,1,0:T(2,128)(2,1)}, u32[]{:S(2)}, u32[]{:S(2)}) %all-to-all-start.2) | async-done | bytes 524320 | tf_op jit(solution)/shard_map/all_to_all | solution.py:318
  271.3 6.7 fusion.88
  281.9 8.2 collective-permute-done
  290.8 3.8 collective-permute-done.5
  297.2 6.4 collective-permute-done.6
  308.2 6.5 fusion.86
  318.7 4.7 multiply_convert_fusion.4
  323.4 6.5 fusion.204
  329.9 7.4 multiply_convert_fusion.7
  357.6 17.0 %all-gather.23.cloned.1.call-done = bf16[2048,1024]{1,0:T(8,128)(2,1)} async-done(((bf16[256,1024]{1,0:T(8,128)(2,1)}), bf16[2048,1024]{1,0:T(8,128)(2,1)}) %all-gather.23.cloned.1.call-update) | async-done | bytes 4194320 | tf_op jit(solution)/shard_map/all_gather | solution.py:397
  374.6 6.9 fusion.206
  381.5 40.4 %all-gather.21.cloned.1.call-done = bf16[2048,1024]{1,0:T(8,128)(2,1)} async-done(((bf16[256,1024]{1,0:T(8,128)(2,1)}), bf16[2048,1024]{1,0:T(8,128)(2,1)}) %all-gather.21.cloned.1.call-update) | async-done | bytes 4194320 | tf_op jit(solution)/shard_map/all_gather | solution.py:397
  421.9 8.4 multiply_convert_fusion.5
  433.2 4.5 convolution_add_fusion
  437.7 3.8 bitcast_add_fusion.1
  441.5 4.9 convert_add_fusion.4
  446.4 5.0 convert_add_fusion.3
  451.5 7.5 fusion.213
  459.2 4.3 fusion.82
  465.4 6.6 dynamic-slice_convert_fusion.1
  492.9 5.0 bitcast_add_fusion
  497.9 4.9 convert_add_fusion.1
  525.6 4.9 convert_add_fusion.2
  545.4 4.1 multiply_add_fusion
  557.7 4.2 all-to-all-start.3
  563.3 28.6 %all-to-all-done.3 = bf16[512,4,2,64]{0,3,2,1:T(8,128)(2,1)} async-done(((bf16[512,4,2,64]{0,3,2,1:T(8,128)(2,1)}), bf16[512,4,2,64]{0,3,2,1:T(8,128)(2,1)}, u32[]{:S(2)}, u32[]{:S(2)}) %all-to-all-start.3) | async-done | bytes 524320 | tf_op jit(solution)/shard_map/all_to_all | solution.py:326
  604.8 6.8 multiply_convert_fusion.3
  615.1 6.5 multiply_convert_fusion
  623.8 3.9 multiply_convert_fusion.1
  629.8 5.2 multiply_convert_fusion.2
  644.7 4.1 fusion.64
  658.1 27.6 %reduce-scatter.17.cloned.1.call-done = bf16[256,1024]{1,0:T(8,128)(2,1)} async-done(((bf16[1024,1024]{1,0:T(8,128)(2,1)}), bf16[256,1024]{1,0:T(8,128)(2,1)}) %reduce-scatter.17.cloned.1.call-update) | async-done | bytes 524304 | tf_op jit(solution)/shard_map/reduce_scatter | solution.py:126
  687.9 43.5 %reduce-scatter.15.cloned.1.call-done = bf16[256,1024]{1,0:T(8,128)(2,1)} async-done(((bf16[1024,1024]{1,0:T(8,128)(2,1)}), bf16[256,1024]{1,0:T(8,128)(2,1)}) %reduce-scatter.15.cloned.1.call-update) | async-done | bytes 524304 | tf_op jit(solution)/shard_map/reduce_scatter | solution.py:126
  733.4 8.4 copy.61
  741.9 5.0 reshape.808
  746.9 4.4 all-to-all-start.4
  751.9 53.1 %all-to-all-done.4 = bf16[4,2,98304]{2,1,0:T(2,128)(2,1)} async-done(((bf16[4,2,98304]{2,1,0:T(2,128)(2,1)}), bf16[4,2,98304]{2,1,0:T(2,128)(2,1)}, u32[]{:S(2)}, u32[]{:S(2)}) %all-to-all-start.4) | async-done | bytes 1572896 | tf_op jit(solution)/shard_map/all_to_all | solution.py:359
  805.0 5.0 reshape.809
  810.0 8.7 copy.69
  820.6 6.2 fusion.133
  837.0 7.0 collective-permute-done.35
  856.8 3.8 collective-permute-done.37
  861.0 4.4 collective-permute-done.33
  884.0 5.0 fusion.205
  896.1 6.2 fusion.16
  902.4 4.8 collective-permute-done.12
  912.9 3.9 collective-permute-done.13
  928.4 9.6 collective-permute-done.15
  954.7 10.0 %reduce-scatter.23.cloned.1.call-done = bf16[256,1664]{0,1:T(8,128)(2,1)} async-done(((bf16[1024,1664]{0,1:T(8,128)(2,1)}), bf16[256,1664]{0,1:T(8,128)(2,1)}) %reduce-scatter.23.cloned.1.call-update) | async-done | bytes 851984 | tf_op jit(solution)/shard_map/reduce_scatter | solution.py:126
  (560 shorter events, 301.4 us)
Async XLA Ops:
  7.2 71.0 %all-gather.11.cloned.1.call-start = ((), (), s32[]{:S(2)}) async-start(), calls=%async_computation.13 | async-start | bytes 7077888 | tf_op jit(solution)/shard_map/all_gather | solution.py:383
  9.4 254.1 %all-gather.13.cloned.1.call-start = ((), (), s32[]{:S(2)}) async-start(), calls=%async_computation.14 | async-start | bytes 2359296 | tf_op jit(solution)/shard_map/all_gather | solution.py:384
  10.2 37.6 %copy-start = (bf16[1,512,2048]{2,1,0:T(8,128)(2,1)S(1)}, bf16[1,512,2048]{2,1,0:T(8,128)(2,1)}, u32[]{:S(2)}) copy-start(bf16[1,512,2048]{2,1,0:T(8,128)(2,1)} %param.13) | copy-start | bytes 6291460
  10.2 261.2 %all-gather.19.cloned.1.call-start = ((), (), s32[]{:S(2)}) async-start(), calls=%async_computation.17 | async-start | bytes 4718592 | tf_op jit(solution)/shard_map/all_gather | solution.py:397
  12.6 295.5 %all-gather.25.cloned.1.call-start = ((), (), s32[]{:S(2)}) async-start(), calls=%async_computation.20 | async-start | bytes 4718592 | tf_op jit(solution)/shard_map/all_gather | solution.py:397
  13.2 310.2 %all-gather.17.cloned.1.call-start = ((), (), s32[]{:S(2)}) async-start(), calls=%async_computation.16 | async-start | bytes 4718592 | tf_op jit(solution)/shard_map/all_gather | solution.py:397
  14.3 315.6 %all-gather.15.cloned.1.call-start = ((), (), s32[]{:S(2)}) async-start(), calls=%async_computation.15 | async-start | bytes 4718592 | tf_op jit(solution)/shard_map/all_gather | solution.py:397
  17.3 79.0 %all-to-all-start.1 = ((s32[4,2,512]{2,1,0:T(2,128)}), s32[4,2,512]{2,1,0:T(2,128)S(1)}, u32[]{:S(2)}, u32[]{:S(2)}) async-start(s32[4,2,512]{2,1,0:T(2,128)} %broadcast_in_dim.158), calls=%async_computation.1 | async-start | bytes 32768 | tf_op jit(solution)/shard_map/all_to_all | solution.py:276
  47.8 36.0 %copy-start.85 = (f32[1,2,8,128]{3,1,2,0:T(2,128)}, f32[1,2,8,128]{3,1,2,0:T(2,128)S(1)}, u32[]{:S(2)}) copy-start(f32[1,2,8,128]{3,1,2,0:T(2,128)S(1)} %copy.72) | copy-start | bytes 24580
  96.4 64.7 %all-to-all-start = ((bf16[512,3,4,2,64]{0,4,3,1,2:T(8,128)(2,1)}), bf16[512,3,4,2,64]{0,4,3,1,2:T(8,128)(2,1)}, u32[]{:S(2)}, u32[]{:S(2)}) async-start(bf16[512,3,4,2,64]{0,4,3,1,2:T(8,128)(2,1)} %copy.55), calls=%async_computation | async-start | bytes 3145728 | tf_op jit(solution)/shard_map/all_to_all | solution.py:269
  100.7 273.9 %all-gather.23.cloned.1.call-start = ((), (), s32[]{:S(2)}) async-start(), calls=%async_computation.19 | async-start | bytes 4718592 | tf_op jit(solution)/shard_map/all_gather | solution.py:397
  106.6 105.2 %copy-start.39 = (pred[512,2048]{1,0:T(8,128)(4,1)}, pred[512,2048]{1,0:T(8,128)(4,1)S(1)}, u32[]{:S(2)}) copy-start(pred[512,2048]{1,0:T(8,128)(4,1)S(1)} %get-tuple-element.182) | copy-start | bytes 3145732
  225.3 33.2 %all-to-all-start.2 = ((bf16[4,2,32768]{2,1,0:T(2,128)(2,1)}), bf16[4,2,32768]{2,1,0:T(2,128)(2,1)}, u32[]{:S(2)}, u32[]{:S(2)}) async-start(bf16[4,2,32768]{2,1,0:T(2,128)(2,1)} %reshape.806), calls=%async_computation.2 | async-start | bytes 1048576 | tf_op jit(solution)/shard_map/all_to_all | solution.py:318
  229.4 192.5 %all-gather.21.cloned.1.call-start = ((), (), s32[]{:S(2)}) async-start(), calls=%async_computation.18 | async-start | bytes 4718592 | tf_op jit(solution)/shard_map/all_gather | solution.py:397
  230.2 366.9 %reduce-scatter.13.cloned.1.call-start = ((), (), s32[]{:S(2)}) async-start(), calls=%async_computation.23 | async-start | bytes 2621440 | tf_op jit(solution)/shard_map/reduce_scatter | solution.py:126
  269.7 9.9 %collective-permute-start.4 = (bf16[128,2048]{1,0:T(8,128)(2,1)S(1)}, bf16[128,2048]{1,0:T(8,128)(2,1)}, u32[]{:S(2)}, u32[]{:S(2)}) collective-permute-start(bf16[128,2048]{1,0:T(8,128)(2,1)S(1)} %dynamic-slice_convert_fusion.13), channel_id=1, source_target_pairs={{0,2},{1,3},{2,0},{3,1},{4,6},{5,7},{6,4},{7,5},{8,10},{9,11},{10,... | collective-permute-start | bytes 1572872 | tf_op jit(solution)/shard_map/ppermute | solution.py:99
  278.1 12.0 %collective-permute-start = (bf16[128,2048]{1,0:T(8,128)(2,1)S(1)}, bf16[128,2048]{1,0:T(8,128)(2,1)S(1)}, u32[]{:S(2)}, u32[]{:S(2)}) collective-permute-start(bf16[128,2048]{1,0:T(8,128)(2,1)S(1)} %dynamic-slice_convert_fusion.14), channel_id=1, source_target_pairs={{0,1},{1,0},{2,3},{3,2},{4,5},{5,4},{6,7},{7,6},{8,9},{9,8},{10,11... | collective-permute-start | bytes 1572872 | tf_op jit(solution)/shard_map/ppermute | solution.py:99
  280.8 13.7 %collective-permute-start.5 = (bf16[64,2048]{1,0:T(8,128)(2,1)S(1)}, bf16[64,2048]{1,0:T(8,128)(2,1)S(1)}, u32[]{:S(2)}, u32[]{:S(2)}) collective-permute-start(bf16[64,2048]{1,0:T(8,128)(2,1)S(1)} %dynamic-slice_convert_fusion.21), channel_id=1, source_target_pairs={{0,1},{1,0},{2,3},{3,2},{4,5},{5,4},{6,7},{7,6},{8,9},{9,8},{10,11... | collective-permute-start | bytes 786440 | tf_op jit(solution)/shard_map/ppermute | solution.py:99
  290.3 6.4 collective-permute-start.1
  294.6 9.0 collective-permute-start.6
  296.8 9.0 collective-permute-start.2
  304.6 10.1 %collective-permute-start.7 = (bf16[128,2048]{1,0:T(8,128)(2,1)}, bf16[128,2048]{1,0:T(8,128)(2,1)}, u32[]{:S(2)}, u32[]{:S(2)}) collective-permute-start(bf16[128,2048]{1,0:T(8,128)(2,1)} %pad_maximum_fusion.13), channel_id=1, source_target_pairs={{0,2},{1,3},{2,0},{3,1},{4,6},{5,7},{6,4},{7,5},{8,10},{9,11},{10,... | collective-permute-start | bytes 1572872 | tf_op jit(solution)/shard_map/ppermute | solution.py:112
  306.8 9.5 collective-permute-start.3
  341.4 96.3 %collective-permute-start.18 = (bf16[1024,1024]{0,1:T(8,128)(2,1)}, bf16[1024,1024]{0,1:T(8,128)(2,1)}, u32[]{:S(2)}, u32[]{:S(2)}) collective-permute-start(bf16[1024,1024]{0,1:T(8,128)(2,1)} %fusion.79), channel_id=1, source_target_pairs={{0,16},{16,0},{1,17},{17,1},{2,18},{18,2},{3,19},{19,3},{4,20},{20... | collective-permute-start | bytes 6291464 | tf_op jit(solution)/shard_map/ppermute | solution.py:121
  348.3 93.2 %collective-permute-start.16 = (bf16[1024,1024]{1,0:T(8,128)(2,1)}, bf16[1024,1024]{1,0:T(8,128)(2,1)}, u32[]{:S(2)}, u32[]{:S(2)}) collective-permute-start(bf16[1024,1024]{1,0:T(8,128)(2,1)} %dynamic-slice_convert_fusion.5), channel_id=1, source_target_pairs={{0,16},{16,0},{1,17},{17,1},{2,18},{18,2},{3,19},{19,3},{4,20},{20... | collective-permute-start | bytes 6291464 | tf_op jit(solution)/shard_map/ppermute | solution.py:121
  357.6 88.9 %collective-permute-start.17 = (bf16[1024,1024]{1,0:T(8,128)(2,1)}, bf16[1024,1024]{1,0:T(8,128)(2,1)}, u32[]{:S(2)}, u32[]{:S(2)}) collective-permute-start(bf16[1024,1024]{1,0:T(8,128)(2,1)} %dynamic-slice_convert_fusion.4), channel_id=1, source_target_pairs={{0,16},{16,0},{1,17},{17,1},{2,18},{18,2},{3,19},{19,3},{4,20},{20... | collective-permute-start | bytes 6291464 | tf_op jit(solution)/shard_map/ppermute | solution.py:121
  451.4 147.7 %reduce-scatter.11.cloned.1.call-start = ((), (), s32[]{:S(2)}) async-start(), calls=%async_computation.22 | async-start | bytes 2621440 | tf_op jit(solution)/shard_map/reduce_scatter | solution.py:126
  459.0 142.3 %reduce-scatter.9.cloned.1.call-start = ((), (), s32[]{:S(2)}) async-start(), calls=%async_computation.21 | async-start | bytes 2621440 | tf_op jit(solution)/shard_map/reduce_scatter | solution.py:126
  465.2 27.7 %collective-permute-start.29 = (bf16[1024,1024]{0,1:T(8,128)(2,1)}, bf16[1024,1024]{0,1:T(8,128)(2,1)}, u32[]{:S(2)}, u32[]{:S(2)}) collective-permute-start(bf16[1024,1024]{0,1:T(8,128)(2,1)} %fusion.80), channel_id=1, source_target_pairs={{0,16},{16,0},{1,17},{17,1},{2,18},{18,2},{3,19},{19,3},{4,20},{20... | collective-permute-start | bytes 6291464 | tf_op jit(solution)/shard_map/ppermute | solution.py:121
  472.1 25.9 %collective-permute-start.28 = (bf16[1024,1024]{1,0:T(8,128)(2,1)}, bf16[1024,1024]{1,0:T(8,128)(2,1)}, u32[]{:S(2)}, u32[]{:S(2)}) collective-permute-start(bf16[1024,1024]{1,0:T(8,128)(2,1)} %dynamic-slice_convert_fusion.1), channel_id=1, source_target_pairs={{0,16},{16,0},{1,17},{17,1},{2,18},{18,2},{3,19},{19,3},{4,20},{20... | collective-permute-start | bytes 6291464 | tf_op jit(solution)/shard_map/ppermute | solution.py:121
  479.5 46.0 %collective-permute-start.27 = (bf16[1024,1024]{1,0:T(8,128)(2,1)}, bf16[1024,1024]{1,0:T(8,128)(2,1)}, u32[]{:S(2)}, u32[]{:S(2)}) collective-permute-start(bf16[1024,1024]{1,0:T(8,128)(2,1)} %dynamic-slice_convert_fusion.2), channel_id=1, source_target_pairs={{0,16},{16,0},{1,17},{17,1},{2,18},{18,2},{3,19},{19,3},{4,20},{20... | collective-permute-start | bytes 6291464 | tf_op jit(solution)/shard_map/ppermute | solution.py:121
  488.8 14.4 %collective-permute-start.23 = (bf16[128,2048]{1,0:T(8,128)(2,1)}, bf16[128,2048]{1,0:T(8,128)(2,1)}, u32[]{:S(2)}, u32[]{:S(2)}) collective-permute-start(bf16[128,2048]{1,0:T(8,128)(2,1)} %dynamic-slice_convert_fusion.9), channel_id=1, source_target_pairs={{0,2},{1,3},{2,0},{3,1},{4,6},{5,7},{6,4},{7,5},{8,10},{9,11},{10,... | collective-permute-start | bytes 1572872 | tf_op jit(solution)/shard_map/ppermute | solution.py:99
  491.2 15.2 %collective-permute-start.19 = (bf16[128,2048]{1,0:T(8,128)(2,1)}, bf16[128,2048]{1,0:T(8,128)(2,1)}, u32[]{:S(2)}, u32[]{:S(2)}) collective-permute-start(bf16[128,2048]{1,0:T(8,128)(2,1)} %dynamic-slice_convert_fusion.10), channel_id=1, source_target_pairs={{0,1},{1,0},{2,3},{3,2},{4,5},{5,4},{6,7},{7,6},{8,9},{9,8},{10,11... | collective-permute-start | bytes 1572872 | tf_op jit(solution)/shard_map/ppermute | solution.py:99
  492.7 163.3 %reduce-scatter.19.cloned.1.call-start = ((), (), s32[]{:S(2)}) async-start(), calls=%async_computation.26 | async-start | bytes 2621440 | tf_op jit(solution)/shard_map/reduce_scatter | solution.py:126
  504.8 7.7 collective-permute-start.24
  507.9 7.4 collective-permute-start.20
  512.5 6.9 collective-permute-start.25
  515.3 7.2 collective-permute-start.21
  521.1 12.2 %collective-permute-start.26 = (bf16[128,2048]{1,0:T(8,128)(2,1)}, bf16[128,2048]{1,0:T(8,128)(2,1)}, u32[]{:S(2)}, u32[]{:S(2)}) collective-permute-start(bf16[128,2048]{1,0:T(8,128)(2,1)} %pad_maximum_fusion.17), channel_id=1, source_target_pairs={{0,2},{1,3},{2,0},{3,1},{4,6},{5,7},{6,4},{7,5},{8,10},{9,11},{10,... | collective-permute-start | bytes 1572872 | tf_op jit(solution)/shard_map/ppermute | solution.py:112
  524.1 11.8 %collective-permute-start.22 = (bf16[128,2048]{1,0:T(8,128)(2,1)}, bf16[128,2048]{1,0:T(8,128)(2,1)}, u32[]{:S(2)}, u32[]{:S(2)}) collective-permute-start(bf16[128,2048]{1,0:T(8,128)(2,1)} %pad_maximum_fusion.16), channel_id=1, source_target_pairs={{0,1},{1,0},{2,3},{3,2},{4,5},{5,4},{6,7},{7,6},{8,9},{9,8},{10,11... | collective-permute-start | bytes 1572872 | tf_op jit(solution)/shard_map/ppermute | solution.py:111
  539.8 145.9 %reduce-scatter.17.cloned.1.call-start = ((), (), s32[]{:S(2)}) async-start(), calls=%async_computation.25 | async-start | bytes 2621440 | tf_op jit(solution)/shard_map/reduce_scatter | solution.py:126
  555.9 37.9 %collective-permute-start.30 = (bf16[1024,512]{1,0:T(8,128)(2,1)}, bf16[1024,512]{1,0:T(8,128)(2,1)}, u32[]{:S(2)}, u32[]{:S(2)}) collective-permute-start(bf16[1024,512]{1,0:T(8,128)(2,1)} %dynamic-slice_convert_fusion.6), channel_id=1, source_target_pairs={{0,16},{16,0},{1,17},{17,1},{2,18},{18,2},{3,19},{19,3},{4,20},{20... | collective-permute-start | bytes 3145736 | tf_op jit(solution)/shard_map/ppermute | solution.py:121
  557.7 34.2 %all-to-all-start.3 = ((bf16[512,4,2,64]{0,3,2,1:T(8,128)(2,1)}), bf16[512,4,2,64]{0,3,2,1:T(8,128)(2,1)}, u32[]{:S(2)}, u32[]{:S(2)}) async-start(bf16[512,4,2,64]{0,3,2,1:T(8,128)(2,1)} %bitcast.349), calls=%async_computation.3 | async-start | bytes 1048576 | tf_op jit(solution)/shard_map/all_to_all | solution.py:326
  561.9 169.4 %reduce-scatter.15.cloned.1.call-start = ((), (), s32[]{:S(2)}) async-start(), calls=%async_computation.24 | async-start | bytes 2621440 | tf_op jit(solution)/shard_map/reduce_scatter | solution.py:126
  746.9 58.1 %all-to-all-start.4 = ((bf16[4,2,98304]{2,1,0:T(2,128)(2,1)}), bf16[4,2,98304]{2,1,0:T(2,128)(2,1)}, u32[]{:S(2)}, u32[]{:S(2)}) async-start(bf16[4,2,98304]{2,1,0:T(2,128)(2,1)} %reshape.808), calls=%async_computation.10 | async-start | bytes 3145728 | tf_op jit(solution)/shard_map/all_to_all | solution.py:359
  751.2 81.0 %reduce-scatter.21.cloned.1.call-start = ((), (), s32[]{:S(2)}) async-start(), calls=%async_computation.27 | async-start | bytes 1310720 | tf_op jit(solution)/shard_map/reduce_scatter | solution.py:126
  751.8 212.9 %reduce-scatter.23.cloned.1.call-start = ((), (), s32[]{:S(2)}) async-start(), calls=%async_computation.28 | async-start | bytes 4259840 | tf_op jit(solution)/shard_map/reduce_scatter | solution.py:126
  830.8 13.3 %collective-permute-start.35 = (bf16[128,2048]{1,0:T(8,128)(2,1)}, bf16[128,2048]{1,0:T(8,128)(2,1)}, u32[]{:S(2)}, u32[]{:S(2)}) collective-permute-start(bf16[128,2048]{1,0:T(8,128)(2,1)} %dynamic-slice_convert_fusion.7), channel_id=1, source_target_pairs={{0,2},{1,3},{2,0},{3,1},{4,6},{5,7},{6,4},{7,5},{8,10},{9,11},{10,... | collective-permute-start | bytes 1572872 | tf_op jit(solution)/shard_map/ppermute | solution.py:99
  835.5 14.4 %collective-permute-start.31 = (bf16[128,2048]{1,0:T(8,128)(2,1)S(1)}, bf16[128,2048]{1,0:T(8,128)(2,1)S(1)}, u32[]{:S(2)}, u32[]{:S(2)}) collective-permute-start(bf16[128,2048]{1,0:T(8,128)(2,1)S(1)} %dynamic-slice_convert_fusion.8), channel_id=1, source_target_pairs={{0,1},{1,0},{2,3},{3,2},{4,5},{5,4},{6,7},{7,6},{8,9},{9,8},{10,11... | collective-permute-start | bytes 1572872 | tf_op jit(solution)/shard_map/ppermute | solution.py:99
  845.6 8.2 collective-permute-start.36
  850.1 6.6 collective-permute-start.32
  853.9 6.7 collective-permute-start.37
  856.8 8.7 collective-permute-start.33
  860.7 13.7 %collective-permute-start.38 = (bf16[128,2048]{1,0:T(8,128)(2,1)S(1)}, bf16[128,2048]{1,0:T(8,128)(2,1)S(1)}, u32[]{:S(2)}, u32[]{:S(2)}) collective-permute-start(bf16[128,2048]{1,0:T(8,128)(2,1)S(1)} %pad_maximum_fusion.19), channel_id=1, source_target_pairs={{0,2},{1,3},{2,0},{3,1},{4,6},{5,7},{6,4},{7,5},{8,10},{9,11},{10,... | collective-permute-start | bytes 1572872 | tf_op jit(solution)/shard_map/ppermute | solution.py:112
  865.5 10.2 %collective-permute-start.34 = (bf16[128,2048]{1,0:T(8,128)(2,1)S(1)}, bf16[128,2048]{1,0:T(8,128)(2,1)S(1)}, u32[]{:S(2)}, u32[]{:S(2)}) collective-permute-start(bf16[128,2048]{1,0:T(8,128)(2,1)S(1)} %pad_maximum_fusion.18), channel_id=1, source_target_pairs={{0,1},{1,0},{2,3},{3,2},{4,5},{5,4},{6,7},{7,6},{8,9},{9,8},{10,11... | collective-permute-start | bytes 1572872 | tf_op jit(solution)/shard_map/ppermute | solution.py:111
  884.0 12.1 %collective-permute-start.39 = (bf16[1024,1664]{0,1:T(8,128)(2,1)}, bf16[1024,1664]{0,1:T(8,128)(2,1)S(1)}, u32[]{:S(2)}, u32[]{:S(2)}) collective-permute-start(bf16[1024,1664]{0,1:T(8,128)(2,1)} %fusion.13), channel_id=1, source_target_pairs={{0,16},{16,0},{1,17},{17,1},{2,18},{18,2},{3,19},{19,3},{4,20},{20... | collective-permute-start | bytes 10223624 | tf_op jit(solution)/shard_map/ppermute | solution.py:121
  892.6 14.5 %collective-permute-start.12 = (bf16[128,2048]{1,0:T(8,128)(2,1)}, bf16[128,2048]{1,0:T(8,128)(2,1)}, u32[]{:S(2)}, u32[]{:S(2)}) collective-permute-start(bf16[128,2048]{1,0:T(8,128)(2,1)} %dynamic-slice_convert_fusion.11), channel_id=1, source_target_pairs={{0,2},{1,3},{2,0},{3,1},{4,6},{5,7},{6,4},{7,5},{8,10},{9,11},{10,... | collective-permute-start | bytes 1572872 | tf_op jit(solution)/shard_map/ppermute | solution.py:99
  894.1 16.7 %collective-permute-start.8 = (bf16[128,2048]{1,0:T(8,128)(2,1)}, bf16[128,2048]{1,0:T(8,128)(2,1)}, u32[]{:S(2)}, u32[]{:S(2)}) collective-permute-start(bf16[128,2048]{1,0:T(8,128)(2,1)} %dynamic-slice_convert_fusion.12), channel_id=1, source_target_pairs={{0,1},{1,0},{2,3},{3,2},{4,5},{5,4},{6,7},{7,6},{8,9},{9,8},{10,11... | collective-permute-start | bytes 1572872 | tf_op jit(solution)/shard_map/ppermute | solution.py:99
  908.7 8.1 collective-permute-start.13
  912.3 7.5 collective-permute-start.9
  916.9 7.3 collective-permute-start.14
  920.0 8.3 collective-permute-start.10
  924.3 13.7 %collective-permute-start.15 = (bf16[128,2048]{1,0:T(8,128)(2,1)S(1)}, bf16[128,2048]{1,0:T(8,128)(2,1)S(1)}, u32[]{:S(2)}, u32[]{:S(2)}) collective-permute-start(bf16[128,2048]{1,0:T(8,128)(2,1)S(1)} %pad_maximum_fusion.15), channel_id=1, source_target_pairs={{0,2},{1,3},{2,0},{3,1},{4,6},{5,7},{6,4},{7,5},{8,10},{9,11},{10,... | collective-permute-start | bytes 1572872 | tf_op jit(solution)/shard_map/ppermute | solution.py:112
  928.3 10.2 %collective-permute-start.11 = (bf16[128,2048]{1,0:T(8,128)(2,1)S(1)}, bf16[128,2048]{1,0:T(8,128)(2,1)S(1)}, u32[]{:S(2)}, u32[]{:S(2)}) collective-permute-start(bf16[128,2048]{1,0:T(8,128)(2,1)S(1)} %pad_maximum_fusion.14), channel_id=1, source_target_pairs={{0,1},{1,0},{2,3},{3,2},{4,5},{5,4},{6,7},{7,6},{8,9},{9,8},{10,11... | collective-permute-start | bytes 1572872 | tf_op jit(solution)/shard_map/ppermute | solution.py:111
  (132 other events, 969.4 us)
Sparse Core Ops, SparseCore 0:
  10.2 67.9 all-gather.10
  79.7 37.2 all-gather.12
  119.3 56.3 all-gather.18
  177.7 45.7 all-gather.24
  225.5 54.2 all-gather.16
  281.2 46.0 all-gather.14
  328.9 45.6 all-gather.22
  376.2 45.6 all-gather.20
  451.6 42.4 reduce-scatter.12
  496.2 42.8 reduce-scatter.10
  541.9 51.2 reduce-scatter.8
  595.3 44.6 reduce-scatter.18
  642.9 42.8 reduce-scatter.16
  688.5 42.8 reduce-scatter.14
  754.6 47.3 reduce-scatter.20
  902.5 62.1 reduce-scatter.22

commit v5 on v4

--- a/solution.py
+++ b/solution.py
@@ -222,7 +222,7 @@
         self.log_total = peak + jnp.log(total)
         return self.attended
 
-    def backward(self, grad_heads, early, late):
+    def backward(self, grad_heads, early):
         bf16 = jnp.bfloat16
         query, segment, position = self.query, self.segment, self.position
         rows, heads = query.shape[0], query.shape[1]
@@ -251,7 +251,7 @@
         grad_qin = rotate_back(grad_query, self.cosine, self.sine).astype(bf16)
         grad_kin = rotate_back(grad_key.reshape(rows, heads, HD), self.cosine, self.sine).astype(bf16)
         grad_vin = grad_value.astype(bf16).reshape(rows, heads, HD)
-        return grad_qin, grad_kin, grad_vin, early, late
+        return grad_qin, grad_kin, grad_vin, early
 
 
 class HeadAttention:
@@ -318,7 +318,7 @@
         back = lax.all_to_all(back, "context", 0, 1, tiled=True)
         return back.reshape(self.rows, self.heads, HD)
 
-    def backward(self, grad_heads, early, late):
+    def backward(self, grad_heads, early):
         f32 = jnp.float32
         bf16 = jnp.bfloat16
         scale = 1.0 / math.sqrt(HD)
@@ -353,12 +353,12 @@
         grad_qin = rotate_back(grad_query, self.cos_all, self.sin_all).astype(bf16)
         grad_kin = rotate_back(grad_key, self.cos_all, self.sin_all).astype(bf16)
         grad_vin = grad_value.astype(bf16)
-        stacked = jnp.stack([grad_qin, grad_kin, grad_vin], axis=1)
-        stacked, late = lax.optimization_barrier((stacked, late))
-        stacked = stacked.reshape(self.rows * self.ways, 3, 1, self.group, HD)
-        stacked = lax.all_to_all(stacked, "context", 0, 2, tiled=True)
-        stacked = stacked.reshape(self.rows, 3, self.heads, HD)
-        return stacked[:, 0], stacked[:, 1], stacked[:, 2], early, late
+        returned = []
+        for grad_in in (grad_qin, grad_kin, grad_vin):
+            grad_in = grad_in.reshape(self.rows * self.ways, 1, self.group, HD)
+            grad_in = lax.all_to_all(grad_in, "context", 0, 1, tiled=True)
+            returned.append(grad_in.reshape(self.rows, self.heads, HD))
+        return returned[0], returned[1], returned[2], early
 
 
 def mlp_chunks(hidden_cols):
@@ -431,6 +431,8 @@
     h2_grad_partial = None
     staged = []
     for full_gate, full_up, full_down in fetched:
+        if staged:
+            full_gate, staged[-1] = lax.optimization_barrier((full_gate, staged[-1]))
         gate = jnp.dot(h2_part, full_gate, preferred_element_type=f32)
         up = jnp.dot(h2_part, full_up, preferred_element_type=f32)
         active = jax.nn.silu(gate)
@@ -447,8 +449,6 @@
             contract_first(h2_part, grad_up),
             contract_first(grad_y, hidden),
         )
-        if staged:
-            back_part, staged[-1] = lax.optimization_barrier((back_part, staged[-1]))
         h2_grad_partial = back_part if h2_grad_partial is None else h2_grad_partial + back_part
         staged.append(tuple(chip_total(value) for value in pending))
     grad_h2 = tensor_total(h2_grad_partial)
@@ -467,23 +467,23 @@
         (grad_heads, contract_first(grad_resid_part, attended_flat))
     )
     early = (chip_total(partial_o), reduced[:-1])
-    grad_qin, grad_kin, grad_vin, early, late = attention.backward(grad_heads, early, reduced[-1])
+    grad_qin, grad_kin, grad_vin, early = attention.backward(grad_heads, early)
     staged_o, reduced[:-1] = early
-    reduced[-1] = late
     reduced_o = line_total(staged_o)
     grad_qkv = jnp.concatenate(
         [grad_qin.reshape(rows, cols), grad_kin.reshape(rows, cols), grad_vin.reshape(rows, cols)],
         axis=1,
     )
-    grad_h1 = tensor_total(contract_last(grad_qkv, full_qkv))
-    grad_h1, reduced_o = lax.optimization_barrier((grad_h1, reduced_o))
+    h1_grad_partial, staged_qkv = lax.optimization_barrier(
+        (contract_last(grad_qkv, full_qkv), chip_total(contract_first(h1, grad_qkv)))
+    )
+    grad_h1 = tensor_total(h1_grad_partial)
+    grad_h1, reduced_o, reduced[-1] = lax.optimization_barrier((grad_h1, reduced_o, reduced[-1]))
     grad_gattn = jnp.sum(grad_h1 * norm1, axis=0)
     grad_x_part = (grad_resid + norm_back(grad_h1, norm1, inv1, gain_attn)).astype(bf16)
     gain_slab = jnp.pad(jnp.stack([grad_gattn, grad_gmlp], axis=1), ((0, 0), (0, 126)))
-    reduced_qkv = rows_total(
-        jnp.concatenate([contract_first(h1, grad_qkv), gain_slab], axis=1)
-    )
-    reduced_gains = reduced_qkv[:, 3 * cols :]
+    reduced_qkv = line_total(staged_qkv)
+    reduced_gains = rows_total(gain_slab)
     reduced_gate, reduced_up, reduced_down = (
         jnp.concatenate([chunk[which] for chunk in reduced], axis=1) for which in range(3)
     )
@@ -492,7 +492,7 @@
         grad_x_part.reshape(1, rows, width),
         reduced_qkv[:, :cols],
         reduced_qkv[:, cols : 2 * cols],
-        reduced_qkv[:, 2 * cols : 3 * cols],
+        reduced_qkv[:, 2 * cols :],
         reduced_o,
         reduced_gate,
         reduced_up,

time: 984 us -> 908 us (0.923)
  waiting for transfers between devices: 420 us -> 296 us
  local copies, waits for them, and re-layouts: 124 us -> 148 us
  starting transfers between devices: 63.5 us -> 79.4 us
    reduce_scatter x8 -> x9, waiting for transfers between devices: 81.1 us -> 21.9 us  [line_total(): lax.psum_scatter(staged.astype(jnp.bfloat16), 'context', scatter_dimensio...]
    all_to_all x1 -> x3, waiting for transfers between devices: 53.1 us -> 14.6 us  [backward(): grad_in = lax.all_to_all(grad_in, 'context', 0, 1, tiled=True)]
    all_gather x6, waiting for transfers between devices: 57.5 us -> 38.6 us  [on_device(): lax.all_gather(weight[:, part], ROWS, axis=0, tiled=True)]
    dot_general x4, matrix products: 13.5 us -> 27.8 us  [backward(): jnp.einsum('hqk,qhd->khd', probs.astype(bf16), grad_block, preferred_elem...]
    unnamed x282 -> x273, local copies, waits for them, and re-layouts: 44.7 us -> 53.8 us
    add x7 -> x8, other arithmetic: 31.8 us -> 37 us  [chip_total(): return mine.astype(f32) + got.astype(f32)]
  transfers between devices with their start and end apart: 61 -> 65, of which waited for: 37 -> 31; matrix products, arithmetic and copies ran while one was open for 40% -> 50% of each run, Pallas kernels for 0% -> 0%
where the time goes in v5:
time: 908 us; the launch traced here: 901 us
  waiting for transfers between devices  296 us (33%)
  matrix products  193 us (21%)
  local copies, waits for them, and re-layouts  148 us (16%)
  other arithmetic  143 us (16%)
  starting transfers between devices  79.4 us (9%)
  blocking collectives  24.1 us (3%)
  between operations  16.5 us (2%)
    all_to_all x1, waiting for transfers between devices, __init__(): stacked = lax.all_to_all(stacked, 'context', 2, 0, tiled=True)  54.4 us
    unnamed x273, local copies, waits for them, and re-layouts  53.8 us
    ppermute x16, waiting for transfers between devices, swap(): return lax.ppermute(value.astype(bf16), 'tensor', pairs).astype(f32)  44.7 us
    all_gather x6, waiting for transfers between devices, on_device(): lax.all_gather(weight[:, part], ROWS, axis=0, tiled=True)  38.6 us
    add x8, other arithmetic, chip_total(): return mine.astype(f32) + got.astype(f32)  37 us
    dot_general x8, matrix products, contract_last(): lax.dot_general(left, right, (((1,), (1,)), ((), ())), preferred_element_...  31.7 us
    all_gather x1, waiting for transfers between devices, on_device(): lax.all_gather(jnp.concatenate([w_q, w_k, w_v], axis=1), ROWS, axis=0, ti...  29.5 us
    dot_general x4, matrix products, backward(): jnp.einsum('hqk,qhd->khd', probs.astype(bf16), grad_block, preferred_elem...  27.8 us
  transfers between devices with their start and end apart: 65, of which 31 were waited for; matrix products, arithmetic and copies ran while one was open for 50% of the time, Pallas kernels for 0%

profile of v5, /device:TPU:0, one launch (start us, length us, event | category | flops | bytes accessed | tf_op | source)
XLA Modules:
  0.0 900.5 jit_solution(3794873238333863146)
XLA Ops:
  17.3 6.3 all-to-all-start.1
  23.7 24.1 %all-gather.1 = bf16[8,1,512]{2,1,0:T(2,128)(2,1)S(1)} all-gather(bf16[1,1,512]{2,1,0:T(2,128)(2,1)S(1)} %reshape.803), channel_id=2, replica_groups=mesh['shard'=2,'context'=4,'tensor'=4] {'shard','context'}, dimensions={0}, use_global_device_ids=true | all-gather | bytes 9216 | tf_op jit(solution)/shard_map/all_gather | solution.py:385
  48.7 29.5 %all-gather.11.cloned.1.call-done = bf16[2048,1536]{1,0:T(8,128)(2,1)} async-done(((bf16[256,1536]{1,0:T(8,128)(2,1)}), bf16[2048,1536]{1,0:T(8,128)(2,1)}) %all-gather.11.cloned.1.call-update) | async-done | bytes 6291472 | tf_op jit(solution)/shard_map/all_gather | solution.py:383
  78.1 5.6 fusion.130
  96.4 4.3 all-to-all-start
  102.1 4.5 compare_and_fusion.3
  106.6 54.4 %all-to-all-done = bf16[512,3,4,2,64]{0,4,3,1,2:T(8,128)(2,1)} async-done(((bf16[512,3,4,2,64]{0,4,3,1,2:T(8,128)(2,1)}), bf16[512,3,4,2,64]{0,4,3,1,2:T(8,128)(2,1)}, u32[]{:S(2)}, u32[]{:S(2)}) %all-to-all-start) | async-done | bytes 1572896 | tf_op jit(solution)/shard_map/all_to_all | solution.py:269
  168.6 6.8 fusion.19
  175.4 5.1 fusion.20
  184.6 13.3 %fusion = (f32[2,512]{1,0:T(2,128)S(1)}, f32[2,512]{1,0:T(2,128)S(1)}) fusion(f32[2,512,2048]{2,1,0:T(8,128)} %get-tuple-element.205, f32[2,512]{1,0:T(2,128)S(1)} %get-tuple-element.204, pred[512,2048]{1,0:T(8,128)(4,1)S(1)} %copy-done.42, f32[2,512]{1,0:T(2,128)S(1)} %get-tuple-element.198, f32[2,512,2048]{2,1,0:T(8,128)} %get-tuple-element.199, ...), kind=kLoop, calls=%fused_computation.16 | loop fusion | flops 20969472 | bytes 18890752 | tf_op jit(solution)/shard_map/reduce_sum | solution.py:306
  198.0 5.2 fusion.114
  203.3 5.3 fusion.120
  208.5 5.7 fusion.4
  225.3 4.1 all-to-all-start.2
  229.5 26.8 %all-to-all-done.2 = bf16[4,2,32768]{2,1,0:T(2,128)(2,1)} async-done(((bf16[4,2,32768]{2,1,0:T(2,128)(2,1)}), bf16[4,2,32768]{2,1,0:T(2,128)(2,1)}, u32[]{:S(2)}, u32[]{:S(2)}) %all-to-all-start.2) | async-done | bytes 524320 | tf_op jit(solution)/shard_map/all_to_all | solution.py:318
  273.6 5.9 collective-permute-done.4
  303.2 6.6 fusion.83
  313.6 4.7 multiply_convert_fusion.4
  318.3 6.5 fusion.198
  324.8 7.4 multiply_convert_fusion.8
  352.4 5.5 bitcast_add_fusion.1
  357.9 5.0 convert_add_fusion.5
  362.8 5.0 convert_add_fusion.4
  367.9 6.7 all-gather.25.cloned.1.call-done
  374.6 6.6 fusion.79
  381.2 4.4 fusion.204
  385.7 4.4 fusion.203
  390.0 31.9 %all-gather.23.cloned.1.call-done = bf16[2048,1024]{1,0:T(8,128)(2,1)} async-done(((bf16[256,1024]{1,0:T(8,128)(2,1)}), bf16[2048,1024]{1,0:T(8,128)(2,1)}) %all-gather.23.cloned.1.call-update) | async-done | bytes 4194320 | tf_op jit(solution)/shard_map/all_gather | solution.py:397
  421.9 6.5 fusion.202
  428.6 8.5 multiply_convert_fusion.6
  474.2 5.5 collective-permute-done.24
  482.3 5.0 collective-permute-done.25
  491.8 8.3 collective-permute-done.26
  507.8 4.9 convert_add_fusion.2
  512.8 4.9 bitcast_add_fusion
  522.9 4.1 multiply_add_fusion
  535.2 4.1 all-to-all-start.3
  541.5 25.9 %all-to-all-done.3 = bf16[512,4,2,64]{0,3,2,1:T(8,128)(2,1)} async-done(((bf16[512,4,2,64]{0,3,2,1:T(8,128)(2,1)}), bf16[512,4,2,64]{0,3,2,1:T(8,128)(2,1)}, u32[]{:S(2)}, u32[]{:S(2)}) %all-to-all-start.3) | async-done | bytes 524320 | tf_op jit(solution)/shard_map/all_to_all | solution.py:326
  580.3 6.6 multiply_convert_fusion.3
  590.3 7.3 fusion.37
  597.5 5.2 multiply_convert_fusion.2
  602.8 5.5 fusion.59
  608.3 5.6 multiply_convert_fusion
  615.4 4.8 multiply_convert_fusion.1
  633.7 4.1 all-to-all-start.4
  645.8 7.6 fusion.62
  653.4 13.1 %all-to-all-done.4 = bf16[4,2,32768]{2,1,0:T(2,128)(2,1)} async-done(((bf16[4,2,32768]{2,1,0:T(2,128)(2,1)}), bf16[4,2,32768]{2,1,0:T(2,128)(2,1)}, u32[]{:S(2)}, u32[]{:S(2)}) %all-to-all-start.4) | async-done | bytes 524320 | tf_op jit(solution)/shard_map/all_to_all | solution.py:359
  666.5 4.1 all-to-all-start.5
  670.6 7.4 fusion.71
  685.7 4.1 all-to-all-start.6
  714.5 4.9 fusion.127
  719.4 4.5 copy-done.17
  726.2 5.0 fusion.199
  731.3 4.6 convolution_add_fusion
  735.9 5.3 fusion.128
  741.3 4.7 convert_add_fusion
  745.9 4.1 fusion.184
  758.7 8.2 collective-permute-done.36
  772.7 4.2 collective-permute-done.37
  780.3 4.4 collective-permute-done.38
  814.4 9.3 %collective-permute-done.11 = bf16[128,2048]{1,0:T(8,128)(2,1)} collective-permute-done((bf16[128,2048]{1,0:T(8,128)(2,1)}, bf16[128,2048]{1,0:T(8,128)(2,1)}, u32[]{:S(2)}, u32[]{:S(2)}) %collective-permute-start.11) | collective-permute-done | bytes 524320 | tf_op jit(solution)/shard_map/ppermute | solution.py:99
  833.9 3.9 collective-permute-done.17
  840.8 9.7 %collective-permute-done.18 = bf16[128,2048]{1,0:T(8,128)(2,1)S(1)} collective-permute-done((bf16[128,2048]{1,0:T(8,128)(2,1)S(1)}, bf16[128,2048]{1,0:T(8,128)(2,1)S(1)}, u32[]{:S(2)}, u32[]{:S(2)}) %collective-permute-start.18) | collective-permute-done | bytes 524320 | tf_op jit(solution)/shard_map/ppermute | solution.py:112
  869.5 21.9 %reduce-scatter.24.cloned.1.call-done = bf16[256,1536]{1,0:T(8,128)(2,1)} async-done(((bf16[1024,1536]{1,0:T(8,128)(2,1)}), bf16[256,1536]{1,0:T(8,128)(2,1)}) %reduce-scatter.24.cloned.1.call-update) | async-done | bytes 786448 | tf_op jit(solution)/shard_map/reduce_scatter | solution.py:126
  (569 shorter events, 334.5 us)
Async XLA Ops:
  7.2 71.0 %all-gather.11.cloned.1.call-start = ((), (), s32[]{:S(2)}) async-start(), calls=%async_computation.16 | async-start | bytes 7077888 | tf_op jit(solution)/shard_map/all_gather | solution.py:383
  9.4 251.7 %all-gather.13.cloned.1.call-start = ((), (), s32[]{:S(2)}) async-start(), calls=%async_computation.17 | async-start | bytes 2359296 | tf_op jit(solution)/shard_map/all_gather | solution.py:384
  10.2 293.0 %all-gather.19.cloned.1.call-start = ((), (), s32[]{:S(2)}) async-start(), calls=%async_computation.20 | async-start | bytes 4718592 | tf_op jit(solution)/shard_map/all_gather | solution.py:397
  12.6 305.6 %all-gather.17.cloned.1.call-start = ((), (), s32[]{:S(2)}) async-start(), calls=%async_computation.19 | async-start | bytes 4718592 | tf_op jit(solution)/shard_map/all_gather | solution.py:397
  13.8 311.0 %all-gather.15.cloned.1.call-start = ((), (), s32[]{:S(2)}) async-start(), calls=%async_computation.18 | async-start | bytes 4718592 | tf_op jit(solution)/shard_map/all_gather | solution.py:397
  16.1 351.7 %all-gather.21.cloned.1.call-start = ((), (), s32[]{:S(2)}) async-start(), calls=%async_computation.21 | async-start | bytes 4718592 | tf_op jit(solution)/shard_map/all_gather | solution.py:397
  17.3 79.1 %all-to-all-start.1 = ((s32[4,2,512]{2,1,0:T(2,128)}), s32[4,2,512]{2,1,0:T(2,128)S(1)}, u32[]{:S(2)}, u32[]{:S(2)}) async-start(s32[4,2,512]{2,1,0:T(2,128)} %broadcast_in_dim.158), calls=%async_computation.1 | async-start | bytes 32768 | tf_op jit(solution)/shard_map/all_to_all | solution.py:276
  96.4 64.7 %all-to-all-start = ((bf16[512,3,4,2,64]{0,4,3,1,2:T(8,128)(2,1)}), bf16[512,3,4,2,64]{0,4,3,1,2:T(8,128)(2,1)}, u32[]{:S(2)}, u32[]{:S(2)}) async-start(bf16[512,3,4,2,64]{0,4,3,1,2:T(8,128)(2,1)} %copy.50), calls=%async_computation | async-start | bytes 3145728 | tf_op jit(solution)/shard_map/all_to_all | solution.py:269
  100.7 273.9 %all-gather.25.cloned.1.call-start = ((), (), s32[]{:S(2)}) async-start(), calls=%async_computation.23 | async-start | bytes 4718592 | tf_op jit(solution)/shard_map/all_gather | solution.py:397
  225.3 31.0 %all-to-all-start.2 = ((bf16[4,2,32768]{2,1,0:T(2,128)(2,1)}), bf16[4,2,32768]{2,1,0:T(2,128)(2,1)}, u32[]{:S(2)}, u32[]{:S(2)}) async-start(bf16[4,2,32768]{2,1,0:T(2,128)(2,1)} %reshape.806), calls=%async_computation.2 | async-start | bytes 1048576 | tf_op jit(solution)/shard_map/all_to_all | solution.py:318
  229.4 192.5 %all-gather.23.cloned.1.call-start = ((), (), s32[]{:S(2)}) async-start(), calls=%async_computation.22 | async-start | bytes 4718592 | tf_op jit(solution)/shard_map/all_gather | solution.py:397
  267.3 12.2 %collective-permute-start.4 = (bf16[128,2048]{1,0:T(8,128)(2,1)S(1)}, bf16[128,2048]{1,0:T(8,128)(2,1)}, u32[]{:S(2)}, u32[]{:S(2)}) collective-permute-start(bf16[128,2048]{1,0:T(8,128)(2,1)S(1)} %dynamic-slice_convert_fusion.14), channel_id=1, source_target_pairs={{0,2},{1,3},{2,0},{3,1},{4,6},{5,7},{6,4},{7,5},{8,10},{9,11},{10,... | collective-permute-start | bytes 1572872 | tf_op jit(solution)/shard_map/ppermute | solution.py:99
  270.4 302.1 %reduce-scatter.14.cloned.1.call-start = ((), (), s32[]{:S(2)}) async-start(), calls=%async_computation.26 | async-start | bytes 2621440 | tf_op jit(solution)/shard_map/reduce_scatter | solution.py:126
  272.0 11.9 %collective-permute-start = (bf16[128,2048]{1,0:T(8,128)(2,1)S(1)}, bf16[128,2048]{1,0:T(8,128)(2,1)S(1)}, u32[]{:S(2)}, u32[]{:S(2)}) collective-permute-start(bf16[128,2048]{1,0:T(8,128)(2,1)S(1)} %dynamic-slice_convert_fusion.15), channel_id=1, source_target_pairs={{0,1},{1,0},{2,3},{3,2},{4,5},{5,4},{6,7},{7,6},{8,9},{9,8},{10,11... | collective-permute-start | bytes 1572872 | tf_op jit(solution)/shard_map/ppermute | solution.py:99
  281.1 7.1 collective-permute-start.5
  284.1 7.6 collective-permute-start.1
  288.2 9.2 %collective-permute-start.6 = (bf16[64,2048]{1,0:T(8,128)(2,1)S(1)}, bf16[64,2048]{1,0:T(8,128)(2,1)S(1)}, u32[]{:S(2)}, u32[]{:S(2)}) collective-permute-start(bf16[64,2048]{1,0:T(8,128)(2,1)S(1)} %add_convert_fusion.9), channel_id=1, source_target_pairs={{0,1},{1,0},{2,3},{3,2},{4,5},{5,4},{6,7},{7,6},{8,9},{9,8},{10,11... | collective-permute-start | bytes 786440 | tf_op jit(solution)/shard_map/ppermute | solution.py:110
  291.8 8.5 collective-permute-start.2
  298.4 11.4 %collective-permute-start.7 = (bf16[128,2048]{1,0:T(8,128)(2,1)}, bf16[128,2048]{1,0:T(8,128)(2,1)}, u32[]{:S(2)}, u32[]{:S(2)}) collective-permute-start(bf16[128,2048]{1,0:T(8,128)(2,1)} %pad_maximum_fusion.12), channel_id=1, source_target_pairs={{0,2},{1,3},{2,0},{3,1},{4,6},{5,7},{6,4},{7,5},{8,10},{9,11},{10,... | collective-permute-start | bytes 1572872 | tf_op jit(solution)/shard_map/ppermute | solution.py:112
  301.3 9.8 %collective-permute-start.3 = (bf16[128,2048]{1,0:T(8,128)(2,1)}, bf16[128,2048]{1,0:T(8,128)(2,1)}, u32[]{:S(2)}, u32[]{:S(2)}) collective-permute-start(bf16[128,2048]{1,0:T(8,128)(2,1)} %pad_maximum_fusion.11), channel_id=1, source_target_pairs={{0,1},{1,0},{2,3},{3,2},{4,5},{5,4},{6,7},{7,6},{8,9},{9,8},{10,11... | collective-permute-start | bytes 1572872 | tf_op jit(solution)/shard_map/ppermute | solution.py:111
  336.3 16.1 %collective-permute-start.10 = (bf16[1024,1024]{0,1:T(8,128)(2,1)}, bf16[1024,1024]{0,1:T(8,128)(2,1)}, u32[]{:S(2)}, u32[]{:S(2)}) collective-permute-start(bf16[1024,1024]{0,1:T(8,128)(2,1)} %fusion.74), channel_id=1, source_target_pairs={{0,16},{16,0},{1,17},{17,1},{2,18},{18,2},{3,19},{19,3},{4,20},{20... | collective-permute-start | bytes 6291464 | tf_op jit(solution)/shard_map/ppermute | solution.py:121
  343.2 14.7 %collective-permute-start.8 = (bf16[1024,1024]{1,0:T(8,128)(2,1)}, bf16[1024,1024]{1,0:T(8,128)(2,1)}, u32[]{:S(2)}, u32[]{:S(2)}) collective-permute-start(bf16[1024,1024]{1,0:T(8,128)(2,1)} %dynamic-slice_convert_fusion.6), channel_id=1, source_target_pairs={{0,16},{16,0},{1,17},{17,1},{2,18},{18,2},{3,19},{19,3},{4,20},{20... | collective-permute-start | bytes 6291464 | tf_op jit(solution)/shard_map/ppermute | solution.py:121
  352.4 10.4 %collective-permute-start.9 = (bf16[1024,1024]{1,0:T(8,128)(2,1)}, bf16[1024,1024]{1,0:T(8,128)(2,1)}, u32[]{:S(2)}, u32[]{:S(2)}) collective-permute-start(bf16[1024,1024]{1,0:T(8,128)(2,1)} %dynamic-slice_convert_fusion.5), channel_id=1, source_target_pairs={{0,16},{16,0},{1,17},{17,1},{2,18},{18,2},{3,19},{19,3},{4,20},{20... | collective-permute-start | bytes 6291464 | tf_op jit(solution)/shard_map/ppermute | solution.py:121
  367.8 206.9 %reduce-scatter.12.cloned.1.call-start = ((), (), s32[]{:S(2)}) async-start(), calls=%async_computation.25 | async-start | bytes 2621440 | tf_op jit(solution)/shard_map/reduce_scatter | solution.py:126
  428.4 148.5 %reduce-scatter.10.cloned.1.call-start = ((), (), s32[]{:S(2)}) async-start(), calls=%async_computation.24 | async-start | bytes 2621440 | tf_op jit(solution)/shard_map/reduce_scatter | solution.py:126
  446.2 23.7 %collective-permute-start.23 = (bf16[128,2048]{1,0:T(8,128)(2,1)}, bf16[128,2048]{1,0:T(8,128)(2,1)}, u32[]{:S(2)}, u32[]{:S(2)}) collective-permute-start(bf16[128,2048]{1,0:T(8,128)(2,1)} %dynamic-slice_convert_fusion.10), channel_id=1, source_target_pairs={{0,2},{1,3},{2,0},{3,1},{4,6},{5,7},{6,4},{7,5},{8,10},{9,11},{10,... | collective-permute-start | bytes 1572872 | tf_op jit(solution)/shard_map/ppermute | solution.py:99
  448.7 23.4 %collective-permute-start.19 = (bf16[128,2048]{1,0:T(8,128)(2,1)}, bf16[128,2048]{1,0:T(8,128)(2,1)}, u32[]{:S(2)}, u32[]{:S(2)}) collective-permute-start(bf16[128,2048]{1,0:T(8,128)(2,1)} %dynamic-slice_convert_fusion.11), channel_id=1, source_target_pairs={{0,1},{1,0},{2,3},{3,2},{4,5},{5,4},{6,7},{7,6},{8,9},{9,8},{10,11... | collective-permute-start | bytes 1572872 | tf_op jit(solution)/shard_map/ppermute | solution.py:99
  456.4 47.6 %collective-permute-start.27 = (bf16[1024,1024]{1,0:T(8,128)(2,1)}, bf16[1024,1024]{1,0:T(8,128)(2,1)}, u32[]{:S(2)}, u32[]{:S(2)}) collective-permute-start(bf16[1024,1024]{1,0:T(8,128)(2,1)} %dynamic-slice_convert_fusion.3), channel_id=1, source_target_pairs={{0,16},{16,0},{1,17},{17,1},{2,18},{18,2},{3,19},{19,3},{4,20},{20... | collective-permute-start | bytes 6291464 | tf_op jit(solution)/shard_map/ppermute | solution.py:121
  460.9 46.9 %collective-permute-start.28 = (bf16[1024,1024]{1,0:T(8,128)(2,1)}, bf16[1024,1024]{1,0:T(8,128)(2,1)}, u32[]{:S(2)}, u32[]{:S(2)}) collective-permute-start(bf16[1024,1024]{1,0:T(8,128)(2,1)} %dynamic-slice_convert_fusion.2), channel_id=1, source_target_pairs={{0,16},{16,0},{1,17},{17,1},{2,18},{18,2},{3,19},{19,3},{4,20},{20... | collective-permute-start | bytes 6291464 | tf_op jit(solution)/shard_map/ppermute | solution.py:121
  469.3 43.5 %collective-permute-start.29 = (bf16[1024,1024]{0,1:T(8,128)(2,1)}, bf16[1024,1024]{0,1:T(8,128)(2,1)}, u32[]{:S(2)}, u32[]{:S(2)}) collective-permute-start(bf16[1024,1024]{0,1:T(8,128)(2,1)} %fusion.75), channel_id=1, source_target_pairs={{0,16},{16,0},{1,17},{17,1},{2,18},{18,2},{3,19},{19,3},{4,20},{20... | collective-permute-start | bytes 6291464 | tf_op jit(solution)/shard_map/ppermute | solution.py:121
  469.8 323.8 %reduce-scatter.22.cloned.1.call-start = ((), (), s32[]{:S(2)}) async-start(), calls=%async_computation.30 | async-start | bytes 2621440 | tf_op jit(solution)/shard_map/reduce_scatter | solution.py:126
  471.4 8.3 collective-permute-start.24
  473.6 8.0 collective-permute-start.20
  479.7 7.6 collective-permute-start.25
  481.6 7.6 collective-permute-start.21
  487.4 12.7 %collective-permute-start.26 = (bf16[128,2048]{1,0:T(8,128)(2,1)S(1)}, bf16[128,2048]{1,0:T(8,128)(2,1)S(1)}, u32[]{:S(2)}, u32[]{:S(2)}) collective-permute-start(bf16[128,2048]{1,0:T(8,128)(2,1)S(1)} %pad_maximum_fusion.16), channel_id=1, source_target_pairs={{0,2},{1,3},{2,0},{3,1},{4,6},{5,7},{6,4},{7,5},{8,10},{9,11},{10,... | collective-permute-start | bytes 1572872 | tf_op jit(solution)/shard_map/ppermute | solution.py:112
  489.3 11.8 %collective-permute-start.22 = (bf16[128,2048]{1,0:T(8,128)(2,1)S(1)}, bf16[128,2048]{1,0:T(8,128)(2,1)S(1)}, u32[]{:S(2)}, u32[]{:S(2)}) collective-permute-start(bf16[128,2048]{1,0:T(8,128)(2,1)S(1)} %pad_maximum_fusion.15), channel_id=1, source_target_pairs={{0,1},{1,0},{2,3},{3,2},{4,5},{5,4},{6,7},{7,6},{8,9},{9,8},{10,11... | collective-permute-start | bytes 1572872 | tf_op jit(solution)/shard_map/ppermute | solution.py:111
  533.4 35.8 %collective-permute-start.30 = (bf16[1024,512]{1,0:T(8,128)(2,1)}, bf16[1024,512]{1,0:T(8,128)(2,1)}, u32[]{:S(2)}, u32[]{:S(2)}) collective-permute-start(bf16[1024,512]{1,0:T(8,128)(2,1)} %dynamic-slice_convert_fusion.7), channel_id=1, source_target_pairs={{0,16},{16,0},{1,17},{17,1},{2,18},{18,2},{3,19},{19,3},{4,20},{20... | collective-permute-start | bytes 3145736 | tf_op jit(solution)/shard_map/ppermute | solution.py:121
  535.2 32.1 %all-to-all-start.3 = ((bf16[512,4,2,64]{0,3,2,1:T(8,128)(2,1)}), bf16[512,4,2,64]{0,3,2,1:T(8,128)(2,1)}, u32[]{:S(2)}, u32[]{:S(2)}) async-start(bf16[512,4,2,64]{0,3,2,1:T(8,128)(2,1)} %bitcast.354), calls=%async_computation.3 | async-start | bytes 1048576 | tf_op jit(solution)/shard_map/all_to_all | solution.py:326
  539.4 256.3 %reduce-scatter.20.cloned.1.call-start = ((), (), s32[]{:S(2)}) async-start(), calls=%async_computation.29 | async-start | bytes 2621440 | tf_op jit(solution)/shard_map/reduce_scatter | solution.py:126
  633.7 32.8 %all-to-all-start.4 = ((bf16[4,2,32768]{2,1,0:T(2,128)(2,1)}), bf16[4,2,32768]{2,1,0:T(2,128)(2,1)}, u32[]{:S(2)}, u32[]{:S(2)}) async-start(bf16[4,2,32768]{2,1,0:T(2,128)(2,1)} %reshape.812), calls=%async_computation.7 | async-start | bytes 1048576 | tf_op jit(solution)/shard_map/all_to_all | solution.py:359
  666.5 19.2 %all-to-all-start.5 = ((bf16[4,2,32768]{2,1,0:T(2,128)(2,1)}), bf16[4,2,32768]{2,1,0:T(2,128)(2,1)}, u32[]{:S(2)}, u32[]{:S(2)}) async-start(bf16[4,2,32768]{2,1,0:T(2,128)(2,1)} %reshape.810), calls=%async_computation.8 | async-start | bytes 1048576 | tf_op jit(solution)/shard_map/all_to_all | solution.py:359
  685.7 20.6 %all-to-all-start.6 = ((bf16[4,2,32768]{2,1,0:T(2,128)(2,1)}), bf16[4,2,32768]{2,1,0:T(2,128)(2,1)}, u32[]{:S(2)}, u32[]{:S(2)}) async-start(bf16[4,2,32768]{2,1,0:T(2,128)(2,1)} %reshape.808), calls=%async_computation.9 | async-start | bytes 1048576 | tf_op jit(solution)/shard_map/all_to_all | solution.py:359
  689.9 108.0 %reduce-scatter.18.cloned.1.call-start = ((), (), s32[]{:S(2)}) async-start(), calls=%async_computation.28 | async-start | bytes 2621440 | tf_op jit(solution)/shard_map/reduce_scatter | solution.py:126
  726.1 15.2 %collective-permute-start.31 = (bf16[1024,1536]{1,0:T(8,128)(2,1)}, bf16[1024,1536]{1,0:T(8,128)(2,1)}, u32[]{:S(2)}, u32[]{:S(2)}) collective-permute-start(bf16[1024,1536]{1,0:T(8,128)(2,1)} %dynamic-slice_convert_fusion), channel_id=1, source_target_pairs={{0,16},{16,0},{1,17},{17,1},{2,18},{18,2},{3,19},{19,3},{4,20},{20... | collective-permute-start | bytes 9437192 | tf_op jit(solution)/shard_map/ppermute | solution.py:121
  726.1 73.9 %reduce-scatter.16.cloned.1.call-start = ((), (), s32[]{:S(2)}) async-start(), calls=%async_computation.27 | async-start | bytes 1310720 | tf_op jit(solution)/shard_map/reduce_scatter | solution.py:126
  752.2 14.7 %collective-permute-start.36 = (bf16[128,2048]{1,0:T(8,128)(2,1)}, bf16[128,2048]{1,0:T(8,128)(2,1)}, u32[]{:S(2)}, u32[]{:S(2)}) collective-permute-start(bf16[128,2048]{1,0:T(8,128)(2,1)} %dynamic-slice_convert_fusion.8), channel_id=1, source_target_pairs={{0,2},{1,3},{2,0},{3,1},{4,6},{5,7},{6,4},{7,5},{8,10},{9,11},{10,... | collective-permute-start | bytes 1572872 | tf_op jit(solution)/shard_map/ppermute | solution.py:99
  755.7 112.5 %reduce-scatter.26.cloned.1.call-start = ((), (), s32[]{:S(2)}) async-start(), calls=%async_computation.32 | async-start | bytes 327680 | tf_op jit(solution)/shard_map/reduce_scatter | solution.py:126
  757.2 14.7 %collective-permute-start.32 = (bf16[128,2048]{1,0:T(8,128)(2,1)S(1)}, bf16[128,2048]{1,0:T(8,128)(2,1)S(1)}, u32[]{:S(2)}, u32[]{:S(2)}) collective-permute-start(bf16[128,2048]{1,0:T(8,128)(2,1)S(1)} %dynamic-slice_convert_fusion.9), channel_id=1, source_target_pairs={{0,1},{1,0},{2,3},{3,2},{4,5},{5,4},{6,7},{7,6},{8,9},{9,8},{10,11... | collective-permute-start | bytes 1572872 | tf_op jit(solution)/shard_map/ppermute | solution.py:99
  768.5 8.5 collective-permute-start.37
  772.0 7.2 collective-permute-start.33
  777.0 7.7 collective-permute-start.38
  779.3 7.7 collective-permute-start.34
  786.3 15.5 %collective-permute-start.39 = (bf16[128,2048]{1,0:T(8,128)(2,1)}, bf16[128,2048]{1,0:T(8,128)(2,1)}, u32[]{:S(2)}, u32[]{:S(2)}) collective-permute-start(bf16[128,2048]{1,0:T(8,128)(2,1)} %pad_maximum_fusion.20), channel_id=1, source_target_pairs={{0,2},{1,3},{2,0},{3,1},{4,6},{5,7},{6,4},{7,5},{8,10},{9,11},{10,... | collective-permute-start | bytes 1572872 | tf_op jit(solution)/shard_map/ppermute | solution.py:112
  788.6 14.6 %collective-permute-start.35 = (bf16[128,2048]{1,0:T(8,128)(2,1)}, bf16[128,2048]{1,0:T(8,128)(2,1)}, u32[]{:S(2)}, u32[]{:S(2)}) collective-permute-start(bf16[128,2048]{1,0:T(8,128)(2,1)} %pad_maximum_fusion.19), channel_id=1, source_target_pairs={{0,1},{1,0},{2,3},{3,2},{4,5},{5,4},{6,7},{7,6},{8,9},{9,8},{10,11... | collective-permute-start | bytes 1572872 | tf_op jit(solution)/shard_map/ppermute | solution.py:111
  792.2 18.4 %collective-permute-start.15 = (bf16[128,2048]{1,0:T(8,128)(2,1)}, bf16[128,2048]{1,0:T(8,128)(2,1)}, u32[]{:S(2)}, u32[]{:S(2)}) collective-permute-start(bf16[128,2048]{1,0:T(8,128)(2,1)} %dynamic-slice_convert_fusion.12), channel_id=1, source_target_pairs={{0,2},{1,3},{2,0},{3,1},{4,6},{5,7},{6,4},{7,5},{8,10},{9,11},{10,... | collective-permute-start | bytes 1572872 | tf_op jit(solution)/shard_map/ppermute | solution.py:99
  808.6 15.1 %collective-permute-start.11 = (bf16[128,2048]{1,0:T(8,128)(2,1)}, bf16[128,2048]{1,0:T(8,128)(2,1)}, u32[]{:S(2)}, u32[]{:S(2)}) collective-permute-start(bf16[128,2048]{1,0:T(8,128)(2,1)} %dynamic-slice_convert_fusion.13), channel_id=1, source_target_pairs={{0,1},{1,0},{2,3},{3,2},{4,5},{5,4},{6,7},{7,6},{8,9},{9,8},{10,11... | collective-permute-start | bytes 1572872 | tf_op jit(solution)/shard_map/ppermute | solution.py:99
  810.6 80.8 %reduce-scatter.24.cloned.1.call-start = ((), (), s32[]{:S(2)}) async-start(), calls=%async_computation.31 | async-start | bytes 3932160 | tf_op jit(solution)/shard_map/reduce_scatter | solution.py:126
  813.1 15.7 %collective-permute-start.16 = (bf16[64,2048]{1,0:T(8,128)(2,1)S(1)}, bf16[64,2048]{1,0:T(8,128)(2,1)}, u32[]{:S(2)}, u32[]{:S(2)}) collective-permute-start(bf16[64,2048]{1,0:T(8,128)(2,1)S(1)} %dynamic-slice_convert_fusion.21), channel_id=1, source_target_pairs={{0,1},{1,0},{2,3},{3,2},{4,5},{5,4},{6,7},{7,6},{8,9},{9,8},{10,11... | collective-permute-start | bytes 786440 | tf_op jit(solution)/shard_map/ppermute | solution.py:99
  825.3 7.3 collective-permute-start.12
  830.0 7.8 collective-permute-start.17
  832.7 6.5 collective-permute-start.13
  837.9 12.6 %collective-permute-start.18 = (bf16[128,2048]{1,0:T(8,128)(2,1)S(1)}, bf16[128,2048]{1,0:T(8,128)(2,1)S(1)}, u32[]{:S(2)}, u32[]{:S(2)}) collective-permute-start(bf16[128,2048]{1,0:T(8,128)(2,1)S(1)} %pad_maximum_fusion.14), channel_id=1, source_target_pairs={{0,2},{1,3},{2,0},{3,1},{4,6},{5,7},{6,4},{7,5},{8,10},{9,11},{10,... | collective-permute-start | bytes 1572872 | tf_op jit(solution)/shard_map/ppermute | solution.py:112
  839.2 12.3 %collective-permute-start.14 = (bf16[128,2048]{1,0:T(8,128)(2,1)S(1)}, bf16[128,2048]{1,0:T(8,128)(2,1)S(1)}, u32[]{:S(2)}, u32[]{:S(2)}) collective-permute-start(bf16[128,2048]{1,0:T(8,128)(2,1)S(1)} %pad_maximum_fusion.13), channel_id=1, source_target_pairs={{0,1},{1,0},{2,3},{3,2},{4,5},{5,4},{6,7},{7,6},{8,9},{9,8},{10,11... | collective-permute-start | bytes 1572872 | tf_op jit(solution)/shard_map/ppermute | solution.py:111
  (131 other events, 1198.5 us)
Sparse Core Ops, SparseCore 0:
  10.2 67.9 all-gather.10
  79.7 37.2 all-gather.12
  119.3 56.3 all-gather.18
  177.7 45.7 all-gather.16
  225.5 53.8 all-gather.14
  280.8 45.8 all-gather.20
  328.9 45.6 all-gather.24
  376.2 45.6 all-gather.22
  424.2 42.4 reduce-scatter.13
  468.8 42.8 reduce-scatter.11
  514.5 51.2 reduce-scatter.9
  567.9 44.6 reduce-scatter.21
  614.9 51.2 reduce-scatter.19
  726.2 44.7 reduce-scatter.17
  773.2 26.4 reduce-scatter.15
  810.7 19.8 reduce-scatter.25
  832.8 58.5 reduce-scatter.23

commit v6 on v5

--- a/solution.py
+++ b/solution.py
@@ -111,6 +111,13 @@
     first = joined(first, lax.ppermute(first, "tensor", x_pairs), x_bit)
     second = joined(second, lax.ppermute(second, "tensor", y_pairs), y_bit)
     return jnp.concatenate([first, second], axis=0).astype(f32)
+
+
+def tensor_exact_total(value):
+    if lax.axis_size("tensor") != 4:
+        return lax.psum(value, "tensor")
+    value = value + lax.ppermute(value, "tensor", [(i, i ^ 1) for i in range(4)])
+    return value + lax.ppermute(value, "tensor", [(i, i ^ 2) for i in range(4)])
 
 
 def chip_total(grad):
@@ -380,8 +387,11 @@
     tokens = inputs.reshape(rows, width)
     segment = segments.reshape(rows)
     position = positions.reshape(rows)
-    full_qkv = lax.all_gather(jnp.concatenate([w_q, w_k, w_v], axis=1), ROWS, axis=0, tiled=True)
-    full_o = lax.all_gather(w_o, ROWS, axis=0, tiled=True)
+    full_qkvo = lax.all_gather(
+        jnp.concatenate([w_q, w_k, w_v, w_o], axis=1), ROWS, axis=0, tiled=True
+    )
+    full_qkv = full_qkvo[:, : 3 * cols]
+    full_o = full_qkvo[:, 3 * cols :]
     gains = lax.all_gather(
         jnp.concatenate([g_attn, g_mlp])[None], ROWS, axis=0, tiled=True
     )
@@ -392,11 +402,11 @@
     fetched = []
     for index in range(count):
         part = slice(index * step, (index + 1) * step)
+        pair = lax.all_gather(
+            jnp.concatenate([w_gate[:, part], w_up[:, part]], axis=1), ROWS, axis=0, tiled=True
+        )
         fetched.append(
-            tuple(
-                lax.all_gather(weight[:, part], ROWS, axis=0, tiled=True)
-                for weight in (w_gate, w_up, w_down)
-            )
+            (pair[:, :step], pair[:, step:], lax.all_gather(w_down[:, part], ROWS, axis=0, tiled=True))
         )
     heads = cols // HD
     cosine, sine = rope_tables(position)
@@ -450,10 +460,10 @@
             contract_first(grad_y, hidden),
         )
         h2_grad_partial = back_part if h2_grad_partial is None else h2_grad_partial + back_part
-        staged.append(tuple(chip_total(value) for value in pending))
+        staged.append(chip_total(jnp.concatenate(pending, axis=1)))
     grad_h2 = tensor_total(h2_grad_partial)
     grad_h2, staged[-1] = lax.optimization_barrier((grad_h2, staged[-1]))
-    reduced = [tuple(line_total(value) for value in chunk) for chunk in staged]
+    reduced = [line_total(chunk) for chunk in staged]
     result = (resid2 + tensor_total(mlp_partial)).astype(bf16)
     grad_gmlp = jnp.sum(grad_h2 * norm2, axis=0)
     grad_resid = grad_y.astype(f32) + norm_back(grad_h2, norm2, inv2, gain_mlp)
@@ -463,8 +473,8 @@
         .astype(bf16)
         .reshape(rows, heads, HD)
     )
-    grad_heads, partial_o = lax.optimization_barrier(
-        (grad_heads, contract_first(grad_resid_part, attended_flat))
+    grad_heads, partial_o, result = lax.optimization_barrier(
+        (grad_heads, contract_first(grad_resid_part, attended_flat), result)
     )
     early = (chip_total(partial_o), reduced[:-1])
     grad_qin, grad_kin, grad_vin, early = attention.backward(grad_heads, early)
@@ -474,25 +484,30 @@
         [grad_qin.reshape(rows, cols), grad_kin.reshape(rows, cols), grad_vin.reshape(rows, cols)],
         axis=1,
     )
+    h1_grad_partial = contract_last(grad_qkv, full_qkv)
+    first_tensor = (lax.axis_index("tensor") == 0).astype(f32)
+    gain_parts = jnp.stack(
+        [jnp.sum(h1_grad_partial * norm1, axis=0), grad_gmlp * first_tensor], axis=1
+    )
+    gain_slab = jnp.pad(tensor_exact_total(gain_parts), ((0, 0), (0, 126)))
     h1_grad_partial, staged_qkv = lax.optimization_barrier(
-        (contract_last(grad_qkv, full_qkv), chip_total(contract_first(h1, grad_qkv)))
+        (h1_grad_partial, chip_total(jnp.concatenate([contract_first(h1, grad_qkv), gain_slab], axis=1)))
     )
     grad_h1 = tensor_total(h1_grad_partial)
     grad_h1, reduced_o, reduced[-1] = lax.optimization_barrier((grad_h1, reduced_o, reduced[-1]))
-    grad_gattn = jnp.sum(grad_h1 * norm1, axis=0)
     grad_x_part = (grad_resid + norm_back(grad_h1, norm1, inv1, gain_attn)).astype(bf16)
-    gain_slab = jnp.pad(jnp.stack([grad_gattn, grad_gmlp], axis=1), ((0, 0), (0, 126)))
     reduced_qkv = line_total(staged_qkv)
-    reduced_gains = rows_total(gain_slab)
+    reduced_gains = reduced_qkv[:, 3 * cols :]
     reduced_gate, reduced_up, reduced_down = (
-        jnp.concatenate([chunk[which] for chunk in reduced], axis=1) for which in range(3)
+        jnp.concatenate([chunk[:, which * step : (which + 1) * step] for chunk in reduced], axis=1)
+        for which in range(3)
     )
     return (
         result.reshape(1, rows, width),
         grad_x_part.reshape(1, rows, width),
         reduced_qkv[:, :cols],
         reduced_qkv[:, cols : 2 * cols],
-        reduced_qkv[:, 2 * cols :],
+        reduced_qkv[:, 2 * cols : 3 * cols],
         reduced_o,
         reduced_gate,
         reduced_up,

time: 908 us -> 904 us (level)
  blocking collectives: 24.1 us -> 54.6 us
  other arithmetic: 143 us -> 171 us
  local copies, waits for them, and re-layouts: 148 us -> 125 us
  starting transfers between devices: 79.4 us -> 62.7 us
  waiting for transfers between devices: 296 us -> 283 us
    concatenate x6 -> x9, other arithmetic: 10.7 us -> 44.6 us  [the longest x2 21.3 us: on_device(): staged.append(chip_total(jnp.concatenate(pending, axis=1)))]
    all_to_all x0 -> x1, blocking collectives: none -> 30.6 us  [backward(): grad = lax.all_to_all(grad, 'context', 1, 0, tiled=True)]
    all_to_all x3, waiting for transfers between devices: 14.6 us -> 44.7 us  [backward(): grad_in = lax.all_to_all(grad_in, 'context', 0, 1, tiled=True)]
    all_to_all x1 -> x0, waiting for transfers between devices: 25.9 us -> none  [backward(): grad = lax.all_to_all(grad, 'context', 1, 0, tiled=True)]
    reduce_scatter x9 -> x4, waiting for transfers between devices: 21.9 us -> 0.01 us  [line_total(): lax.psum_scatter(staged.astype(jnp.bfloat16), 'context', scatter_dimensio...]
    unnamed x273 -> x266, local copies, waits for them, and re-layouts: 53.8 us -> 36.7 us
    dot_general x4, matrix products: 27.8 us -> 14.9 us  [backward(): jnp.einsum('hqk,qhd->khd', probs.astype(bf16), grad_block, preferred_elem...]
    dot_general x8, matrix products: 31.7 us -> 44 us  [contract_last(): lax.dot_general(left, right, (((1,), (1,)), ((), ())), preferred_element_...]
  transfers between devices with their start and end apart: 65 -> 53, of which waited for: 31 -> 29; matrix products, arithmetic and copies ran while one was open for 50% -> 47% of each run, Pallas kernels for 0% -> 0%
where the time goes in v6:
time: 904 us; the launch traced here: 898 us
  waiting for transfers between devices  283 us (31%)
  matrix products  185 us (20%)
  other arithmetic  171 us (19%)
  local copies, waits for them, and re-layouts  125 us (14%)
  starting transfers between devices  62.7 us (7%)
  blocking collectives  54.6 us (6%)
  between operations  16.4 us (2%)
    all_to_all x1, waiting for transfers between devices, __init__(): stacked = lax.all_to_all(stacked, 'context', 2, 0, tiled=True)  50.4 us
    all_gather x1, waiting for transfers between devices, on_device(): lax.all_gather(jnp.concatenate([w_q, w_k, w_v, w_o], axis=1), ROWS, axis=...  47.9 us
    all_to_all x3, waiting for transfers between devices, backward(): grad_in = lax.all_to_all(grad_in, 'context', 0, 1, tiled=True)  44.7 us
    ppermute x16, waiting for transfers between devices, swap(): return lax.ppermute(value.astype(bf16), 'tensor', pairs).astype(f32)  44.5 us
    dot_general x8, matrix products, contract_last(): lax.dot_general(left, right, (((1,), (1,)), ((), ())), preferred_element_...  44 us
    unnamed x266, local copies, waits for them, and re-layouts  36.7 us
    add x4, other arithmetic, chip_total(): return mine.astype(f32) + got.astype(f32)  30.7 us
    all_to_all x1, blocking collectives, backward(): grad = lax.all_to_all(grad, 'context', 1, 0, tiled=True)  30.6 us
  transfers between devices with their start and end apart: 53, of which 29 were waited for; matrix products, arithmetic and copies ran while one was open for 47% of the time, Pallas kernels for 0%

profile of v6, /device:TPU:0, one launch (start us, length us, event | category | flops | bytes accessed | tf_op | source)
XLA Modules:
  0.0 897.9 jit_solution(4551759615885758369)
XLA Ops:
  16.3 6.3 all-to-all-start.1
  22.7 24.0 %all-gather.1 = bf16[8,1,512]{2,1,0:T(2,128)(2,1)S(1)} all-gather(bf16[1,1,512]{2,1,0:T(2,128)(2,1)S(1)} %reshape.705), channel_id=2, replica_groups=mesh['shard'=2,'context'=4,'tensor'=4] {'shard','context'}, dimensions={0}, use_global_device_ids=true | all-gather | bytes 9216 | tf_op jit(solution)/shard_map/all_gather | solution.py:395
  47.5 47.9 %all-gather.8.cloned.1.call-done = bf16[2048,2048]{1,0:T(8,128)(2,1)} async-done(((bf16[256,2048]{1,0:T(8,128)(2,1)}), bf16[2048,2048]{1,0:T(8,128)(2,1)}) %all-gather.8.cloned.1.call-update) | async-done | bytes 8388624 | tf_op jit(solution)/shard_map/all_gather | solution.py:390
  95.4 5.6 fusion.18
  115.3 4.4 all-to-all-start
  120.3 4.5 compare_and_fusion.3
  124.9 50.4 %all-to-all-done = bf16[512,3,4,2,64]{0,4,3,1,2:T(8,128)(2,1)} async-done(((bf16[512,3,4,2,64]{0,4,3,1,2:T(8,128)(2,1)}), bf16[512,3,4,2,64]{0,4,3,1,2:T(8,128)(2,1)}, u32[]{:S(2)}, u32[]{:S(2)}) %all-to-all-start) | async-done | bytes 1572896 | tf_op jit(solution)/shard_map/all_to_all | solution.py:276
  175.3 3.9 copy.66
  179.2 3.9 reshape.693
  183.1 6.7 fusion.23
  193.8 5.7 fusion.20
  199.5 8.8 fusion.4
  208.3 5.2 fusion.116
  216.4 8.1 fusion
  235.5 4.1 all-to-all-start.2
  239.7 21.7 %all-to-all-done.2 = bf16[4,2,32768]{2,1,0:T(2,128)(2,1)} async-done(((bf16[4,2,32768]{2,1,0:T(2,128)(2,1)}), bf16[4,2,32768]{2,1,0:T(2,128)(2,1)}, u32[]{:S(2)}, u32[]{:S(2)}) %all-to-all-start.2) | async-done | bytes 524320 | tf_op jit(solution)/shard_map/all_to_all | solution.py:325
  279.0 8.0 collective-permute-done.4
  292.1 4.5 collective-permute-done.5
  298.9 5.1 collective-permute-done.6
  307.3 6.5 fusion.90
  321.9 4.6 multiply_convert_fusion.4
  326.5 5.4 fusion.67
  343.6 10.7 %pad_maximum_fusion = f32[2048,3072]{0,1:T(8,128)} fusion(f32[2048,1024]{0,1:T(8,128)S(1)} %convolution_bitcast_fusion.1, f32[2048,1024]{0,1:T(8,128)S(1)} %fusion.213, f32[2048,1024]{0,1:T(8,128)S(1)} %fusion.212), kind=kLoop, calls=%fused_computation | loop fusion | flops 12582912 | bytes 50331648 | tf_op jit(solution)/shard_map/concatenate | solution.py:463
  354.3 8.4 dynamic-slice_convert_fusion.1
  362.7 6.5 fusion.88
  369.3 21.2 %all-gather.16.cloned.1.call-done = bf16[2048,2048]{1,0:T(8,128)(2,1)} async-done(((bf16[256,2048]{1,0:T(8,128)(2,1)}), bf16[2048,2048]{1,0:T(8,128)(2,1)}) %all-gather.16.cloned.1.call-update) | async-done | bytes 8388624 | tf_op jit(solution)/shard_map/all_gather | solution.py:405
  390.5 4.8 slice.247
  395.2 6.7 fusion.61
  402.0 4.4 fusion.65
  406.3 4.3 fusion.217
  410.7 11.5 %convert_add_fusion.1 = bf16[1024,3072]{0,1:T(8,128)(2,1)} fusion(bf16[1024,3072]{0,1:T(8,128)(2,1)} %collective-permute-done.8, f32[2048,3072]{0,1:T(8,128)} %pad_maximum_fusion, s32[]{:T(128)S(6)} %select_n.291), kind=kLoop, calls=%fused_computation.6 | loop fusion | flops 9437184 | bytes 25165828 | tf_op jit(solution)/shard_map/add | solution.py:129
  422.2 5.1 fusion.214
  427.3 6.2 multiply_convert_fusion.5
  438.5 4.5 fusion.57
  443.0 7.5 add_add_fusion
  457.5 10.6 %pad_maximum_fusion.1 = f32[2048,3072]{0,1:T(8,128)} fusion(f32[2048,1024]{0,1:T(8,128)S(1)} %convolution_bitcast_fusion, f32[2048,1024]{0,1:T(8,128)S(1)} %fusion.216, f32[2048,1024]{0,1:T(8,128)S(1)} %fusion.215), kind=kLoop, calls=%fused_computation.1 | loop fusion | flops 12582912 | bytes 50331648 | tf_op jit(solution)/shard_map/concatenate | solution.py:463
  468.0 8.5 dynamic-slice_convert_fusion
  476.5 4.6 convolution_add_fusion
  489.8 7.8 collective-permute-done.22
  522.8 9.5 %collective-permute-done.16 = bf16[128,2048]{1,0:T(8,128)(2,1)S(1)} collective-permute-done((bf16[128,2048]{1,0:T(8,128)(2,1)S(1)}, bf16[128,2048]{1,0:T(8,128)(2,1)S(1)}, u32[]{:S(2)}, u32[]{:S(2)}) %collective-permute-start.16) | collective-permute-done | bytes 524320 | tf_op jit(solution)/shard_map/ppermute | solution.py:112
  535.3 6.6 collective-permute-done.25
  544.4 11.8 %convert_add_fusion = bf16[1024,3072]{0,1:T(8,128)(2,1)} fusion(bf16[1024,3072]{0,1:T(8,128)(2,1)} %collective-permute-done.17, f32[2048,3072]{0,1:T(8,128)} %pad_maximum_fusion.1, s32[]{:T(128)S(6)} %select_n.291), kind=kLoop, calls=%fused_computation.4 | loop fusion | flops 9437184 | bytes 25165828 | tf_op jit(solution)/shard_map/add | solution.py:129
  556.2 5.1 multiply_reduce_fusion
  562.4 4.1 multiply_add_fusion
  571.7 30.6 %all_to_all.98 = bf16[512,4,2,64]{0,3,2,1:T(8,128)(2,1)S(1)} all-to-all(bf16[512,4,2,64]{0,3,2,1:T(8,128)(2,1)S(1)} %bitcast.298), channel_id=1, replica_groups=mesh['shard'=2,'context'=4,'tensor'=4] {'context'}, dimensions={1} | all-to-all | bytes 1048576 | tf_op jit(solution)/shard_map/all_to_all | solution.py:333
  616.4 6.3 multiply_convert_fusion.3
  626.2 5.9 fusion.36
  647.5 4.3 all-to-all-start.6
  651.9 6.6 multiply_convert_fusion
  658.5 6.2 multiply_convert_fusion.1
  666.2 3.9 multiply_convert_fusion.2
  683.6 4.4 all-to-all-start.5
  693.7 24.2 %all-to-all-done.5 = bf16[4,2,32768]{2,1,0:T(2,128)(2,1)} async-done(((bf16[4,2,32768]{2,1,0:T(2,128)(2,1)}), bf16[4,2,32768]{2,1,0:T(2,128)(2,1)}, u32[]{:S(2)}, u32[]{:S(2)}) %all-to-all-start.5) | async-done | bytes 524320 | tf_op jit(solution)/shard_map/all_to_all | solution.py:366
  717.9 5.6 all-to-all-start.4
  734.7 18.4 %all-to-all-done.4 = bf16[4,2,32768]{2,1,0:T(2,128)(2,1)} async-done(((bf16[4,2,32768]{2,1,0:T(2,128)(2,1)}), bf16[4,2,32768]{2,1,0:T(2,128)(2,1)}, u32[]{:S(2)}, u32[]{:S(2)}) %all-to-all-start.4) | async-done | bytes 524320 | tf_op jit(solution)/shard_map/all_to_all | solution.py:366
  757.9 9.0 %fusion.25 = (f32[2048]{0:T(1024)S(1)}, f32[512,2048]{1,0:T(8,128)}) fusion(bf16[1,512,2048]{2,1,0:T(8,128)(2,1)S(1)} %copy-done.1, f32[512]{0:T(512)S(1)} %copy-done.80, bf16[2048,2048]{1,0:T(8,128)(2,1)} %all-gather.8.cloned.1.call-done, bf16[512,512]{0,1:T(8,128)(2,1)} %bitcast.292, bf16[512,512]{0,1:T(8,128)(2,1)} %bitcast.294, ...), kind=kOutput, calls=%fused_computation.56 | convolution fusion | flops 3230136320 | bytes 14166016 | tf_op jit(solution)/shard_map/dot_general | solution.py:63
  772.4 6.7 fusion.141
  779.2 11.7 %select_maximum_fusion = f32[2048,1664]{0,1:T(8,128)} fusion(f32[2048,2]{0,1:T(2,128)S(1)} %fusion.254, f32[2048,1536]{0,1:T(8,128)} %fusion.141), kind=kLoop, calls=%fused_computation.2 | loop fusion | flops 10223616 | bytes 26230784 | tf_op jit(solution)/shard_map/concatenate | solution.py:494
  794.4 6.0 collective-permute-done.29
  800.4 6.1 convert_add_fusion.2
  812.5 10.7 %collective-permute-done.34 = bf16[128,2048]{1,0:T(8,128)(2,1)} collective-permute-done((bf16[128,2048]{1,0:T(8,128)(2,1)S(1)}, bf16[128,2048]{1,0:T(8,128)(2,1)}, u32[]{:S(2)}, u32[]{:S(2)}) %collective-permute-start.34) | collective-permute-done | bytes 524320 | tf_op jit(solution)/shard_map/ppermute | solution.py:99
  828.5 3.8 collective-permute-done.35
  847.1 6.0 collective-permute-done.37
  881.0 4.6 fusion.85
  (526 shorter events, 284.7 us)
Async XLA Ops:
  7.2 88.3 %all-gather.8.cloned.1.call-start = ((), (), s32[]{:S(2)}) async-start(), calls=%async_computation.11 | async-start | bytes 9437184 | tf_op jit(solution)/shard_map/all_gather | solution.py:390
  9.6 297.7 %all-gather.10.cloned.1.call-start = ((), (), s32[]{:S(2)}) async-start(), calls=%async_computation.12 | async-start | bytes 4718592 | tf_op jit(solution)/shard_map/all_gather | solution.py:409
  12.0 34.7 %copy-start = (bf16[1,512,2048]{2,1,0:T(8,128)(2,1)S(1)}, bf16[1,512,2048]{2,1,0:T(8,128)(2,1)}, u32[]{:S(2)}) copy-start(bf16[1,512,2048]{2,1,0:T(8,128)(2,1)} %param.13) | copy-start | bytes 6291460
  12.0 314.5 %all-gather.12.cloned.1.call-start = ((), (), s32[]{:S(2)}) async-start(), calls=%async_computation.13 | async-start | bytes 9437184 | tf_op jit(solution)/shard_map/all_gather | solution.py:405
  16.3 99.0 %all-to-all-start.1 = ((s32[4,2,512]{2,1,0:T(2,128)}), s32[4,2,512]{2,1,0:T(2,128)S(1)}, u32[]{:S(2)}, u32[]{:S(2)}) async-start(s32[4,2,512]{2,1,0:T(2,128)} %broadcast_in_dim.158), calls=%async_computation.1 | async-start | bytes 32768 | tf_op jit(solution)/shard_map/all_to_all | solution.py:283
  46.7 48.8 %copy-start.73 = (f32[1,2,8,128]{3,1,2,0:T(2,128)}, f32[1,2,8,128]{3,1,2,0:T(2,128)S(1)}, u32[]{:S(2)}) copy-start(f32[1,2,8,128]{3,1,2,0:T(2,128)S(1)} %copy.92) | copy-start | bytes 24580
  46.7 48.8 %copy-start.95 = (f32[32]{0:T(128)}, f32[32]{0:T(128)S(1)}, u32[]{:S(2)}) copy-start(f32[32]{0:T(128)S(1)} %multiply_power_fusion) | copy-start | bytes 388
  47.2 48.2 %copy-start.79 = (f32[512]{0:T(512)}, f32[512]{0:T(512)S(1)}, u32[]{:S(2)}) copy-start(f32[512]{0:T(512)S(1)} %add_rsqrt_fusion.1) | copy-start | bytes 6148
  115.3 60.0 %all-to-all-start = ((bf16[512,3,4,2,64]{0,4,3,1,2:T(8,128)(2,1)}), bf16[512,3,4,2,64]{0,4,3,1,2:T(8,128)(2,1)}, u32[]{:S(2)}, u32[]{:S(2)}) async-start(bf16[512,3,4,2,64]{0,4,3,1,2:T(8,128)(2,1)} %copy.65), calls=%async_computation | async-start | bytes 3145728 | tf_op jit(solution)/shard_map/all_to_all | solution.py:276
  119.7 243.1 %all-gather.14.cloned.1.call-start = ((), (), s32[]{:S(2)}) async-start(), calls=%async_computation.14 | async-start | bytes 4718592 | tf_op jit(solution)/shard_map/all_gather | solution.py:409
  120.3 62.8 %copy-start.75 = (s32[1,4,512]{2,0,1:T(1,128)}, s32[1,4,512]{2,0,1:T(1,128)S(1)}, u32[]{:S(2)}) copy-start(s32[1,4,512]{2,0,1:T(1,128)S(1)} %get-tuple-element.182) | copy-start | bytes 24580
  124.9 99.6 %copy-start.34 = (pred[512,2048]{1,0:T(8,128)(4,1)}, pred[512,2048]{1,0:T(8,128)(4,1)S(1)}, u32[]{:S(2)}) copy-start(pred[512,2048]{1,0:T(8,128)(4,1)S(1)} %get-tuple-element.170) | copy-start | bytes 3145732
  193.8 30.7 %copy-start.18 = (f32[2,512,2048]{2,1,0:T(8,128)}, f32[2,512,2048]{2,1,0:T(8,128)S(1)}, u32[]{:S(2)}) copy-start(f32[2,512,2048]{2,1,0:T(8,128)S(1)} %get-tuple-element.190) | copy-start | bytes 25165828
  193.8 30.7 %copy-start.85 = (f32[2,512]{1,0:T(2,128)}, f32[2,512]{1,0:T(2,128)S(1)}, u32[]{:S(2)}) copy-start(f32[2,512]{1,0:T(2,128)S(1)} %get-tuple-element.189) | copy-start | bytes 12292
  199.5 27.8 %copy-start.87 = (f32[2,512]{1,0:T(2,128)}, f32[2,512]{1,0:T(2,128)S(1)}, u32[]{:S(2)}) copy-start(f32[2,512]{1,0:T(2,128)S(1)} %get-tuple-element.195) | copy-start | bytes 12292
  235.5 25.9 %all-to-all-start.2 = ((bf16[4,2,32768]{2,1,0:T(2,128)(2,1)}), bf16[4,2,32768]{2,1,0:T(2,128)(2,1)}, u32[]{:S(2)}, u32[]{:S(2)}) async-start(bf16[4,2,32768]{2,1,0:T(2,128)(2,1)} %reshape.708), calls=%async_computation.2 | async-start | bytes 1048576 | tf_op jit(solution)/shard_map/all_to_all | solution.py:325
  239.7 150.8 %all-gather.16.cloned.1.call-start = ((), (), s32[]{:S(2)}) async-start(), calls=%async_computation.15 | async-start | bytes 9437184 | tf_op jit(solution)/shard_map/all_gather | solution.py:405
  273.2 13.7 %collective-permute-start.4 = (bf16[128,2048]{1,0:T(8,128)(2,1)S(1)}, bf16[128,2048]{1,0:T(8,128)(2,1)S(1)}, u32[]{:S(2)}, u32[]{:S(2)}) collective-permute-start(bf16[128,2048]{1,0:T(8,128)(2,1)S(1)} %dynamic-slice_convert_fusion.10), channel_id=1, source_target_pairs={{0,2},{1,3},{2,0},{3,1},{4,6},{5,7},{6,4},{7,5},{8,10},{9,11},{10,... | collective-permute-start | bytes 1572872 | tf_op jit(solution)/shard_map/ppermute | solution.py:99
  275.8 328.7 %reduce-scatter.5.cloned.1.call-start = ((), (), s32[]{:S(2)}) async-start(), calls=%async_computation.16 | async-start | bytes 7864320 | tf_op jit(solution)/shard_map/reduce_scatter | solution.py:133
  275.9 46.0 %copy-start.71 = (f32[1,2,8,128]{3,1,2,0:T(2,128)}, f32[1,2,8,128]{3,1,2,0:T(2,128)S(1)}, u32[]{:S(2)}) copy-start(f32[1,2,8,128]{3,1,2,0:T(2,128)S(1)} %copy.93) | copy-start | bytes 24580
  277.4 14.4 %collective-permute-start = (bf16[128,2048]{1,0:T(8,128)(2,1)S(1)}, bf16[128,2048]{1,0:T(8,128)(2,1)S(1)}, u32[]{:S(2)}, u32[]{:S(2)}) collective-permute-start(bf16[128,2048]{1,0:T(8,128)(2,1)S(1)} %dynamic-slice_convert_fusion.11), channel_id=1, source_target_pairs={{0,1},{1,0},{2,3},{3,2},{4,5},{5,4},{6,7},{7,6},{8,9},{9,8},{10,11... | collective-permute-start | bytes 1572872 | tf_op jit(solution)/shard_map/ppermute | solution.py:99
  288.3 8.2 collective-permute-start.5
  292.0 6.4 collective-permute-start.1
  296.6 7.5 collective-permute-start.6
  298.5 6.9 collective-permute-start.2
  305.0 12.6 %collective-permute-start.7 = (bf16[128,2048]{1,0:T(8,128)(2,1)}, bf16[128,2048]{1,0:T(8,128)(2,1)}, u32[]{:S(2)}, u32[]{:S(2)}) collective-permute-start(bf16[128,2048]{1,0:T(8,128)(2,1)} %pad_maximum_fusion.16), channel_id=1, source_target_pairs={{0,2},{1,3},{2,0},{3,1},{4,6},{5,7},{6,4},{7,5},{8,10},{9,11},{10,... | collective-permute-start | bytes 1572872 | tf_op jit(solution)/shard_map/ppermute | solution.py:112
  306.2 12.7 %collective-permute-start.3 = (bf16[128,2048]{1,0:T(8,128)(2,1)}, bf16[128,2048]{1,0:T(8,128)(2,1)}, u32[]{:S(2)}, u32[]{:S(2)}) collective-permute-start(bf16[128,2048]{1,0:T(8,128)(2,1)} %pad_maximum_fusion.15), channel_id=1, source_target_pairs={{0,1},{1,0},{2,3},{3,2},{4,5},{5,4},{6,7},{7,6},{8,9},{9,8},{10,11... | collective-permute-start | bytes 1572872 | tf_op jit(solution)/shard_map/ppermute | solution.py:111
  362.7 47.9 %collective-permute-start.8 = (bf16[1024,3072]{0,1:T(8,128)(2,1)}, bf16[1024,3072]{0,1:T(8,128)(2,1)}, u32[]{:S(2)}, u32[]{:S(2)}) collective-permute-start(bf16[1024,3072]{0,1:T(8,128)(2,1)} %dynamic-slice_convert_fusion.1), channel_id=1, source_target_pairs={{0,16},{16,0},{1,17},{17,1},{2,18},{18,2},{3,19},{19,3},{4,20},{20... | collective-permute-start | bytes 18874376 | tf_op jit(solution)/shard_map/ppermute | solution.py:128
  452.0 32.2 %collective-permute-start.13 = (bf16[128,2048]{1,0:T(8,128)(2,1)}, bf16[128,2048]{1,0:T(8,128)(2,1)}, u32[]{:S(2)}, u32[]{:S(2)}) collective-permute-start(bf16[128,2048]{1,0:T(8,128)(2,1)} %dynamic-slice_convert_fusion.8), channel_id=1, source_target_pairs={{0,2},{1,3},{2,0},{3,1},{4,6},{5,7},{6,4},{7,5},{8,10},{9,11},{10,... | collective-permute-start | bytes 1572872 | tf_op jit(solution)/shard_map/ppermute | solution.py:99
  453.5 34.0 %collective-permute-start.9 = (bf16[128,2048]{1,0:T(8,128)(2,1)S(1)}, bf16[128,2048]{1,0:T(8,128)(2,1)}, u32[]{:S(2)}, u32[]{:S(2)}) collective-permute-start(bf16[128,2048]{1,0:T(8,128)(2,1)S(1)} %dynamic-slice_convert_fusion.9), channel_id=1, source_target_pairs={{0,1},{1,0},{2,3},{3,2},{4,5},{5,4},{6,7},{7,6},{8,9},{9,8},{10,11... | collective-permute-start | bytes 1572872 | tf_op jit(solution)/shard_map/ppermute | solution.py:99
  476.5 67.8 %collective-permute-start.17 = (bf16[1024,3072]{0,1:T(8,128)(2,1)}, bf16[1024,3072]{0,1:T(8,128)(2,1)}, u32[]{:S(2)}, u32[]{:S(2)}) collective-permute-start(bf16[1024,3072]{0,1:T(8,128)(2,1)} %dynamic-slice_convert_fusion), channel_id=1, source_target_pairs={{0,16},{16,0},{1,17},{17,1},{2,18},{18,2},{3,19},{19,3},{4,20},{20... | collective-permute-start | bytes 18874376 | tf_op jit(solution)/shard_map/ppermute | solution.py:128
  482.4 15.1 %collective-permute-start.22 = (bf16[128,2048]{1,0:T(8,128)(2,1)}, bf16[128,2048]{1,0:T(8,128)(2,1)}, u32[]{:S(2)}, u32[]{:S(2)}) collective-permute-start(bf16[128,2048]{1,0:T(8,128)(2,1)} %dynamic-slice_convert_fusion.6), channel_id=1, source_target_pairs={{0,2},{1,3},{2,0},{3,1},{4,6},{5,7},{6,4},{7,5},{8,10},{9,11},{10,... | collective-permute-start | bytes 1572872 | tf_op jit(solution)/shard_map/ppermute | solution.py:99
  483.6 15.8 %collective-permute-start.18 = (bf16[128,2048]{1,0:T(8,128)(2,1)S(1)}, bf16[128,2048]{1,0:T(8,128)(2,1)}, u32[]{:S(2)}, u32[]{:S(2)}) collective-permute-start(bf16[128,2048]{1,0:T(8,128)(2,1)S(1)} %dynamic-slice_convert_fusion.7), channel_id=1, source_target_pairs={{0,1},{1,0},{2,3},{3,2},{4,5},{5,4},{6,7},{7,6},{8,9},{9,8},{10,11... | collective-permute-start | bytes 1572872 | tf_op jit(solution)/shard_map/ppermute | solution.py:99
  484.2 361.2 %reduce-scatter.7.cloned.1.call-start = ((), (), s32[]{:S(2)}) async-start(), calls=%async_computation.17 | async-start | bytes 1310720 | tf_op jit(solution)/shard_map/reduce_scatter | solution.py:133
  485.9 18.1 %collective-permute-start.14 = (bf16[64,2048]{1,0:T(8,128)(2,1)S(1)}, bf16[64,2048]{1,0:T(8,128)(2,1)S(1)}, u32[]{:S(2)}, u32[]{:S(2)}) collective-permute-start(bf16[64,2048]{1,0:T(8,128)(2,1)S(1)} %dynamic-slice_convert_fusion.16), channel_id=1, source_target_pairs={{0,1},{1,0},{2,3},{3,2},{4,5},{5,4},{6,7},{7,6},{8,9},{9,8},{10,11... | collective-permute-start | bytes 786440 | tf_op jit(solution)/shard_map/ppermute | solution.py:99
  488.8 15.8 %collective-permute-start.10 = (bf16[64,2048]{1,0:T(8,128)(2,1)S(1)}, bf16[64,2048]{1,0:T(8,128)(2,1)S(1)}, u32[]{:S(2)}, u32[]{:S(2)}) collective-permute-start(bf16[64,2048]{1,0:T(8,128)(2,1)S(1)} %dynamic-slice_convert_fusion.17), channel_id=1, source_target_pairs={{0,2},{1,3},{2,0},{3,1},{4,6},{5,7},{6,4},{7,5},{8,10},{9,11},{10,... | collective-permute-start | bytes 786440 | tf_op jit(solution)/shard_map/ppermute | solution.py:99
  498.7 10.9 %collective-permute-start.23 = (bf16[64,2048]{1,0:T(8,128)(2,1)S(1)}, bf16[64,2048]{1,0:T(8,128)(2,1)S(1)}, u32[]{:S(2)}, u32[]{:S(2)}) collective-permute-start(bf16[64,2048]{1,0:T(8,128)(2,1)S(1)} %dynamic-slice_convert_fusion.14), channel_id=1, source_target_pairs={{0,1},{1,0},{2,3},{3,2},{4,5},{5,4},{6,7},{7,6},{8,9},{9,8},{10,11... | collective-permute-start | bytes 786440 | tf_op jit(solution)/shard_map/ppermute | solution.py:99
  500.6 9.7 %collective-permute-start.19 = (bf16[64,2048]{1,0:T(8,128)(2,1)S(1)}, bf16[64,2048]{1,0:T(8,128)(2,1)S(1)}, u32[]{:S(2)}, u32[]{:S(2)}) collective-permute-start(bf16[64,2048]{1,0:T(8,128)(2,1)S(1)} %dynamic-slice_convert_fusion.15), channel_id=1, source_target_pairs={{0,2},{1,3},{2,0},{3,1},{4,6},{5,7},{6,4},{7,5},{8,10},{9,11},{10,... | collective-permute-start | bytes 786440 | tf_op jit(solution)/shard_map/ppermute | solution.py:99
  504.0 11.2 %collective-permute-start.15 = (bf16[64,2048]{1,0:T(8,128)(2,1)S(1)}, bf16[64,2048]{1,0:T(8,128)(2,1)S(1)}, u32[]{:S(2)}, u32[]{:S(2)}) collective-permute-start(bf16[64,2048]{1,0:T(8,128)(2,1)S(1)} %add_convert_fusion.7), channel_id=1, source_target_pairs={{0,1},{1,0},{2,3},{3,2},{4,5},{5,4},{6,7},{7,6},{8,9},{9,8},{10,11... | collective-permute-start | bytes 786440 | tf_op jit(solution)/shard_map/ppermute | solution.py:110
  504.7 11.7 %collective-permute-start.11 = (bf16[64,2048]{1,0:T(8,128)(2,1)S(1)}, bf16[64,2048]{1,0:T(8,128)(2,1)S(1)}, u32[]{:S(2)}, u32[]{:S(2)}) collective-permute-start(bf16[64,2048]{1,0:T(8,128)(2,1)S(1)} %add_convert_fusion.8), channel_id=1, source_target_pairs={{0,2},{1,3},{2,0},{3,1},{4,6},{5,7},{6,4},{7,5},{8,10},{9,11},{10,... | collective-permute-start | bytes 786440 | tf_op jit(solution)/shard_map/ppermute | solution.py:109
  509.7 11.2 %collective-permute-start.24 = (bf16[64,2048]{1,0:T(8,128)(2,1)S(1)}, bf16[64,2048]{1,0:T(8,128)(2,1)S(1)}, u32[]{:S(2)}, u32[]{:S(2)}) collective-permute-start(bf16[64,2048]{1,0:T(8,128)(2,1)S(1)} %add_convert_fusion.5), channel_id=1, source_target_pairs={{0,1},{1,0},{2,3},{3,2},{4,5},{5,4},{6,7},{7,6},{8,9},{9,8},{10,11... | collective-permute-start | bytes 786440 | tf_op jit(solution)/shard_map/ppermute | solution.py:110
  510.3 11.7 %collective-permute-start.20 = (bf16[64,2048]{1,0:T(8,128)(2,1)S(1)}, bf16[64,2048]{1,0:T(8,128)(2,1)S(1)}, u32[]{:S(2)}, u32[]{:S(2)}) collective-permute-start(bf16[64,2048]{1,0:T(8,128)(2,1)S(1)} %add_convert_fusion.6), channel_id=1, source_target_pairs={{0,2},{1,3},{2,0},{3,1},{4,6},{5,7},{6,4},{7,5},{8,10},{9,11},{10,... | collective-permute-start | bytes 786440 | tf_op jit(solution)/shard_map/ppermute | solution.py:109
  515.3 17.0 %collective-permute-start.16 = (bf16[128,2048]{1,0:T(8,128)(2,1)S(1)}, bf16[128,2048]{1,0:T(8,128)(2,1)S(1)}, u32[]{:S(2)}, u32[]{:S(2)}) collective-permute-start(bf16[128,2048]{1,0:T(8,128)(2,1)S(1)} %pad_maximum_fusion.18), channel_id=1, source_target_pairs={{0,2},{1,3},{2,0},{3,1},{4,6},{5,7},{6,4},{7,5},{8,10},{9,11},{10,... | collective-permute-start | bytes 1572872 | tf_op jit(solution)/shard_map/ppermute | solution.py:112
  516.5 16.0 %collective-permute-start.12 = (bf16[128,2048]{1,0:T(8,128)(2,1)S(1)}, bf16[128,2048]{1,0:T(8,128)(2,1)S(1)}, u32[]{:S(2)}, u32[]{:S(2)}) collective-permute-start(bf16[128,2048]{1,0:T(8,128)(2,1)S(1)} %pad_maximum_fusion.17), channel_id=1, source_target_pairs={{0,1},{1,0},{2,3},{3,2},{4,5},{5,4},{6,7},{7,6},{8,9},{9,8},{10,11... | collective-permute-start | bytes 1572872 | tf_op jit(solution)/shard_map/ppermute | solution.py:111
  520.9 21.0 %collective-permute-start.25 = (bf16[128,2048]{1,0:T(8,128)(2,1)S(1)}, bf16[128,2048]{1,0:T(8,128)(2,1)S(1)}, u32[]{:S(2)}, u32[]{:S(2)}) collective-permute-start(bf16[128,2048]{1,0:T(8,128)(2,1)S(1)} %pad_maximum_fusion.20), channel_id=1, source_target_pairs={{0,2},{1,3},{2,0},{3,1},{4,6},{5,7},{6,4},{7,5},{8,10},{9,11},{10,... | collective-permute-start | bytes 1572872 | tf_op jit(solution)/shard_map/ppermute | solution.py:112
  522.1 21.0 %collective-permute-start.21 = (bf16[128,2048]{1,0:T(8,128)(2,1)S(1)}, bf16[128,2048]{1,0:T(8,128)(2,1)S(1)}, u32[]{:S(2)}, u32[]{:S(2)}) collective-permute-start(bf16[128,2048]{1,0:T(8,128)(2,1)S(1)} %pad_maximum_fusion.19), channel_id=1, source_target_pairs={{0,1},{1,0},{2,3},{3,2},{4,5},{5,4},{6,7},{7,6},{8,9},{9,8},{10,11... | collective-permute-start | bytes 1572872 | tf_op jit(solution)/shard_map/ppermute | solution.py:111
  571.7 31.5 %collective-permute-start.26 = (bf16[1024,512]{1,0:T(8,128)(2,1)S(1)}, bf16[1024,512]{1,0:T(8,128)(2,1)S(1)}, u32[]{:S(2)}, u32[]{:S(2)}) collective-permute-start(bf16[1024,512]{1,0:T(8,128)(2,1)S(1)} %dynamic-slice_convert_fusion.3), channel_id=1, source_target_pairs={{0,16},{16,0},{1,17},{17,1},{2,18},{18,2},{3,19},{19,3},{4,20},{20... | collective-permute-start | bytes 3145736 | tf_op jit(solution)/shard_map/ppermute | solution.py:128
  607.8 250.6 %reduce-scatter.9.cloned.1.call-start = ((), (), s32[]{:S(2)}) async-start(), calls=%async_computation.18 | async-start | bytes 7864320 | tf_op jit(solution)/shard_map/reduce_scatter | solution.py:133
  647.5 36.1 %all-to-all-start.6 = ((bf16[4,2,32768]{2,1,0:T(2,128)(2,1)}), bf16[4,2,32768]{2,1,0:T(2,128)(2,1)}, u32[]{:S(2)}, u32[]{:S(2)}) async-start(bf16[4,2,32768]{2,1,0:T(2,128)(2,1)} %reshape.710), calls=%async_computation.7 | async-start | bytes 1048576 | tf_op jit(solution)/shard_map/all_to_all | solution.py:366
  683.6 34.3 %all-to-all-start.5 = ((bf16[4,2,32768]{2,1,0:T(2,128)(2,1)}), bf16[4,2,32768]{2,1,0:T(2,128)(2,1)}, u32[]{:S(2)}, u32[]{:S(2)}) async-start(bf16[4,2,32768]{2,1,0:T(2,128)(2,1)} %reshape.712), calls=%async_computation.6 | async-start | bytes 1048576 | tf_op jit(solution)/shard_map/all_to_all | solution.py:366
  717.9 35.2 %all-to-all-start.4 = ((bf16[4,2,32768]{2,1,0:T(2,128)(2,1)}), bf16[4,2,32768]{2,1,0:T(2,128)(2,1)}, u32[]{:S(2)}, u32[]{:S(2)}) async-start(bf16[4,2,32768]{2,1,0:T(2,128)(2,1)} %reshape.714), calls=%async_computation.5 | async-start | bytes 1048576 | tf_op jit(solution)/shard_map/all_to_all | solution.py:366
  723.5 162.1 %reduce-scatter.11.cloned.1.call-start = ((), (), s32[]{:S(2)}) async-start(), calls=%async_computation.19 | async-start | bytes 4259840 | tf_op jit(solution)/shard_map/reduce_scatter | solution.py:133
  729.1 28.8 %copy-start.80 = (f32[512]{0:T(512)S(1)}, f32[512]{0:T(512)}, u32[]{:S(2)}) copy-start(f32[512]{0:T(512)} %copy-done.79) | copy-start | bytes 6148
  766.9 3.8 collective-permute-start.27
  770.8 8.4 collective-permute-start.28
  794.3 6.1 collective-permute-start.29
  809.1 14.1 %collective-permute-start.34 = (bf16[128,2048]{1,0:T(8,128)(2,1)S(1)}, bf16[128,2048]{1,0:T(8,128)(2,1)}, u32[]{:S(2)}, u32[]{:S(2)}) collective-permute-start(bf16[128,2048]{1,0:T(8,128)(2,1)S(1)} %dynamic-slice_convert_fusion.4), channel_id=1, source_target_pairs={{0,2},{1,3},{2,0},{3,1},{4,6},{5,7},{6,4},{7,5},{8,10},{9,11},{10,... | collective-permute-start | bytes 1572872 | tf_op jit(solution)/shard_map/ppermute | solution.py:99
  811.0 15.3 %collective-permute-start.30 = (bf16[128,2048]{1,0:T(8,128)(2,1)S(1)}, bf16[128,2048]{1,0:T(8,128)(2,1)}, u32[]{:S(2)}, u32[]{:S(2)}) collective-permute-start(bf16[128,2048]{1,0:T(8,128)(2,1)S(1)} %dynamic-slice_convert_fusion.5), channel_id=1, source_target_pairs={{0,1},{1,0},{2,3},{3,2},{4,5},{5,4},{6,7},{7,6},{8,9},{9,8},{10,11... | collective-permute-start | bytes 1572872 | tf_op jit(solution)/shard_map/ppermute | solution.py:99
  824.8 7.6 collective-permute-start.35
  827.9 7.3 collective-permute-start.31
  832.4 6.8 collective-permute-start.36
  835.2 7.5 collective-permute-start.32
  840.2 12.9 %collective-permute-start.37 = (bf16[128,2048]{1,0:T(8,128)(2,1)}, bf16[128,2048]{1,0:T(8,128)(2,1)}, u32[]{:S(2)}, u32[]{:S(2)}) collective-permute-start(bf16[128,2048]{1,0:T(8,128)(2,1)} %pad_maximum_fusion.24), channel_id=1, source_target_pairs={{0,2},{1,3},{2,0},{3,1},{4,6},{5,7},{6,4},{7,5},{8,10},{9,11},{10,... | collective-permute-start | bytes 1572872 | tf_op jit(solution)/shard_map/ppermute | solution.py:112
  843.8 10.7 %collective-permute-start.33 = (bf16[128,2048]{1,0:T(8,128)(2,1)}, bf16[128,2048]{1,0:T(8,128)(2,1)}, u32[]{:S(2)}, u32[]{:S(2)}) collective-permute-start(bf16[128,2048]{1,0:T(8,128)(2,1)} %pad_maximum_fusion.23), channel_id=1, source_target_pairs={{0,1},{1,0},{2,3},{3,2},{4,5},{5,4},{6,7},{7,6},{8,9},{9,8},{10,11... | collective-permute-start | bytes 1572872 | tf_op jit(solution)/shard_map/ppermute | solution.py:111
  (113 other events, 714.8 us)
Sparse Core Ops, SparseCore 0:
  10.2 85.2 all-gather.7
  97.6 71.4 all-gather.9
  171.3 89.7 all-gather.11
  262.6 44.9 all-gather.13
  309.6 80.8 all-gather.15
  484.3 116.1 reduce-scatter.4
  608.0 26.9 reduce-scatter.6
  637.2 134.5 reduce-scatter.8
  812.6 63.4 reduce-scatter.10
